TPU v7x, 32 devices: a whole 2x2x4 slice. The times are simulated.
32 devices in a mesh: batch: 4 (over z), seq: 8 (over y, x, core).
Axes of the slice: x: 2, y: 2, z: 4, core: 2. Of those that a mesh axis runs over, the one named last changes fastest.
Arguments:
- block_input: bfloat16 [16384, 768], P(('batch', 'seq')), may hold values from -6 to 6
- history: bfloat16 [8, 16384, 768], P(None, ('batch', 'seq')), may hold values from -6 to 6
- cotangent: bfloat16 [16384, 768], P(('batch', 'seq')), may hold values from -6 to 6
- qkv_weight: bfloat16 [768, 2304], P('batch', 'seq'), may hold values from -0.21875 to 0.21875
- proj_weight: bfloat16 [768, 768], P('batch', 'seq'), may hold values from -1.25 to 1.25
- up_weight: bfloat16 [768, 3072], P('batch', 'seq'), may hold values from -0.21875 to 0.21875
- down_weight: bfloat16 [3072, 768], P('batch', 'seq'), may hold values from -0.109375 to 0.109375
- norm1_gain: float32 [768], replicated, may hold values from 0.5 to 1.5
- norm1_bias: float32 [768], replicated, may hold values from -1.2 to 1.2
- norm2_gain: float32 [768], replicated, may hold values from 0.5 to 1.5
- norm2_bias: float32 [768], replicated, may hold values from -1.2 to 1.2
- dwa_weights: float32 [9], replicated, may hold values from 0.3 to 1
- pair_order: int32 [4, 24], P('batch'), may hold values from 0 to 23, each once within a row
- long_group: int32 [4, 2], P('batch'), may hold values from 0 to 2
Outputs:
- block_output: bfloat16 [16384, 768], P(('batch', 'seq'))
- input_grad: bfloat16 [16384, 768], P(('batch', 'seq'))
- history_grad: bfloat16 [8, 16384, 768], P(None, ('batch', 'seq'))
- row_lse: float32 [4, 24, 2048], P('batch', 'seq')
- qkv_grad: float32 [768, 2304], P('batch', 'seq')
- proj_grad: float32 [768, 768], P('batch', 'seq')
- up_grad: float32 [768, 3072], P('batch', 'seq')
- down_grad: float32 [3072, 768], P('batch', 'seq')
- norm1_gain_grad: float32 [768], replicated
- norm1_bias_grad: float32 [768], replicated
- norm2_gain_grad: float32 [768], replicated
- norm2_bias_grad: float32 [768], replicated
- dwa_grad: float32 [9], replicated
Inputs may be any that keep to these rules, and one draw needn't show every extreme that they name: `pair_order`: each row lists each of its group's 24 pairs once. `long_group`: an entry v: that slot holds 2^v sequences of 2048 // 2^v tokens.
All inputs are finite; a program needn't handle non-finite values.
Results may differ from a plain program's by a relative error of at most 0.017.
Values may be sent and summed in bfloat16 or wider, within the bound.
No kernel may reach another device: no remote copies, remote signals or barrier semaphores. Data moves between devices by JAX's collectives and lax.ppermute only.
A program may use at most 192 MiB of HBM per device.

v0:
```python
import jax
import jax.numpy as jnp
from jax import lax
from jax.sharding import PartitionSpec as P
from jax.experimental import pallas as pl
from jax.experimental.pallas import tpu as pltpu
import functools

D = 768
HEADS = 12
HD = 64
SLOT = 2048
HIST = 8


NORM_EPS = 1e-05
MASKED = -1e30
NT_DIMS = (((1,), (1,)), ((), ()))


def fwd_kernel(seg_ref, q_ref, k_ref, v_ref, o_ref, lse_ref, *, bq, bk, scale):
    pair = pl.program_id(0)
    qi = pl.program_id(1)
    seg_len = seg_ref[pair]
    q_start = qi * bq
    seg_start = (q_start // seg_len) * seg_len
    query = (q_ref[0, 0].astype(jnp.float32).T * scale).astype(jnp.bfloat16)

    def step(j, carry, masked):
        m_old, l_old, acc = carry
        k_off = pl.multiple_of(j * bk, bk)
        key_t = k_ref[0, 0, :, pl.ds(k_off, bk)]
        value_t = v_ref[0, 0, :, pl.ds(k_off, bk)]
        s = jnp.dot(query, key_t, preferred_element_type=jnp.float32)
        if masked:
            rows = q_start + lax.broadcasted_iota(jnp.int32, (bq, bk), 0)
            cols = k_off + lax.broadcasted_iota(jnp.int32, (bq, bk), 1)
            s = jnp.where(cols <= rows, s, MASKED)
        m_new = jnp.maximum(m_old, jnp.max(s, axis=-1, keepdims=True))
        alpha = jnp.exp(m_old - m_new)
        weights = jnp.exp(s - m_new)
        l_new = alpha * l_old + jnp.sum(weights, axis=-1, keepdims=True)
        acc = alpha * acc + lax.dot_general(
            weights.astype(jnp.bfloat16), value_t, NT_DIMS, preferred_element_type=jnp.float32
        )
        return m_new, l_new, acc

    carry = (
        jnp.full((bq, 1), MASKED, jnp.float32),
        jnp.zeros((bq, 1), jnp.float32),
        jnp.zeros((bq, HD), jnp.float32),
    )
    j_diag = q_start // bk
    carry = lax.fori_loop(seg_start // bk, j_diag, lambda j, c: step(j, c, False), carry)
    for r in range(bq // bk):
        carry = step(j_diag + r, carry, True)
    m_fin, l_fin, acc = carry
    o_ref[0] = (acc / l_fin).T.astype(o_ref.dtype)
    lse = m_fin + jnp.log(l_fin)
    lse_ref[0] = jnp.transpose(jnp.broadcast_to(lse, (bq, 128)))[0:1, :]


def attn_forward(qkv_t, seg_pairs, bq=512, bk=512):
    pairs, _, head_size, seq_len = qkv_t.shape
    scale = head_size ** (-0.5)
    n_q = seq_len // bq
    blocks_done = pairs * (seq_len // bk) * (seq_len // bk + 1) // 2
    cost = pl.CostEstimate(
        flops=4 * blocks_done * bk * bk * head_size,
        transcendentals=blocks_done * bk * bk,
        bytes_accessed=pairs * seq_len * head_size * 2 * 4 + pairs * seq_len * 4,
    )
    grid_spec = pltpu.PrefetchScalarGridSpec(
        num_scalar_prefetch=1,
        grid=(pairs, n_q),
        in_specs=[
            pl.BlockSpec((1, 1, head_size, bq), lambda p, i, seg: (p, 0, 0, i)),
            pl.BlockSpec((1, 1, head_size, seq_len), lambda p, i, seg: (p, 1, 0, 0)),
            pl.BlockSpec((1, 1, head_size, seq_len), lambda p, i, seg: (p, 2, 0, 0)),
        ],
        out_specs=[
            pl.BlockSpec((1, head_size, bq), lambda p, i, seg: (p, 0, i)),
            pl.BlockSpec((1, 1, bq), lambda p, i, seg: (p, 0, i)),
        ],
    )
    return pl.pallas_call(
        functools.partial(fwd_kernel, bq=bq, bk=bk, scale=scale),
        grid_spec=grid_spec,
        out_shape=[
            jax.ShapeDtypeStruct((pairs, head_size, seq_len), jnp.bfloat16),
            jax.ShapeDtypeStruct((pairs, 1, seq_len), jnp.float32),
        ],
        cost_estimate=cost,
        name="attn_fwd",
    )(seg_pairs, qkv_t, qkv_t, qkv_t)


def bwd_kernel(seg_ref, q_ref, k_ref, v_ref, do_ref, o_ref, lse_ref, out_ref, dq_acc, *, bk, bq, scale):
    pair = pl.program_id(0)
    kj = pl.program_id(1)

    @pl.when(kj == 0)
    def _():
        dq_acc[...] = jnp.zeros_like(dq_acc)

    seg_len = seg_ref[pair]
    k_start = kj * bk
    seg_end = (k_start // seg_len + 1) * seg_len
    key_t = k_ref[0, 0]
    key = key_t.astype(jnp.float32).T.astype(jnp.bfloat16)
    value_s = (v_ref[0, 0].astype(jnp.float32).T * scale).astype(jnp.bfloat16)

    def step(i, carry, masked):
        dk_t, dv_t = carry
        q_off = pl.multiple_of(i * bq, bq)
        query_t = q_ref[0, 0, :, pl.ds(q_off, bq)]
        query_ts = (query_t.astype(jnp.float32) * scale).astype(jnp.bfloat16)
        dout_t = do_ref[0, :, pl.ds(q_off, bq)]
        out_t = o_ref[0, :, pl.ds(q_off, bq)]
        lse = lse_ref[0, :, pl.ds(q_off, bq)]
        delta = jnp.sum(
            dout_t.astype(jnp.float32) * out_t.astype(jnp.float32), axis=0, keepdims=True
        ) * scale
        s_t = jnp.dot(key, query_ts, preferred_element_type=jnp.float32)
        if masked:
            keys_at = k_start + lax.broadcasted_iota(jnp.int32, (bk, bq), 0)
            queries_at = q_off + lax.broadcasted_iota(jnp.int32, (bk, bq), 1)
            s_t = jnp.where(keys_at <= queries_at, s_t, MASKED)
        p_t = jnp.exp(s_t - lse)
        dv_t = dv_t + lax.dot_general(
            dout_t, p_t.astype(jnp.bfloat16), NT_DIMS, preferred_element_type=jnp.float32
        )
        dp_t = jnp.dot(value_s, dout_t, preferred_element_type=jnp.float32)
        ds_t = (p_t * (dp_t - delta)).astype(jnp.bfloat16)
        dk_t = dk_t + lax.dot_general(query_t, ds_t, NT_DIMS, preferred_element_type=jnp.float32)
        dq_acc[:, pl.ds(q_off, bq)] += jnp.dot(key_t, ds_t, preferred_element_type=jnp.float32)
        return dk_t, dv_t

    carry = (jnp.zeros((HD, bk), jnp.float32), jnp.zeros((HD, bk), jnp.float32))
    for r in range(bk // bq):
        carry = step(k_start // bq + r, carry, True)
    dk_t, dv_t = lax.fori_loop(
        (k_start + bk) // bq, seg_end // bq, lambda i, c: step(i, c, False), carry
    )
    out_ref[0, 0] = dq_acc[:, pl.ds(pl.multiple_of(k_start, bk), bk)].astype(out_ref.dtype)
    out_ref[0, 1] = dk_t.astype(out_ref.dtype)
    out_ref[0, 2] = dv_t.astype(out_ref.dtype)


def attn_backward(qkv_t, dout_t, out_t, lse, seg_pairs, bk=512, bq=512):
    pairs, _, head_size, seq_len = qkv_t.shape
    scale = head_size ** (-0.5)
    n_k = seq_len // bk
    blocks_done = pairs * (seq_len // bq) * (seq_len // bq + 1) // 2
    cost = pl.CostEstimate(
        flops=10 * blocks_done * bq * bq * head_size,
        transcendentals=blocks_done * bq * bq,
        bytes_accessed=pairs * seq_len * head_size * 2 * 8 + pairs * seq_len * 4,
    )
    grid_spec = pltpu.PrefetchScalarGridSpec(
        num_scalar_prefetch=1,
        grid=(pairs, n_k),
        in_specs=[
            pl.BlockSpec((1, 1, head_size, seq_len), lambda p, j, seg: (p, 0, 0, 0)),
            pl.BlockSpec((1, 1, head_size, bk), lambda p, j, seg: (p, 1, 0, j)),
            pl.BlockSpec((1, 1, head_size, bk), lambda p, j, seg: (p, 2, 0, j)),
            pl.BlockSpec((1, head_size, seq_len), lambda p, j, seg: (p, 0, 0)),
            pl.BlockSpec((1, head_size, seq_len), lambda p, j, seg: (p, 0, 0)),
            pl.BlockSpec((1, 1, seq_len), lambda p, j, seg: (p, 0, 0)),
        ],
        out_specs=pl.BlockSpec((1, 3, head_size, bk), lambda p, j, seg: (p, 0, 0, j)),
        scratch_shapes=[pltpu.VMEM((head_size, seq_len), jnp.float32)],
    )
    return pl.pallas_call(
        functools.partial(bwd_kernel, bk=bk, bq=bq, scale=scale),
        grid_spec=grid_spec,
        out_shape=jax.ShapeDtypeStruct((pairs, 3, head_size, seq_len), jnp.bfloat16),
        cost_estimate=cost,
        name="attn_bwd",
    )(seg_pairs, qkv_t, qkv_t, qkv_t, dout_t, out_t, lse)


def norm_rows(values, gain, shift):
    row_mean = jnp.mean(values, axis=-1, keepdims=True)
    centred = values - row_mean
    variance = jnp.mean(centred * centred, axis=-1, keepdims=True)
    inv_std = lax.rsqrt(variance + NORM_EPS)
    normed = centred * inv_std
    return (normed * gain + shift, normed, inv_std)


def norm_back(grad_in, normed, inv_std, gain):
    scaled = grad_in * gain
    centred = (
        scaled
        - jnp.mean(scaled, axis=-1, keepdims=True)
        - normed * jnp.mean(scaled * normed, axis=-1, keepdims=True)
    )
    return (centred * inv_std, jnp.sum(grad_in * normed, axis=0), jnp.sum(grad_in, axis=0))


def rotate(values, cosine, sine_tab):
    half_size = values.shape[-1] // 2
    front = values[..., :half_size]
    behind = values[..., half_size:]
    cos_part = cosine[..., None, :]
    sin_part = sine_tab[..., None, :]
    return jnp.concatenate(
        [front * cos_part - behind * sin_part, behind * cos_part + front * sin_part], axis=-1
    )


def unrotate(values, cosine, sine_tab):
    half_size = values.shape[-1] // 2
    front = values[..., :half_size]
    behind = values[..., half_size:]
    cos_part = cosine[..., None, :]
    sin_part = sine_tab[..., None, :]
    return jnp.concatenate(
        [front * cos_part + behind * sin_part, behind * cos_part - front * sin_part], axis=-1
    )


def local(
    block_input,
    history,
    cotangent,
    qkv_weight,
    proj_weight,
    up_weight,
    down_weight,
    norm1_gain,
    norm1_bias,
    norm2_gain,
    norm2_bias,
    dwa_weights,
    pair_order,
    long_group,
):
    n_seq = lax.axis_size("seq")
    row_count = block_input.shape[0]
    piece_len = SLOT // n_seq
    slot_count = row_count // piece_len
    pair_count = slot_count * HEADS
    per_dev = pair_count // n_seq
    slot_flags = long_group[0]
    seg_len = SLOT // jnp.left_shift(jnp.ones_like(slot_flags), slot_flags)
    position = jnp.arange(SLOT, dtype=jnp.int32)
    doc_place = (position[None, :] % seg_len[:, None]).astype(jnp.float32)
    frequency = jnp.power(10000.0, jnp.arange(HD // 2, dtype=jnp.float32) * (-2.0 / HD))
    angles = doc_place[..., None] * frequency
    my_index = lax.axis_index("seq")
    my_start = my_index * piece_len
    cosine = lax.dynamic_slice_in_dim(jnp.cos(angles), my_start, piece_len, 1)
    sine_tab = lax.dynamic_slice_in_dim(jnp.sin(angles), my_start, piece_len, 1)
    head_groups = HEADS // per_dev
    order_row = pair_order[0]
    held_pairs = lax.dynamic_slice_in_dim(order_row, my_index * per_dev, per_dev, 0)
    my_pairs = my_index * per_dev + jnp.arange(per_dev, dtype=jnp.int32)
    seg_pairs = jnp.take(seg_len, my_pairs // HEADS).astype(jnp.int32)
    n_batch = lax.axis_size("batch")
    batch_index = lax.axis_index("batch")

    def gather_rows(local):
        acc = local
        bits = n_batch.bit_length() - 1
        for bit in reversed(range(bits)):
            partner = [(i, i ^ (1 << bit)) for i in range(n_batch)]
            got = lax.ppermute(acc, "batch", partner)
            low = ((batch_index >> bit) & 1) == 0
            acc = jnp.where(low, jnp.stack([acc, got]), jnp.stack([got, acc]))
        return jnp.transpose(acc, list(range(bits))[::-1] + list(range(bits, acc.ndim))).reshape(
            (n_batch,) + local.shape
        )

    w_qkv = lax.all_gather(
        gather_rows(qkv_weight).reshape(-1, qkv_weight.shape[1]), "seq", axis=1, tiled=True
    )
    inputs32 = block_input.astype(jnp.float32)
    norm1_out, normed1, inv_std1 = norm_rows(inputs32, norm1_gain, norm1_bias)
    norm1_low = norm1_out.astype(jnp.bfloat16)
    qkv_out = jnp.dot(norm1_low, w_qkv, preferred_element_type=jnp.float32)
    queries = rotate(qkv_out[:, :D].reshape(slot_count, piece_len, HEADS, HD), cosine, sine_tab)
    keys_rot = rotate(
        qkv_out[:, D : 2 * D].reshape(slot_count, piece_len, HEADS, HD), cosine, sine_tab
    )
    values_in = qkv_out[:, 2 * D :].reshape(slot_count, piece_len, HEADS, HD)
    stacked = jnp.stack([queries, keys_rot, values_in], axis=2).astype(jnp.bfloat16)
    send = jnp.transpose(
        stacked.reshape(slot_count, piece_len, 3, head_groups, per_dev, HD), (0, 3, 4, 2, 5, 1)
    ).reshape(n_seq, per_dev, 3, HD, piece_len)
    incoming = lax.all_to_all(send, "seq", split_axis=0, concat_axis=0, tiled=True)
    later = (proj_weight, up_weight, down_weight)
    later_rows = gather_rows(jnp.concatenate([w.reshape(-1) for w in later]))
    offset = 0
    later_full = []
    for w in later:
        rows = later_rows[:, offset : offset + w.size].reshape(-1, w.shape[1])
        later_full.append(lax.all_gather(rows, "seq", axis=1, tiled=True))
        offset += w.size
    w_proj, w_up, w_down = later_full
    qkv_t = jnp.transpose(incoming, (1, 2, 3, 0, 4)).reshape(per_dev, 3, HD, SLOT)
    attn_t, lse_rows = attn_forward(qkv_t, seg_pairs)
    back = jnp.transpose(attn_t.reshape(per_dev, HD, n_seq, piece_len), (2, 0, 1, 3))
    returned = lax.all_to_all(back, "seq", split_axis=0, concat_axis=0, tiled=True)
    lse_all = lax.all_gather(lse_rows.reshape(per_dev, SLOT), "seq", axis=0, tiled=True)
    lse_all, returned = lax.optimization_barrier((lse_all, returned))
    attended = jnp.transpose(
        returned.reshape(slot_count, head_groups, per_dev, HD, piece_len), (0, 4, 1, 2, 3)
    ).reshape(row_count, D)
    middle = inputs32 + jnp.dot(attended, w_proj, preferred_element_type=jnp.float32)
    norm2_out, normed2, inv_std2 = norm_rows(middle, norm2_gain, norm2_bias)
    norm2_low = norm2_out.astype(jnp.bfloat16)
    hidden_up = jnp.dot(norm2_low, w_up, preferred_element_type=jnp.float32)
    gelu_out, gelu_pull = jax.vjp(lambda hidden: jax.nn.gelu(hidden, approximate=True), hidden_up)
    gelu_low = gelu_out.astype(jnp.bfloat16)
    block_out = middle + jnp.dot(gelu_low, w_down, preferred_element_type=jnp.float32)
    dwa_out = dwa_weights[HIST] * block_out
    for layer_idx in range(HIST):
        dwa_out = dwa_out + dwa_weights[layer_idx] * history[layer_idx].astype(jnp.float32)
    block_output = dwa_out.astype(jnp.bfloat16)
    grad_out = cotangent.astype(jnp.float32)
    history_grad = (dwa_weights[:HIST, None, None] * grad_out[None]).astype(jnp.bfloat16)
    dwa_terms = [
        jnp.sum(history[layer_idx].astype(jnp.float32) * grad_out) for layer_idx in range(HIST)
    ]
    dwa_terms.append(jnp.sum(block_out * grad_out))
    dwa_local = jnp.stack(dwa_terms)
    dy_full = dwa_weights[HIST] * grad_out
    dmlp_low = dy_full.astype(jnp.bfloat16)
    down_local = jnp.einsum("nf,nd->fd", gelu_low, dmlp_low, preferred_element_type=jnp.float32)
    dgelu = jnp.einsum("nd,fd->nf", dmlp_low, w_down, preferred_element_type=jnp.float32)
    dup_low = gelu_pull(dgelu)[0].astype(jnp.bfloat16)
    up_local = jnp.einsum("nd,nf->df", norm2_low, dup_low, preferred_element_type=jnp.float32)
    dnorm2 = jnp.einsum("nf,df->nd", dup_low, w_up, preferred_element_type=jnp.float32)
    dmid_norm, gain2_local, bias2_local = norm_back(dnorm2, normed2, inv_std2, norm2_gain)
    dmiddle = dy_full + dmid_norm
    dmiddle_low = dmiddle.astype(jnp.bfloat16)
    proj_local = jnp.einsum("nd,ne->de", attended, dmiddle_low, preferred_element_type=jnp.float32)
    dattended = jnp.einsum(
        "ne,de->nd", dmiddle_low, w_proj, preferred_element_type=jnp.float32
    ).astype(jnp.bfloat16)
    dsend = jnp.transpose(
        dattended.reshape(slot_count, piece_len, head_groups, per_dev, HD), (0, 2, 3, 4, 1)
    ).reshape(n_seq, per_dev, HD, piece_len)
    dattn_in = lax.all_to_all(dsend, "seq", split_axis=0, concat_axis=0, tiled=True)
    dout_t = jnp.transpose(dattn_in, (1, 2, 0, 3)).reshape(per_dev, HD, SLOT)
    dpairs = attn_backward(qkv_t, dout_t, attn_t, lse_rows, seg_pairs)
    dback = jnp.transpose(
        dpairs.reshape(per_dev, 3, HD, n_seq, piece_len), (3, 0, 1, 2, 4)
    )
    dreturned = lax.all_to_all(dback, "seq", split_axis=0, concat_axis=0, tiled=True)
    dtokens = jnp.transpose(
        dreturned.reshape(slot_count, head_groups, per_dev, 3, HD, piece_len), (0, 5, 3, 1, 2, 4)
    ).reshape(slot_count, piece_len, 3, HEADS, HD)
    dq_rows = unrotate(dtokens[:, :, 0].astype(jnp.float32), cosine, sine_tab).reshape(row_count, D)
    dk_rows = unrotate(dtokens[:, :, 1].astype(jnp.float32), cosine, sine_tab).reshape(row_count, D)
    dv_rows = dtokens[:, :, 2].astype(jnp.float32).reshape(row_count, D)
    dqkv_low = jnp.concatenate([dq_rows, dk_rows, dv_rows], axis=-1).astype(jnp.bfloat16)
    qkv_local = jnp.einsum("nd,nf->df", norm1_low, dqkv_low, preferred_element_type=jnp.float32)
    dnorm1 = jnp.einsum("nf,df->nd", dqkv_low, w_qkv, preferred_element_type=jnp.float32)
    dinput_norm, gain1_local, bias1_local = norm_back(dnorm1, normed1, inv_std1, norm1_gain)
    input_grad = (dmiddle + dinput_norm).astype(jnp.bfloat16)

    def by_cols(partial):
        rows, cols = partial.shape
        bits = n_seq.bit_length() - 1
        acc = partial.reshape((rows,) + (2,) * bits + (cols // n_seq,))
        for bit in range(bits):
            mine = (my_index >> bit) & 1
            keep = lax.dynamic_index_in_dim(acc, mine, axis=acc.ndim - 2, keepdims=False)
            send = lax.dynamic_index_in_dim(acc, 1 - mine, axis=acc.ndim - 2, keepdims=False)
            partner = [(i, i ^ (1 << bit)) for i in range(n_seq)]
            got = lax.ppermute(send.astype(jnp.bfloat16), "seq", partner)
            acc = keep + got.astype(jnp.float32)
        return acc.astype(jnp.bfloat16)

    def by_rows(col_sum):
        return lax.psum_scatter(col_sum, "batch", scatter_dimension=0, tiled=True).astype(
            jnp.float32
        )

    qkv_grad = by_rows(by_cols(qkv_local))
    proj_grad = by_rows(by_cols(proj_local))
    up_grad = by_rows(by_cols(up_local))
    down_grad = by_rows(by_cols(down_local))
    small_sums = jnp.concatenate([gain1_local, bias1_local, gain2_local, bias2_local, dwa_local])
    for axis in ("seq", "batch"):
        size = lax.axis_size(axis)
        hop = 1
        while hop < size:
            partner = [(i, i ^ hop) for i in range(size)]
            small_sums = small_sums + lax.ppermute(small_sums, axis, partner)
            hop *= 2
    gain1_grad, bias1_grad, gain2_grad, bias2_grad = (
        small_sums[k * D : (k + 1) * D] for k in range(4)
    )
    dwa_grad = small_sums[4 * D :]
    row_lse = jnp.take(lse_all, held_pairs, axis=0).reshape(1, per_dev, SLOT)
    return (
        block_output,
        input_grad,
        history_grad,
        row_lse,
        qkv_grad,
        proj_grad,
        up_grad,
        down_grad,
        gain1_grad,
        bias1_grad,
        gain2_grad,
        bias2_grad,
        dwa_grad,
    )


def solution(mesh):
    placed = (
        P(("batch", "seq"), None),
        P(None, ("batch", "seq"), None),
        P(("batch", "seq"), None),
        P("batch", "seq"),
        P("batch", "seq"),
        P("batch", "seq"),
        P("batch", "seq"),
        P(),
        P(),
        P(),
        P(),
        P(),
        P("batch", None),
        P("batch", None),
    )

    return jax.shard_map(
        local,
        mesh=mesh,
        in_specs=placed,
        out_specs=(
            P(("batch", "seq"), None),
            P(("batch", "seq"), None),
            P(None, ("batch", "seq"), None),
            P("batch", "seq", None),
            P("batch", "seq"),
            P("batch", "seq"),
            P("batch", "seq"),
            P("batch", "seq"),
            P(),
            P(),
            P(),
            P(),
            P(),
        ),
        check_vma=False,
    )
```

profile of v0, /device:TPU:0, one launch (start us, length us, event | category | flops | bytes accessed | tf_op | source)
XLA Modules:
  0.0 498.7 jit_solution(15302604183611001016)
XLA Ops:
  7.2 4.1 collective-permute-start
  15.6 10.8 %collective-permute-done = bf16[192,288]{1,0:T(8,128)(2,1)S(1)} collective-permute-done((bf16[192,288]{1,0:T(8,128)(2,1)}, bf16[192,288]{1,0:T(8,128)(2,1)S(1)}, u32[]{:S(2)}, u32[]{:S(2)}) %collective-permute-start) | collective-permute-done | bytes 110624 | tf_op jit(solution)/shard_map/ppermute | solution.py:269
  26.9 6.0 %collective-permute-done.2 = bf16[165888]{0:T(1024)(128)(2,1)S(1)} collective-permute-done((bf16[165888]{0:T(1024)(128)(2,1)S(1)}, bf16[165888]{0:T(1024)(128)(2,1)S(1)}, u32[]{:S(2)}, u32[]{:S(2)}) %collective-permute-start.2) | collective-permute-done | bytes 331808 | tf_op jit(solution)/shard_map/ppermute | solution.py:269
  42.3 11.0 %collective-permute-done.3 = bf16[2,165888]{1,0:T(2,128)(2,1)S(1)} collective-permute-done((bf16[2,165888]{1,0:T(2,128)(2,1)S(1)}, bf16[2,165888]{1,0:T(2,128)(2,1)S(1)}, u32[]{:S(2)}, u32[]{:S(2)}) %collective-permute-start.3) | collective-permute-done | bytes 663584 | tf_op jit(solution)/shard_map/ppermute | solution.py:269
  55.3 4.1 copy.105
  67.4 9.9 %all-gather.6.cloned.1.call-done = bf16[768,2304]{0,1:T(8,128)(2,1)} async-done(((bf16[768,288]{0,1:T(8,128)(2,1)}), bf16[768,2304]{0,1:T(8,128)(2,1)}) %all-gather.6.cloned.1.call-update) | async-done | bytes 3538960 | tf_op jit(solution)/shard_map/all_gather | solution.py:276
  77.3 4.2 fusion.76
  104.1 4.1 all-to-all-start
  112.1 31.8 %all-to-all-done = bf16[8,3,3,64,256]{4,3,2,1,0:T(8,128)(2,1)S(1)} async-done(((bf16[8,3,3,64,256]{4,3,2,1,0:T(8,128)(2,1)}), bf16[8,3,3,64,256]{4,3,2,1,0:T(8,128)(2,1)S(1)}, u32[]{:S(2)}, u32[]{:S(2)}) %all-to-all-start) | async-done | bytes 2359328 | tf_op jit(solution)/shard_map/all_to_all | solution.py:292
  145.7 17.1 %attn_fwd.1 = (bf16[3,64,2048]{2,1,0:T(8,128)(2,1)}, f32[3,1,2048]{2,1,0:T(1,128)}) custom-call(s32[3]{0:T(128)} %and_select_fusion.2.seg_ref, bf16[3,3,64,2048]{3,2,1,0:T(8,128)(2,1)} %bitcast.269, bf16[3,3,64,2048]{3,2,1,0:T(8,128)(2,1)} %bitcast.270, bf16[3,3,64,2048]{3,2,1,0:T(8,128)(2,1)} %bitcast.271), custom_call_target="tpu_custom_call" | custom-call | flops 2013265920 | bytes 3170304 | tf_op jit(solution)/shard_map/attn_fwd/pallas_call | solution.py:86
  169.9 4.5 multiply_convert_fusion
  174.4 15.9 %all-gather = f32[24,1,2048]{2,1,0:T(1,128)S(1)} all-gather(f32[3,1,2048]{2,1,0:T(1,128)S(1)} %copy-done.24), channel_id=2, replica_groups=mesh['batch'=4,'seq'=8] {'seq'}, dimensions={0}, use_global_device_ids=true | all-gather | bytes 221184 | tf_op jit(solution)/shard_map/all_gather | solution.py:306
  195.3 4.8 fusion.79
  202.7 6.1 %fusion.56 = f32[3072,768]{0,1:T(8,128)} fusion(bf16[512,768]{1,0:T(8,128)(2,1)S(1)} %copy-done.13, f32[]{:T(128)} %bitcast, f32[512,3072]{1,0:T(8,128)S(1)} %fusion.79), kind=kOutput, calls=%fused_computation.133 | convolution fusion | flops 2431254528 | bytes 16515076 | tf_op jit(solution)/shard_map/nf,nd->fd/dot_general | solution.py:331
  208.8 9.8 %fusion.6 = bf16[512,3072]{1,0:T(8,128)(2,1)S(1)} fusion(f32[512,3072]{1,0:T(8,128)} %copy-done.41, bf16[3072,768]{0,1:T(8,128)(2,1)} %all-gather.12.cloned.1.call-done, bf16[512,768]{1,0:T(8,128)(2,1)S(1)} %copy-done.13, f32[]{:T(128)} %bitcast), kind=kOutput, calls=%fused_computation.11 | convolution fusion | flops 2448556032 | bytes 14942212 | tf_op jit(solution)/shard_map/nd,fd->nf/dot_general | solution.py:332
  218.6 5.6 %fusion.78 = f32[768,3072]{1,0:T(8,128)} fusion(bf16[512,3072]{1,0:T(8,128)(2,1)S(1)} %fusion.6, f32[512,768]{1,0:T(8,128)S(1)} %get-tuple-element.130, f32[768]{0:T(1024)S(1)} %copy-done.37, f32[768]{0:T(1024)S(1)} %copy-done.29, f32[512]{0:T(512)S(1)} %add_rsqrt_fusion, f32[512]{0:T(512)S(1)} %broadcast_multiply_fusion.5), kind=kOutput, calls=%fused_computation.196 | convolution fusion | flops 2417885184 | bytes 14166016 | tf_op jit(solution)/shard_map/nd,nf->df/dot_general | solution.py:334
  224.2 6.1 %multiply_reduce_fusion = (f32[768]{0:T(1024)}, f32[512]{0:T(512)S(1)}, f32[512]{0:T(512)S(1)}, f32[768]{0:T(1024)}, f32[512,768]{1,0:T(8,128)S(1)}) fusion(f32[512,768]{1,0:T(8,128)S(1)} %get-tuple-element.130, f32[512]{0:T(512)S(1)} %add_rsqrt_fusion, f32[512]{0:T(512)S(1)} %broadcast_multiply_fusion.5, f32[768]{0:T(1024)S(1)} %copy-done.29, ...), kind=kOutput, calls=%fused_computation.88 | convolution fusion | flops 2419455488 | bytes 11027456 | tf_op jit(solution)/shard_map/nf,df->nd/dot_general | solution.py:335
  230.4 13.9 %fusion.35 = (bf16[512,768]{1,0:T(8,128)(2,1)}, f32[512,768]{1,0:T(8,128)S(1)}) fusion(f32[]{:T(128)} %bitcast.34, f32[]{:T(128)} %bitcast.32, f32[]{:T(128)} %bitcast.30, f32[]{:T(128)} %bitcast.28, f32[]{:T(128)} %bitcast.26, f32[]{:T(128)} %bitcast.24, f32[]{:T(128)} %bitcast.22, f32[]{:T(128)} %bitcast.20, f32[]{:T(128)} %bitcast, ...), kind=kOutput, calls=%fused_computation.77 | convolution fusion | flops 2440691712 | bytes 21233700 | tf_op jit(solution)/shard_map/dot_general | solution.py:317
  251.4 4.2 all-to-all-start.2
  255.7 4.1 fusion.8
  263.5 13.2 %reshape.542 = f32[768,2,2,2,384]{4,3,2,1,0:T(2,128)} reshape(f32[768,3072]{1,0:T(8,128)} %fusion.78) | data formatting | bytes 18874368 | tf_op jit(solution)/shard_map/reshape | solution.py:368
  276.9 6.8 %constant_dynamic-slice_fusion.2 = bf16[768,2,2,1,384]{4,3,2,1,0:T(2,128)(2,1)S(1)} fusion(f32[768,2,2,2,384]{4,3,2,1,0:T(2,128)} %reshape.542, s32[]{:T(128)S(6)} %select_n.229), kind=kLoop, calls=%fused_computation.165 | loop fusion | bytes 4718596 | tf_op jit(solution)/shard_map/jit(dynamic_index_in_dim)/dynamic_slice | solution.py:372
  285.9 5.1 %constant_dynamic-slice_fusion.3 = f32[768,2,2,1,384]{4,3,2,1,0:T(1,128)} fusion(f32[768,2,2,2,384]{4,3,2,1,0:T(2,128)S(1)} %copy-done, s32[]{:T(128)S(6)} %select_n.228), kind=kLoop, calls=%fused_computation.166 | loop fusion | bytes 9437188 | tf_op jit(solution)/shard_map/jit(dynamic_index_in_dim)/dynamic_slice | solution.py:371
  296.7 20.8 %attn_bwd.1 = bf16[3,3,64,2048]{3,2,1,0:T(8,128)(2,1)} custom-call(s32[3]{0:T(128)} %and_select_fusion.2.seg_ref, bf16[3,3,64,2048]{3,2,1,0:T(8,128)(2,1)} %bitcast.272, bf16[3,3,64,2048]{3,2,1,0:T(8,128)(2,1)} %bitcast.273, bf16[3,3,64,2048]{3,2,1,0:T(8,128)(2,1)} %bitcast.274, bf16[3,64,2048]{2,1,0:T(8,128)(2,1)} %bitcast.278, ...), custom_call_target="tpu_custom_call" | custom-call | flops 5033164800 | bytes 6316032 | tf_op jit(solution)/shard_map/attn_bwd/pallas_call | solution.py:174
  340.7 13.8 %all-to-all-done.3 = bf16[8,3,3,64,256]{4,3,2,1,0:T(8,128)(2,1)S(1)} async-done(((bf16[8,3,3,64,256]{4,3,2,1,0:T(8,128)(2,1)}), bf16[8,3,3,64,256]{4,3,2,1,0:T(8,128)(2,1)S(1)}, u32[]{:S(2)}, u32[]{:S(2)}) %all-to-all-start.3) | async-done | bytes 2359328 | tf_op jit(solution)/shard_map/all_to_all | solution.py:352
  365.8 13.2 %collective-permute-done.14 = bf16[3072,2,96]{0,2,1:T(8,128)(2,1)} collective-permute-done((bf16[3072,2,96]{0,2,1:T(8,128)(2,1)}, bf16[3072,2,96]{0,2,1:T(8,128)(2,1)}, u32[]{:S(2)}, u32[]{:S(2)}) %collective-permute-start.14) | collective-permute-done | bytes 1179680 | tf_op jit(solution)/shard_map/ppermute | solution.py:374
  385.6 18.1 %collective-permute-done.11 = bf16[768,2,384]{2,0,1:T(8,128)(2,1)} collective-permute-done((bf16[768,2,384]{2,0,1:T(8,128)(2,1)}, bf16[768,2,384]{2,0,1:T(8,128)(2,1)}, u32[]{:S(2)}, u32[]{:S(2)}) %collective-permute-start.11) | collective-permute-done | bytes 1179680 | tf_op jit(solution)/shard_map/ppermute | solution.py:374
  416.0 4.1 fusion.25
  420.1 6.5 %concatenate.62 = f32[3081]{0:T(1024)S(1)} concatenate(f32[768]{0:T(1024)} %get-tuple-element.83, f32[768]{0:T(1024)} %get-tuple-element.88, f32[768]{0:T(1024)} %get-tuple-element.81, f32[768]{0:T(1024)} %get-tuple-element.87, f32[1]{0:T(128)} %bitcast.83, f32[1]{0:T(128)} %bitcast.85, f32[1]{0:T(128)} %bitcast.87, f32[1]{0:T(128)} %bitcast.89, f32[1]{0:T(128)} %bitcast.91, ...), dimensions={0} | concatenate | bytes 24648 | tf_op jit(solution)/shard_map/concatenate | solution.py:387
  444.2 5.6 %collective-permute-done.6 = bf16[768,288]{0,1:T(8,128)(2,1)S(1)} collective-permute-done((bf16[768,288]{0,1:T(8,128)(2,1)S(1)}, bf16[768,288]{0,1:T(8,128)(2,1)S(1)}, u32[]{:S(2)}, u32[]{:S(2)}) %collective-permute-start.6) | collective-permute-done | bytes 442400 | tf_op jit(solution)/shard_map/ppermute | solution.py:374
  452.2 14.3 %collective-permute-start.19 = (f32[3081]{0:T(1024)S(1)}, f32[3081]{0:T(1024)S(1)}, u32[]{:S(2)}, u32[]{:S(2)}) collective-permute-start(f32[3081]{0:T(1024)S(1)} %add.340), channel_id=1, source_target_pairs={{0,8},{8,0},{16,24},{24,16},{1,9},{9,1},{17,25},{25,17},{2,10},{10... | collective-permute-start | bytes 36980 | tf_op jit(solution)/shard_map/ppermute | solution.py:393
  478.5 11.3 %reduce-scatter.13.cloned.1.call-done = bf16[192,288]{1,0:T(8,128)(2,1)} async-done(((bf16[768,288]{1,0:T(8,128)(2,1)}), bf16[192,288]{1,0:T(8,128)(2,1)}) %reduce-scatter.13.cloned.1.call-update) | async-done | bytes 110608
  (305 shorter events, 172.2 us)
Async XLA Ops:
  7.2 70.1 %all-gather.6.cloned.1.call-start = ((), (), s32[]{:S(2)}) async-start(), calls=%async_computation.8 | async-start | bytes 3981312 | tf_op jit(solution)/shard_map/all_gather | solution.py:276
  7.2 19.2 %collective-permute-start = (bf16[192,288]{1,0:T(8,128)(2,1)}, bf16[192,288]{1,0:T(8,128)(2,1)S(1)}, u32[]{:S(2)}, u32[]{:S(2)}) collective-permute-start(bf16[192,288]{1,0:T(8,128)(2,1)} %param.17), channel_id=1, source_target_pairs={{0,16},{8,24},{16,0},{24,8},{1,17},{9,25},{17,1},{25,9},{2,18},{10... | collective-permute-start | bytes 331784 | tf_op jit(solution)/shard_map/ppermute | solution.py:269
  14.7 18.2 %collective-permute-start.2 = (bf16[165888]{0:T(1024)(128)(2,1)S(1)}, bf16[165888]{0:T(1024)(128)(2,1)S(1)}, u32[]{:S(2)}, u32[]{:S(2)}) collective-permute-start(bf16[165888]{0:T(1024)(128)(2,1)S(1)} %constant_dynamic-update-slice_fusion.4), channel_id=1, source_target_pairs={{0,16},{8,24},{16,0},{24,8},{1,17},{9,25},{17,1},{25,9},{2,18},{10... | collective-permute-start | bytes 995336 | tf_op jit(solution)/shard_map/ppermute | solution.py:269
  26.5 13.7 %collective-permute-start.1 = (bf16[2,192,288]{2,1,0:T(8,128)(2,1)S(1)}, bf16[2,192,288]{2,1,0:T(8,128)(2,1)S(1)}, u32[]{:S(2)}, u32[]{:S(2)}) collective-permute-start(bf16[2,192,288]{2,1,0:T(8,128)(2,1)S(1)} %maximum_select_fusion.2), channel_id=1, source_target_pairs={{0,8},{8,0},{16,24},{24,16},{1,9},{9,1},{17,25},{25,17},{2,10},{10... | collective-permute-start | bytes 663560 | tf_op jit(solution)/shard_map/ppermute | solution.py:269
  36.2 17.1 %collective-permute-start.3 = (bf16[2,165888]{1,0:T(2,128)(2,1)S(1)}, bf16[2,165888]{1,0:T(2,128)(2,1)S(1)}, u32[]{:S(2)}, u32[]{:S(2)}) collective-permute-start(bf16[2,165888]{1,0:T(2,128)(2,1)S(1)} %broadcast_select_fusion.1), channel_id=1, source_target_pairs={{0,8},{8,0},{16,24},{24,16},{1,9},{9,1},{17,25},{25,17},{2,10},{10... | collective-permute-start | bytes 1990664 | tf_op jit(solution)/shard_map/ppermute | solution.py:269
  42.2 149.9 %all-gather.8.cloned.1.call-start = ((), (), s32[]{:S(2)}) async-start(), calls=%async_computation.9 | async-start | bytes 1327104 | tf_op jit(solution)/shard_map/all_gather | solution.py:299
  61.0 134.0 %all-gather.10.cloned.1.call-start = ((), (), s32[]{:S(2)}) async-start(), calls=%async_computation.10 | async-start | bytes 5308416 | tf_op jit(solution)/shard_map/all_gather | solution.py:299
  62.7 146.2 %all-gather.12.cloned.1.call-start = ((), (), s32[]{:S(2)}) async-start(), calls=%async_computation.11 | async-start | bytes 5308416 | tf_op jit(solution)/shard_map/all_gather | solution.py:299
  104.1 39.8 %all-to-all-start = ((bf16[8,3,3,64,256]{4,3,2,1,0:T(8,128)(2,1)}), bf16[8,3,3,64,256]{4,3,2,1,0:T(8,128)(2,1)S(1)}, u32[]{:S(2)}, u32[]{:S(2)}) async-start(bf16[8,3,3,64,256]{4,3,2,1,0:T(8,128)(2,1)} %copy.100), calls=%async_computation | async-start | bytes 4718592 | tf_op jit(solution)/shard_map/all_to_all | solution.py:292
  165.0 26.1 %all-to-all-start.1 = ((bf16[8,3,64,256]{3,2,1,0:T(8,128)(2,1)}), bf16[8,3,64,256]{3,2,1,0:T(8,128)(2,1)S(1)}, u32[]{:S(2)}, u32[]{:S(2)}) async-start(bf16[8,3,64,256]{3,2,1,0:T(8,128)(2,1)} %bitcast.257), calls=%async_computation.1 | async-start | bytes 1572864 | tf_op jit(solution)/shard_map/all_to_all | solution.py:305
  251.4 43.1 %all-to-all-start.2 = ((bf16[8,3,64,256]{3,2,1,0:T(8,128)(2,1)}), bf16[8,3,64,256]{3,2,1,0:T(8,128)(2,1)}, u32[]{:S(2)}, u32[]{:S(2)}) async-start(bf16[8,3,64,256]{3,2,1,0:T(8,128)(2,1)} %bitcast.37), calls=%async_computation.2 | async-start | bytes 1572864 | tf_op jit(solution)/shard_map/all_to_all | solution.py:346
  259.7 69.3 %collective-permute-start.13 = (bf16[3072,2,2,96]{0,3,1,2:T(8,128)(2,1)}, bf16[3072,2,2,96]{0,3,1,2:T(8,128)(2,1)}, u32[]{:S(2)}, u32[]{:S(2)}) collective-permute-start(bf16[3072,2,2,96]{0,3,1,2:T(8,128)(2,1)} %fusion.8), channel_id=1, source_target_pairs={{0,1},{1,0},{2,3},{3,2},{4,5},{5,4},{6,7},{7,6},{8,9},{9,8},{10,11... | collective-permute-start | bytes 7077896 | tf_op jit(solution)/shard_map/ppermute | solution.py:374
  276.7 14.3 %collective-permute-start.7 = (bf16[768,2,2,96]{0,3,2,1:T(8,128)(2,1)S(1)}, bf16[768,2,2,96]{0,3,2,1:T(8,128)(2,1)S(1)}, u32[]{:S(2)}, u32[]{:S(2)}) collective-permute-start(bf16[768,2,2,96]{0,3,2,1:T(8,128)(2,1)S(1)} %fusion.62), channel_id=1, source_target_pairs={{0,1},{1,0},{2,3},{3,2},{4,5},{5,4},{6,7},{7,6},{8,9},{9,8},{10,11... | collective-permute-start | bytes 1769480 | tf_op jit(solution)/shard_map/ppermute | solution.py:374
  285.5 49.9 %collective-permute-start.10 = (bf16[768,2,2,384]{3,0,1,2:T(8,128)(2,1)}, bf16[768,2,2,384]{3,0,1,2:T(8,128)(2,1)}, u32[]{:S(2)}, u32[]{:S(2)}) collective-permute-start(bf16[768,2,2,384]{3,0,1,2:T(8,128)(2,1)} %bitcast.231), channel_id=1, source_target_pairs={{0,1},{1,0},{2,3},{3,2},{4,5},{5,4},{6,7},{7,6},{8,9},{9,8},{10,11... | collective-permute-start | bytes 7077896 | tf_op jit(solution)/shard_map/ppermute | solution.py:374
  292.9 32.1 %collective-permute-start.8 = (bf16[768,2,96]{0,2,1:T(8,128)(2,1)}, bf16[768,2,96]{0,2,1:T(8,128)(2,1)}, u32[]{:S(2)}, u32[]{:S(2)}) collective-permute-start(bf16[768,2,96]{0,2,1:T(8,128)(2,1)} %fusion.68), channel_id=1, source_target_pairs={{0,2},{1,3},{2,0},{3,1},{4,6},{5,7},{6,4},{7,5},{8,10},{9,11},{10,... | collective-permute-start | bytes 884744 | tf_op jit(solution)/shard_map/ppermute | solution.py:374
  320.9 33.6 %all-to-all-start.3 = ((bf16[8,3,3,64,256]{4,3,2,1,0:T(8,128)(2,1)}), bf16[8,3,3,64,256]{4,3,2,1,0:T(8,128)(2,1)S(1)}, u32[]{:S(2)}, u32[]{:S(2)}) async-start(bf16[8,3,3,64,256]{4,3,2,1,0:T(8,128)(2,1)} %bitcast.245), calls=%async_computation.3 | async-start | bytes 4718592 | tf_op jit(solution)/shard_map/all_to_all | solution.py:352
  324.6 115.6 %reduce-scatter.15.cloned.1.call-start = ((), (), s32[]{:S(2)}) async-start(), calls=%async_computation.15 | async-start | bytes 245760
  327.1 55.1 %collective-permute-start.9 = (bf16[768,96]{0,1:T(8,128)(2,1)}, bf16[768,96]{0,1:T(8,128)(2,1)}, u32[]{:S(2)}, u32[]{:S(2)}) collective-permute-start(bf16[768,96]{0,1:T(8,128)(2,1)} %fusion.70), channel_id=1, source_target_pairs={{0,4},{1,5},{2,6},{3,7},{4,0},{5,1},{6,2},{7,3},{8,12},{9,13},{10,... | collective-permute-start | bytes 442376 | tf_op jit(solution)/shard_map/ppermute | solution.py:374
  334.0 45.0 %collective-permute-start.14 = (bf16[3072,2,96]{0,2,1:T(8,128)(2,1)}, bf16[3072,2,96]{0,2,1:T(8,128)(2,1)}, u32[]{:S(2)}, u32[]{:S(2)}) collective-permute-start(bf16[3072,2,96]{0,2,1:T(8,128)(2,1)} %fusion.47), channel_id=1, source_target_pairs={{0,2},{1,3},{2,0},{3,1},{4,6},{5,7},{6,4},{7,5},{8,10},{9,11},{10,... | collective-permute-start | bytes 3538952 | tf_op jit(solution)/shard_map/ppermute | solution.py:374
  340.1 63.6 %collective-permute-start.11 = (bf16[768,2,384]{2,0,1:T(8,128)(2,1)}, bf16[768,2,384]{2,0,1:T(8,128)(2,1)}, u32[]{:S(2)}, u32[]{:S(2)}) collective-permute-start(bf16[768,2,384]{2,0,1:T(8,128)(2,1)} %fusion.46), channel_id=1, source_target_pairs={{0,2},{1,3},{2,0},{3,1},{4,6},{5,7},{6,4},{7,5},{8,10},{9,11},{10,... | collective-permute-start | bytes 3538952 | tf_op jit(solution)/shard_map/ppermute | solution.py:374
  365.8 45.2 %collective-permute-start.4 = (bf16[768,2,2,288]{0,3,2,1:T(8,128)(2,1)}, bf16[768,2,2,288]{0,3,2,1:T(8,128)(2,1)}, u32[]{:S(2)}, u32[]{:S(2)}) collective-permute-start(bf16[768,2,2,288]{0,3,2,1:T(8,128)(2,1)} %fusion.17), channel_id=1, source_target_pairs={{0,1},{1,0},{2,3},{3,2},{4,5},{5,4},{6,7},{7,6},{8,9},{9,8},{10,11... | collective-permute-start | bytes 5308424 | tf_op jit(solution)/shard_map/ppermute | solution.py:374
  380.6 29.1 %collective-permute-start.15 = (bf16[3072,96]{0,1:T(8,128)(2,1)S(1)}, bf16[3072,96]{0,1:T(8,128)(2,1)S(1)}, u32[]{:S(2)}, u32[]{:S(2)}) collective-permute-start(bf16[3072,96]{0,1:T(8,128)(2,1)S(1)} %fusion.64), channel_id=1, source_target_pairs={{0,4},{1,5},{2,6},{3,7},{4,0},{5,1},{6,2},{7,3},{8,12},{9,13},{10,... | collective-permute-start | bytes 1769480 | tf_op jit(solution)/shard_map/ppermute | solution.py:374
  385.6 89.7 %reduce-scatter.11.cloned.1.call-start = ((), (), s32[]{:S(2)}) async-start(), calls=%async_computation.13 | async-start | bytes 737280 | tf_op jit(solution)/shard_map/reduce_scatter | solution.py:379
  408.3 18.3 %collective-permute-start.12 = (bf16[768,384]{1,0:T(8,128)(2,1)}, bf16[768,384]{1,0:T(8,128)(2,1)}, u32[]{:S(2)}, u32[]{:S(2)}) collective-permute-start(bf16[768,384]{1,0:T(8,128)(2,1)} %fusion.63), channel_id=1, source_target_pairs={{0,4},{1,5},{2,6},{3,7},{4,0},{5,1},{6,2},{7,3},{8,12},{9,13},{10,... | collective-permute-start | bytes 1769480 | tf_op jit(solution)/shard_map/ppermute | solution.py:374
  410.7 66.1 %reduce-scatter.9.cloned.1.call-start = ((), (), s32[]{:S(2)}) async-start(), calls=%async_computation.12 | async-start | bytes 737280 | tf_op jit(solution)/shard_map/reduce_scatter | solution.py:379
  415.1 21.1 %collective-permute-start.5 = (bf16[768,2,288]{0,2,1:T(8,128)(2,1)}, bf16[768,2,288]{0,2,1:T(8,128)(2,1)}, u32[]{:S(2)}, u32[]{:S(2)}) collective-permute-start(bf16[768,2,288]{0,2,1:T(8,128)(2,1)} %fusion.50), channel_id=1, source_target_pairs={{0,2},{1,3},{2,0},{3,1},{4,6},{5,7},{6,4},{7,5},{8,10},{9,11},{10,... | collective-permute-start | bytes 2654216 | tf_op jit(solution)/shard_map/ppermute | solution.py:374
  426.5 6.1 %collective-permute-start.16 = (f32[3081]{0:T(1024)S(1)}, f32[3081]{0:T(1024)}, u32[]{:S(2)}, u32[]{:S(2)}) collective-permute-start(f32[3081]{0:T(1024)S(1)} %concatenate.62), channel_id=1, source_target_pairs={{0,1},{1,0},{2,3},{3,2},{4,5},{5,4},{6,7},{7,6},{8,9},{9,8},{10,11... | collective-permute-start | bytes 36980 | tf_op jit(solution)/shard_map/ppermute | solution.py:393
  429.1 60.7 %reduce-scatter.13.cloned.1.call-start = ((), (), s32[]{:S(2)}) async-start(), calls=%async_computation.14 | async-start | bytes 737280
  433.4 8.4 %collective-permute-start.17 = (f32[3081]{0:T(1024)S(1)}, f32[3081]{0:T(1024)}, u32[]{:S(2)}, u32[]{:S(2)}) collective-permute-start(f32[3081]{0:T(1024)S(1)} %add.338), channel_id=1, source_target_pairs={{0,2},{1,3},{2,0},{3,1},{4,6},{5,7},{6,4},{7,5},{8,10},{9,11},{10,... | collective-permute-start | bytes 36980 | tf_op jit(solution)/shard_map/ppermute | solution.py:393
  438.9 10.9 %collective-permute-start.6 = (bf16[768,288]{0,1:T(8,128)(2,1)S(1)}, bf16[768,288]{0,1:T(8,128)(2,1)S(1)}, u32[]{:S(2)}, u32[]{:S(2)}) collective-permute-start(bf16[768,288]{0,1:T(8,128)(2,1)S(1)} %fusion.66), channel_id=1, source_target_pairs={{0,4},{1,5},{2,6},{3,7},{4,0},{5,1},{6,2},{7,3},{8,12},{9,13},{10,... | collective-permute-start | bytes 1327112 | tf_op jit(solution)/shard_map/ppermute | solution.py:374
  442.6 9.6 %collective-permute-start.18 = (f32[3081]{0:T(1024)S(1)}, f32[3081]{0:T(1024)S(1)}, u32[]{:S(2)}, u32[]{:S(2)}) collective-permute-start(f32[3081]{0:T(1024)S(1)} %add.339), channel_id=1, source_target_pairs={{0,4},{1,5},{2,6},{3,7},{4,0},{5,1},{6,2},{7,3},{8,12},{9,13},{10,... | collective-permute-start | bytes 36980 | tf_op jit(solution)/shard_map/ppermute | solution.py:393
  452.2 16.1 %collective-permute-start.19 = (f32[3081]{0:T(1024)S(1)}, f32[3081]{0:T(1024)S(1)}, u32[]{:S(2)}, u32[]{:S(2)}) collective-permute-start(f32[3081]{0:T(1024)S(1)} %add.340), channel_id=1, source_target_pairs={{0,8},{8,0},{16,24},{24,16},{1,9},{9,1},{17,25},{25,17},{2,10},{10... | collective-permute-start | bytes 36980 | tf_op jit(solution)/shard_map/ppermute | solution.py:393
  (51 other events, 1152.5 us)
Sparse Core Ops, SparseCore 0:
  42.4 34.9 all-gather.5
  79.8 23.9 all-gather.7
  105.6 53.5 all-gather.9
  161.0 46.1 all-gather.11
  385.7 30.6 reduce-scatter.14
  418.5 25.5 reduce-scatter.10
  446.3 20.4 reduce-scatter.8
  469.2 20.5 reduce-scatter.12
where the time goes:
time: 509 us; the launch traced here: 499 us
  waiting for transfers between devices  135 us (27%)
  local copies, waits for them, and re-layouts  116 us (23%)
  other arithmetic  63.5 us (12%)
  matrix products  62.2 us (12%)
  starting transfers between devices  52.5 us (10%)
  Pallas kernels  38 us (7%)
  blocking collectives  15.9 us (3%)
  between operations  15.5 us (3%)
    ppermute x12, waiting for transfers between devices, by_cols(): got = lax.ppermute(send.astype(jnp.bfloat16), 'seq', partner)  38.5 us
    all_to_all x1, waiting for transfers between devices, local(): lax.all_to_all(send, 'seq', split_axis=0, concat_axis=0, tiled=True)  31.8 us
    ppermute x4, waiting for transfers between devices, gather_rows(): got = lax.ppermute(acc, 'batch', partner)  27.9 us
    unnamed x118, local copies, waits for them, and re-layouts  20.9 us
    pallas_call x1, Pallas kernels, attn_backward(): pl.pallas_call(functools.partial(bwd_kernel, bk=bk, bq=bq, scale=scale),...  20.8 us
    ppermute x5, starting transfers between devices, local(): small_sums = small_sums + lax.ppermute(small_sums, axis, partner)  20.1 us
    pallas_call x1, Pallas kernels, attn_forward(): pl.pallas_call(functools.partial(fwd_kernel, bq=bq, bk=bk, scale=scale),...  17.1 us
    all_gather x1, blocking collectives, local(): lax.all_gather(lse_rows.reshape(per_dev, SLOT), 'seq', axis=0, tiled=True)  15.9 us
  transfers between devices with their start and end apart: 33, of which 12 were waited for; matrix products, arithmetic and copies ran while one was open for 38% of the time, Pallas kernels for 8%

commit v1 on v0

--- a/solution.py
+++ b/solution.py
@@ -273,9 +273,8 @@
             (n_batch,) + local.shape
         )
 
-    w_qkv = lax.all_gather(
-        gather_rows(qkv_weight).reshape(-1, qkv_weight.shape[1]), "seq", axis=1, tiled=True
-    )
+    qkv_rows = gather_rows(qkv_weight).reshape(-1, qkv_weight.shape[1])
+    w_qkv = lax.all_gather(qkv_rows, "seq", axis=1, tiled=True)
     inputs32 = block_input.astype(jnp.float32)
     norm1_out, normed1, inv_std1 = norm_rows(inputs32, norm1_gain, norm1_bias)
     norm1_low = norm1_out.astype(jnp.bfloat16)
@@ -291,7 +290,10 @@
     ).reshape(n_seq, per_dev, 3, HD, piece_len)
     incoming = lax.all_to_all(send, "seq", split_axis=0, concat_axis=0, tiled=True)
     later = (proj_weight, up_weight, down_weight)
-    later_rows = gather_rows(jnp.concatenate([w.reshape(-1) for w in later]))
+    later_flat, _ = lax.optimization_barrier(
+        (jnp.concatenate([w.reshape(-1) for w in later]), qkv_rows)
+    )
+    later_rows = gather_rows(later_flat)
     offset = 0
     later_full = []
     for w in later:
@@ -328,15 +330,24 @@
     dwa_local = jnp.stack(dwa_terms)
     dy_full = dwa_weights[HIST] * grad_out
     dmlp_low = dy_full.astype(jnp.bfloat16)
-    down_local = jnp.einsum("nf,nd->fd", gelu_low, dmlp_low, preferred_element_type=jnp.float32)
+    down_local = jnp.einsum(
+        "nf,nbd->bfd", gelu_low, dmlp_low.reshape(row_count, n_seq, -1),
+        preferred_element_type=jnp.float32,
+    )
     dgelu = jnp.einsum("nd,fd->nf", dmlp_low, w_down, preferred_element_type=jnp.float32)
     dup_low = gelu_pull(dgelu)[0].astype(jnp.bfloat16)
-    up_local = jnp.einsum("nd,nf->df", norm2_low, dup_low, preferred_element_type=jnp.float32)
+    up_local = jnp.einsum(
+        "nd,nbf->bdf", norm2_low, dup_low.reshape(row_count, n_seq, -1),
+        preferred_element_type=jnp.float32,
+    )
     dnorm2 = jnp.einsum("nf,df->nd", dup_low, w_up, preferred_element_type=jnp.float32)
     dmid_norm, gain2_local, bias2_local = norm_back(dnorm2, normed2, inv_std2, norm2_gain)
     dmiddle = dy_full + dmid_norm
     dmiddle_low = dmiddle.astype(jnp.bfloat16)
-    proj_local = jnp.einsum("nd,ne->de", attended, dmiddle_low, preferred_element_type=jnp.float32)
+    proj_local = jnp.einsum(
+        "nd,nbe->bde", attended, dmiddle_low.reshape(row_count, n_seq, -1),
+        preferred_element_type=jnp.float32,
+    )
     dattended = jnp.einsum(
         "ne,de->nd", dmiddle_low, w_proj, preferred_element_type=jnp.float32
     ).astype(jnp.bfloat16)
@@ -357,19 +368,21 @@
     dk_rows = unrotate(dtokens[:, :, 1].astype(jnp.float32), cosine, sine_tab).reshape(row_count, D)
     dv_rows = dtokens[:, :, 2].astype(jnp.float32).reshape(row_count, D)
     dqkv_low = jnp.concatenate([dq_rows, dk_rows, dv_rows], axis=-1).astype(jnp.bfloat16)
-    qkv_local = jnp.einsum("nd,nf->df", norm1_low, dqkv_low, preferred_element_type=jnp.float32)
+    qkv_local = jnp.einsum(
+        "nd,nbf->bdf", norm1_low, dqkv_low.reshape(row_count, n_seq, -1),
+        preferred_element_type=jnp.float32,
+    )
     dnorm1 = jnp.einsum("nf,df->nd", dqkv_low, w_qkv, preferred_element_type=jnp.float32)
     dinput_norm, gain1_local, bias1_local = norm_back(dnorm1, normed1, inv_std1, norm1_gain)
     input_grad = (dmiddle + dinput_norm).astype(jnp.bfloat16)
 
-    def by_cols(partial):
-        rows, cols = partial.shape
+    def by_cols(blocks):
         bits = n_seq.bit_length() - 1
-        acc = partial.reshape((rows,) + (2,) * bits + (cols // n_seq,))
+        acc = blocks.reshape((2,) * bits + blocks.shape[1:])
         for bit in range(bits):
             mine = (my_index >> bit) & 1
-            keep = lax.dynamic_index_in_dim(acc, mine, axis=acc.ndim - 2, keepdims=False)
-            send = lax.dynamic_index_in_dim(acc, 1 - mine, axis=acc.ndim - 2, keepdims=False)
+            keep = lax.dynamic_index_in_dim(acc, mine, axis=bits - 1 - bit, keepdims=False)
+            send = lax.dynamic_index_in_dim(acc, 1 - mine, axis=bits - 1 - bit, keepdims=False)
             partner = [(i, i ^ (1 << bit)) for i in range(n_seq)]
             got = lax.ppermute(send.astype(jnp.bfloat16), "seq", partner)
             acc = keep + got.astype(jnp.float32)

time: 509 us -> 508 us (level)
  local copies, waits for them, and re-layouts: 116 us -> 107 us
    all_gather x1, waiting for transfers between devices: 9.89 us -> 0.02 us  [local(): w_qkv = lax.all_gather(qkv_rows, 'seq', axis=1, tiled=True)]
    ppermute x4, waiting for transfers between devices: 27.9 us -> 36.7 us  [gather_rows(): got = lax.ppermute(acc, 'batch', partner)]
    reshape x4, local copies, waits for them, and re-layouts: 15.4 us -> 7.01 us  [the longest x1 4.81 us: local(): dup_low.reshape(row_count, n_seq, -1)]
    unnamed x118 -> x142, local copies, waits for them, and re-layouts: 20.9 us -> 29.1 us
    dot_general x1, matrix products: 4.84 us -> 12.3 us  [local(): hidden_up = jnp.dot(norm2_low, w_up, preferred_element_type=jnp.float32)]
    dot_general x4, matrix products: 16.1 us -> 10.8 us  [the longest x1 5 us: local(): jnp.einsum('nf,nbd->bfd', gelu_low, dmlp_low.reshape(row_count, n_seq, -1...]
    dynamic_slice x2 -> x3, local copies, waits for them, and re-layouts: 11.9 us -> 11.1 us  [the longest x2 8.49 us: by_cols(): lax.dynamic_index_in_dim(acc, mine, axis=bits - 1 - bit, keepdims=False)]
  transfers between devices with their start and end apart: 33 -> 33, of which waited for: 12 -> 13; matrix products, arithmetic and copies ran while one was open for 38% -> 34% of each run, Pallas kernels for 8% -> 8%
where the time goes in v1:
time: 508 us; the launch traced here: 499 us
  waiting for transfers between devices  134 us (26%)
  local copies, waits for them, and re-layouts  107 us (21%)
  other arithmetic  68.5 us (13%)
  matrix products  64.1 us (13%)
  starting transfers between devices  54.7 us (11%)
  Pallas kernels  38 us (7%)
  blocking collectives  16.8 us (3%)
  between operations  15.5 us (3%)
    ppermute x4, waiting for transfers between devices, gather_rows(): got = lax.ppermute(acc, 'batch', partner)  36.7 us
    ppermute x12, waiting for transfers between devices, by_cols(): got = lax.ppermute(send.astype(jnp.bfloat16), 'seq', partner)  36.5 us
    unnamed x142, local copies, waits for them, and re-layouts  29.1 us
    all_to_all x1, waiting for transfers between devices, local(): lax.all_to_all(send, 'seq', split_axis=0, concat_axis=0, tiled=True)  28.3 us
    pallas_call x1, Pallas kernels, attn_backward(): pl.pallas_call(functools.partial(bwd_kernel, bk=bk, bq=bq, scale=scale),...  20.9 us
    ppermute x5, starting transfers between devices, local(): small_sums = small_sums + lax.ppermute(small_sums, axis, partner)  18 us
    pallas_call x1, Pallas kernels, attn_forward(): pl.pallas_call(functools.partial(fwd_kernel, bq=bq, bk=bk, scale=scale),...  17.1 us
    add x8, other arithmetic, by_cols(): acc = keep + got.astype(jnp.float32)  16.8 us
  transfers between devices with their start and end apart: 33, of which 13 were waited for; matrix products, arithmetic and copies ran while one was open for 34% of the time, Pallas kernels for 8%

profile of v1, /device:TPU:0, one launch (start us, length us, event | category | flops | bytes accessed | tf_op | source)
XLA Modules:
  0.0 499.0 jit_solution(1156320763831191151)
XLA Ops:
  7.2 4.1 collective-permute-start
  14.7 3.9 collective-permute-done
  20.7 7.2 %collective-permute-done.1 = bf16[2,192,288]{2,1,0:T(8,128)(2,1)S(1)} collective-permute-done((bf16[2,192,288]{2,1,0:T(8,128)(2,1)S(1)}, bf16[2,192,288]{2,1,0:T(8,128)(2,1)S(1)}, u32[]{:S(2)}, u32[]{:S(2)}) %collective-permute-start.1) | collective-permute-done | bytes 221216 | tf_op jit(solution)/shard_map/ppermute | solution.py:269
  33.9 13.6 %collective-permute-done.2 = bf16[165888]{0:T(1024)(128)(2,1)S(1)} collective-permute-done((bf16[165888]{0:T(1024)(128)(2,1)S(1)}, bf16[165888]{0:T(1024)(128)(2,1)S(1)}, u32[]{:S(2)}, u32[]{:S(2)}) %collective-permute-start.2) | collective-permute-done | bytes 331808 | tf_op jit(solution)/shard_map/ppermute | solution.py:269
  54.9 11.9 %collective-permute-done.3 = bf16[2,165888]{1,0:T(2,128)(2,1)S(1)} collective-permute-done((bf16[2,165888]{1,0:T(2,128)(2,1)S(1)}, bf16[2,165888]{1,0:T(2,128)(2,1)S(1)}, u32[]{:S(2)}, u32[]{:S(2)}) %collective-permute-start.3) | collective-permute-done | bytes 663584 | tf_op jit(solution)/shard_map/ppermute | solution.py:269
  68.8 4.1 copy.153
  81.0 4.2 fusion.73
  101.6 4.3 all-to-all-start
  113.3 28.3 %all-to-all-done = bf16[8,3,3,64,256]{4,3,2,1,0:T(8,128)(2,1)S(1)} async-done(((bf16[8,3,3,64,256]{4,3,2,1,0:T(8,128)(2,1)}), bf16[8,3,3,64,256]{4,3,2,1,0:T(8,128)(2,1)S(1)}, u32[]{:S(2)}, u32[]{:S(2)}) %all-to-all-start) | async-done | bytes 2359328 | tf_op jit(solution)/shard_map/all_to_all | solution.py:291
  143.3 17.1 %attn_fwd.1 = (bf16[3,64,2048]{2,1,0:T(8,128)(2,1)}, f32[3,1,2048]{2,1,0:T(1,128)}) custom-call(s32[3]{0:T(128)} %and_select_fusion.2.seg_ref, bf16[3,3,64,2048]{3,2,1,0:T(8,128)(2,1)} %bitcast.307, bf16[3,3,64,2048]{3,2,1,0:T(8,128)(2,1)} %bitcast.308, bf16[3,3,64,2048]{3,2,1,0:T(8,128)(2,1)} %bitcast.309), custom_call_target="tpu_custom_call" | custom-call | flops 2013265920 | bytes 3170304 | tf_op jit(solution)/shard_map/attn_fwd/pallas_call | solution.py:86
  166.9 4.5 multiply_convert_fusion
  171.4 16.8 %all-gather = f32[24,1,2048]{2,1,0:T(1,128)S(1)} all-gather(f32[3,1,2048]{2,1,0:T(1,128)S(1)} %copy-done.41), channel_id=2, replica_groups=mesh['batch'=4,'seq'=8] {'seq'}, dimensions={0}, use_global_device_ids=true | all-gather | bytes 221184 | tf_op jit(solution)/shard_map/all_gather | solution.py:308
  195.1 7.0 %fusion.84 = f32[512,3072]{1,0:T(8,128)} fusion(bf16[512,768]{1,0:T(8,128)(2,1)S(1)} %copy-done.5, bf16[3072,768]{0,1:T(8,128)(2,1)} %all-gather.12.cloned.1.call-done), kind=kOutput, calls=%fused_computation.201 | convolution fusion | flops 2415919104 | bytes 11796480 | tf_op jit(solution)/shard_map/nd,fd->nf/dot_general | solution.py:337
  202.0 4.7 all-gather.10.cloned.1.call-done
  206.7 12.3 %fusion.6 = (bf16[512,3072]{1,0:T(8,128)(2,1)}, f32[512,3072]{1,0:T(8,128)}) fusion(f32[512,3072]{1,0:T(8,128)} %fusion.84, bf16[768,3072]{1,0:T(8,128)(2,1)} %all-gather.10.cloned.1.call-done, f32[512,768]{1,0:T(8,128)S(1)} %get-tuple-element.145, f32[768]{0:T(1024)S(1)} %copy-done.53, f32[768]{0:T(1024)S(1)} %copy-done.46, f32[512]{0:T(512)S(1)} %add_rsqrt_fusion, ...), kind=kOutput, calls=%fused_computation.11 | convolution fusion | flops 2449342464 | bytes 22030336 | tf_op jit(solution)/shard_map/dot_general | solution.py:316
  219.0 4.8 copy.181
  223.8 7.5 %multiply_reduce_fusion = (f32[768]{0:T(1024)}, f32[512]{0:T(512)S(1)}, f32[512]{0:T(512)S(1)}, f32[768]{0:T(1024)}, f32[512,768]{1,0:T(8,128)S(1)}) fusion(f32[512,768]{1,0:T(8,128)} %copy-done.11, f32[512]{0:T(512)S(1)} %add_rsqrt_fusion, f32[512]{0:T(512)S(1)} %broadcast_multiply_fusion.5, f32[768]{0:T(1024)S(1)} %copy-done.46, ...), kind=kOutput, calls=%fused_computation.92 | convolution fusion | flops 2419455488 | bytes 11027456 | tf_op jit(solution)/shard_map/nf,df->nd/dot_general | solution.py:343
  231.3 13.7 %fusion.36 = (bf16[512,768]{1,0:T(8,128)(2,1)}, f32[512,768]{1,0:T(8,128)S(1)}) fusion(f32[]{:T(128)} %bitcast.34, f32[]{:T(128)} %bitcast.32, f32[]{:T(128)} %bitcast.30, f32[]{:T(128)} %bitcast.28, f32[]{:T(128)} %bitcast.26, f32[]{:T(128)} %bitcast.24, f32[]{:T(128)} %bitcast.22, f32[]{:T(128)} %bitcast.20, f32[]{:T(128)} %bitcast, ...), kind=kOutput, calls=%fused_computation.79 | convolution fusion | flops 2440691712 | bytes 21233700 | tf_op jit(solution)/shard_map/dot_general | solution.py:319
  245.0 4.8 fusion.44
  254.9 4.2 all-to-all-start.2
  259.2 5.0 %fusion.7 = f32[8,96,3072]{2,1,0:T(8,128)S(1)} fusion(bf16[512,8,96]{0,2,1:T(8,128)(2,1)S(1)} %bitcast.318, f32[512,3072]{1,0:T(8,128)} %get-tuple-element.149), kind=kOutput, calls=%fused_computation.29 | convolution fusion | flops 2430074880 | bytes 16515072 | tf_op jit(solution)/shard_map/nf,nbd->bfd/dot_general | solution.py:333
  280.5 6.1 %copy.169 = f32[2,2,1,768,384]{4,3,0,1,2:T(8,128)} copy(f32[2,2,1,768,384]{3,4,2,1,0:T(8,128)} %constant_dynamic-slice_fusion.3) | data formatting | bytes 9437184 | tf_op jit(solution)/shard_map/jit(dynamic_index_in_dim)/dynamic_slice | solution.py:384
  298.1 20.9 %attn_bwd.1 = bf16[3,3,64,2048]{3,2,1,0:T(8,128)(2,1)} custom-call(s32[3]{0:T(128)} %and_select_fusion.2.seg_ref, bf16[3,3,64,2048]{3,2,1,0:T(8,128)(2,1)} %bitcast.310, bf16[3,3,64,2048]{3,2,1,0:T(8,128)(2,1)} %bitcast.311, bf16[3,3,64,2048]{3,2,1,0:T(8,128)(2,1)} %bitcast.312, bf16[3,64,2048]{2,1,0:T(8,128)(2,1)} %bitcast.319, ...), custom_call_target="tpu_custom_call" | custom-call | flops 5033164800 | bytes 6316032 | tf_op jit(solution)/shard_map/attn_bwd/pallas_call | solution.py:174
  330.2 3.7 bitcast_add_fusion
  341.6 14.3 %all-to-all-done.3 = bf16[8,3,3,64,256]{4,3,2,1,0:T(8,128)(2,1)S(1)} async-done(((bf16[8,3,3,64,256]{4,3,2,1,0:T(8,128)(2,1)}), bf16[8,3,3,64,256]{4,3,2,1,0:T(8,128)(2,1)S(1)}, u32[]{:S(2)}, u32[]{:S(2)}) %all-to-all-start.3) | async-done | bytes 2359328 | tf_op jit(solution)/shard_map/all_to_all | solution.py:363
  368.4 12.0 %collective-permute-done.14 = bf16[2,3072,96]{1,2,0:T(8,128)(2,1)} collective-permute-done((bf16[2,3072,96]{1,2,0:T(8,128)(2,1)}, bf16[2,3072,96]{1,2,0:T(8,128)(2,1)}, u32[]{:S(2)}, u32[]{:S(2)}) %collective-permute-start.14) | collective-permute-done | bytes 1179680 | tf_op jit(solution)/shard_map/ppermute | solution.py:387
  387.8 17.3 %collective-permute-done.11 = bf16[2,768,384]{2,1,0:T(8,128)(2,1)} collective-permute-done((bf16[2,768,384]{2,1,0:T(8,128)(2,1)S(1)}, bf16[2,768,384]{2,1,0:T(8,128)(2,1)}, u32[]{:S(2)}, u32[]{:S(2)}) %collective-permute-start.11) | collective-permute-done | bytes 1179680 | tf_op jit(solution)/shard_map/ppermute | solution.py:387
  418.5 4.1 fusion.26
  422.6 6.3 %concatenate.59 = f32[3081]{0:T(1024)S(1)} concatenate(f32[768]{0:T(1024)} %get-tuple-element.98, f32[768]{0:T(1024)} %get-tuple-element.103, f32[768]{0:T(1024)} %get-tuple-element.96, f32[768]{0:T(1024)} %get-tuple-element.102, f32[1]{0:T(128)} %bitcast.98, f32[1]{0:T(128)} %bitcast.100, f32[1]{0:T(128)} %bitcast.102, f32[1]{0:T(128)} %bitcast.104, f32[1]{0:T(128)} %bitcast.106, ...), dimensions={0} | concatenate | bytes 24648 | tf_op jit(solution)/shard_map/concatenate | solution.py:400
  446.7 5.5 %collective-permute-done.6 = bf16[768,288]{0,1:T(8,128)(2,1)S(1)} collective-permute-done((bf16[768,288]{0,1:T(8,128)(2,1)S(1)}, bf16[768,288]{0,1:T(8,128)(2,1)S(1)}, u32[]{:S(2)}, u32[]{:S(2)}) %collective-permute-start.6) | collective-permute-done | bytes 442400 | tf_op jit(solution)/shard_map/ppermute | solution.py:387
  454.5 12.2 %collective-permute-start.19 = (f32[3081]{0:T(1024)S(1)}, f32[3081]{0:T(1024)S(1)}, u32[]{:S(2)}, u32[]{:S(2)}) collective-permute-start(f32[3081]{0:T(1024)S(1)} %add.340), channel_id=1, source_target_pairs={{0,8},{8,0},{16,24},{24,16},{1,9},{9,1},{17,25},{25,17},{2,10},{10... | collective-permute-start | bytes 36980 | tf_op jit(solution)/shard_map/ppermute | solution.py:406
  478.7 11.4 %reduce-scatter.13.cloned.1.call-done = bf16[192,288]{1,0:T(8,128)(2,1)} async-done(((bf16[768,288]{1,0:T(8,128)(2,1)}), bf16[192,288]{1,0:T(8,128)(2,1)}) %reduce-scatter.13.cloned.1.call-update) | async-done | bytes 110608
  (331 shorter events, 185.7 us)
Async XLA Ops:
  7.2 73.8 %all-gather.6.cloned.1.call-start = ((), (), s32[]{:S(2)}) async-start(), calls=%async_computation.8 | async-start | bytes 3981312 | tf_op jit(solution)/shard_map/all_gather | solution.py:277
  7.2 11.4 %collective-permute-start = (bf16[192,288]{1,0:T(8,128)(2,1)}, bf16[192,288]{1,0:T(8,128)(2,1)S(1)}, u32[]{:S(2)}, u32[]{:S(2)}) collective-permute-start(bf16[192,288]{1,0:T(8,128)(2,1)} %param.17), channel_id=1, source_target_pairs={{0,16},{8,24},{16,0},{24,8},{1,17},{9,25},{17,1},{25,9},{2,18},{10... | collective-permute-start | bytes 331784 | tf_op jit(solution)/shard_map/ppermute | solution.py:269
  19.7 8.2 %collective-permute-start.1 = (bf16[2,192,288]{2,1,0:T(8,128)(2,1)S(1)}, bf16[2,192,288]{2,1,0:T(8,128)(2,1)S(1)}, u32[]{:S(2)}, u32[]{:S(2)}) collective-permute-start(bf16[2,192,288]{2,1,0:T(8,128)(2,1)S(1)} %maximum_select_fusion.2), channel_id=1, source_target_pairs={{0,8},{8,0},{16,24},{24,16},{1,9},{9,1},{17,25},{25,17},{2,10},{10... | collective-permute-start | bytes 663560 | tf_op jit(solution)/shard_map/ppermute | solution.py:269
  29.9 17.6 %collective-permute-start.2 = (bf16[165888]{0:T(1024)(128)(2,1)S(1)}, bf16[165888]{0:T(1024)(128)(2,1)S(1)}, u32[]{:S(2)}, u32[]{:S(2)}) collective-permute-start(bf16[165888]{0:T(1024)(128)(2,1)S(1)} %pad_maximum_fusion.5), channel_id=1, source_target_pairs={{0,16},{8,24},{16,0},{24,8},{1,17},{9,25},{17,1},{25,9},{2,18},{10... | collective-permute-start | bytes 995336 | tf_op jit(solution)/shard_map/ppermute | solution.py:269
  33.0 157.8 %all-gather.8.cloned.1.call-start = ((), (), s32[]{:S(2)}) async-start(), calls=%async_computation.9 | async-start | bytes 1327104 | tf_op jit(solution)/shard_map/all_gather | solution.py:301
  50.8 16.0 %collective-permute-start.3 = (bf16[2,165888]{1,0:T(2,128)(2,1)S(1)}, bf16[2,165888]{1,0:T(2,128)(2,1)S(1)}, u32[]{:S(2)}, u32[]{:S(2)}) collective-permute-start(bf16[2,165888]{1,0:T(2,128)(2,1)S(1)} %broadcast_select_fusion.1), channel_id=1, source_target_pairs={{0,8},{8,0},{16,24},{24,16},{1,9},{9,1},{17,25},{25,17},{2,10},{10... | collective-permute-start | bytes 1990664 | tf_op jit(solution)/shard_map/ppermute | solution.py:269
  74.4 119.3 %all-gather.12.cloned.1.call-start = ((), (), s32[]{:S(2)}) async-start(), calls=%async_computation.11 | async-start | bytes 5308416 | tf_op jit(solution)/shard_map/all_gather | solution.py:301
  76.7 130.0 %all-gather.10.cloned.1.call-start = ((), (), s32[]{:S(2)}) async-start(), calls=%async_computation.10 | async-start | bytes 5308416 | tf_op jit(solution)/shard_map/all_gather | solution.py:301
  101.6 39.9 %all-to-all-start = ((bf16[8,3,3,64,256]{4,3,2,1,0:T(8,128)(2,1)}), bf16[8,3,3,64,256]{4,3,2,1,0:T(8,128)(2,1)S(1)}, u32[]{:S(2)}, u32[]{:S(2)}) async-start(bf16[8,3,3,64,256]{4,3,2,1,0:T(8,128)(2,1)} %copy.148), calls=%async_computation | async-start | bytes 4718592 | tf_op jit(solution)/shard_map/all_to_all | solution.py:291
  162.6 26.3 %all-to-all-start.1 = ((bf16[8,3,64,256]{3,2,1,0:T(8,128)(2,1)}), bf16[8,3,64,256]{3,2,1,0:T(8,128)(2,1)S(1)}, u32[]{:S(2)}, u32[]{:S(2)}) async-start(bf16[8,3,64,256]{3,2,1,0:T(8,128)(2,1)} %bitcast.298), calls=%async_computation.1 | async-start | bytes 1572864 | tf_op jit(solution)/shard_map/all_to_all | solution.py:307
  254.9 41.0 %all-to-all-start.2 = ((bf16[8,3,64,256]{3,2,1,0:T(8,128)(2,1)}), bf16[8,3,64,256]{3,2,1,0:T(8,128)(2,1)}, u32[]{:S(2)}, u32[]{:S(2)}) async-start(bf16[8,3,64,256]{3,2,1,0:T(8,128)(2,1)} %bitcast.37), calls=%async_computation.2 | async-start | bytes 1572864 | tf_op jit(solution)/shard_map/all_to_all | solution.py:357
  265.9 64.3 %collective-permute-start.13 = (bf16[2,2,3072,96]{2,3,0,1:T(8,128)(2,1)}, bf16[2,2,3072,96]{2,3,0,1:T(8,128)(2,1)}, u32[]{:S(2)}, u32[]{:S(2)}) collective-permute-start(bf16[2,2,3072,96]{2,3,0,1:T(8,128)(2,1)} %fusion.9), channel_id=1, source_target_pairs={{0,1},{1,0},{2,3},{3,2},{4,5},{5,4},{6,7},{7,6},{8,9},{9,8},{10,11... | collective-permute-start | bytes 7077896 | tf_op jit(solution)/shard_map/ppermute | solution.py:387
  270.5 21.5 %collective-permute-start.7 = (bf16[2,2,768,96]{2,3,1,0:T(8,128)(2,1)S(1)}, bf16[2,2,768,96]{2,3,1,0:T(8,128)(2,1)}, u32[]{:S(2)}, u32[]{:S(2)}) collective-permute-start(bf16[2,2,768,96]{2,3,1,0:T(8,128)(2,1)S(1)} %fusion.63), channel_id=1, source_target_pairs={{0,1},{1,0},{2,3},{3,2},{4,5},{5,4},{6,7},{7,6},{8,9},{9,8},{10,11... | collective-permute-start | bytes 1769480 | tf_op jit(solution)/shard_map/ppermute | solution.py:387
  291.6 45.0 %collective-permute-start.10 = (bf16[2,2,768,384]{3,2,0,1:T(8,128)(2,1)}, bf16[2,2,768,384]{3,2,0,1:T(8,128)(2,1)}, u32[]{:S(2)}, u32[]{:S(2)}) collective-permute-start(bf16[2,2,768,384]{3,2,0,1:T(8,128)(2,1)} %bitcast.313), channel_id=1, source_target_pairs={{0,1},{1,0},{2,3},{3,2},{4,5},{5,4},{6,7},{7,6},{8,9},{9,8},{10,11... | collective-permute-start | bytes 7077896 | tf_op jit(solution)/shard_map/ppermute | solution.py:387
  294.3 32.1 %collective-permute-start.8 = (bf16[2,768,96]{1,2,0:T(8,128)(2,1)}, bf16[2,768,96]{1,2,0:T(8,128)(2,1)}, u32[]{:S(2)}, u32[]{:S(2)}) collective-permute-start(bf16[2,768,96]{1,2,0:T(8,128)(2,1)} %fusion.66), channel_id=1, source_target_pairs={{0,2},{1,3},{2,0},{3,1},{4,6},{5,7},{6,4},{7,5},{8,10},{9,11},{10,... | collective-permute-start | bytes 884744 | tf_op jit(solution)/shard_map/ppermute | solution.py:387
  322.3 33.6 %all-to-all-start.3 = ((bf16[8,3,3,64,256]{4,3,2,1,0:T(8,128)(2,1)}), bf16[8,3,3,64,256]{4,3,2,1,0:T(8,128)(2,1)S(1)}, u32[]{:S(2)}, u32[]{:S(2)}) async-start(bf16[8,3,3,64,256]{4,3,2,1,0:T(8,128)(2,1)} %bitcast.275), calls=%async_computation.3 | async-start | bytes 4718592 | tf_op jit(solution)/shard_map/all_to_all | solution.py:363
  325.9 116.8 %reduce-scatter.15.cloned.1.call-start = ((), (), s32[]{:S(2)}) async-start(), calls=%async_computation.15 | async-start | bytes 245760
  328.3 56.1 %collective-permute-start.9 = (bf16[768,96]{0,1:T(8,128)(2,1)}, bf16[768,96]{0,1:T(8,128)(2,1)}, u32[]{:S(2)}, u32[]{:S(2)}) collective-permute-start(bf16[768,96]{0,1:T(8,128)(2,1)} %fusion.68), channel_id=1, source_target_pairs={{0,4},{1,5},{2,6},{3,7},{4,0},{5,1},{6,2},{7,3},{8,12},{9,13},{10,... | collective-permute-start | bytes 442376 | tf_op jit(solution)/shard_map/ppermute | solution.py:387
  335.2 45.2 %collective-permute-start.14 = (bf16[2,3072,96]{1,2,0:T(8,128)(2,1)}, bf16[2,3072,96]{1,2,0:T(8,128)(2,1)}, u32[]{:S(2)}, u32[]{:S(2)}) collective-permute-start(bf16[2,3072,96]{1,2,0:T(8,128)(2,1)} %fusion.48), channel_id=1, source_target_pairs={{0,2},{1,3},{2,0},{3,1},{4,6},{5,7},{6,4},{7,5},{8,10},{9,11},{10,... | collective-permute-start | bytes 3538952 | tf_op jit(solution)/shard_map/ppermute | solution.py:387
  341.0 64.1 %collective-permute-start.11 = (bf16[2,768,384]{2,1,0:T(8,128)(2,1)S(1)}, bf16[2,768,384]{2,1,0:T(8,128)(2,1)}, u32[]{:S(2)}, u32[]{:S(2)}) collective-permute-start(bf16[2,768,384]{2,1,0:T(8,128)(2,1)S(1)} %fusion.47), channel_id=1, source_target_pairs={{0,2},{1,3},{2,0},{3,1},{4,6},{5,7},{6,4},{7,5},{8,10},{9,11},{10,... | collective-permute-start | bytes 3538952 | tf_op jit(solution)/shard_map/ppermute | solution.py:387
  368.4 45.0 %collective-permute-start.4 = (bf16[2,2,768,288]{2,3,1,0:T(8,128)(2,1)}, bf16[2,2,768,288]{2,3,1,0:T(8,128)(2,1)}, u32[]{:S(2)}, u32[]{:S(2)}) collective-permute-start(bf16[2,2,768,288]{2,3,1,0:T(8,128)(2,1)} %fusion.18), channel_id=1, source_target_pairs={{0,1},{1,0},{2,3},{3,2},{4,5},{5,4},{6,7},{7,6},{8,9},{9,8},{10,11... | collective-permute-start | bytes 5308424 | tf_op jit(solution)/shard_map/ppermute | solution.py:387
  382.9 28.3 %collective-permute-start.15 = (bf16[3072,96]{0,1:T(8,128)(2,1)}, bf16[3072,96]{0,1:T(8,128)(2,1)}, u32[]{:S(2)}, u32[]{:S(2)}) collective-permute-start(bf16[3072,96]{0,1:T(8,128)(2,1)} %fusion.62), channel_id=1, source_target_pairs={{0,4},{1,5},{2,6},{3,7},{4,0},{5,1},{6,2},{7,3},{8,12},{9,13},{10,... | collective-permute-start | bytes 1769480 | tf_op jit(solution)/shard_map/ppermute | solution.py:387
  387.7 87.7 %reduce-scatter.11.cloned.1.call-start = ((), (), s32[]{:S(2)}) async-start(), calls=%async_computation.13 | async-start | bytes 737280 | tf_op jit(solution)/shard_map/reduce_scatter | solution.py:392
  409.7 19.3 %collective-permute-start.12 = (bf16[768,384]{1,0:T(8,128)(2,1)}, bf16[768,384]{1,0:T(8,128)(2,1)}, u32[]{:S(2)}, u32[]{:S(2)}) collective-permute-start(bf16[768,384]{1,0:T(8,128)(2,1)} %fusion.61), channel_id=1, source_target_pairs={{0,4},{1,5},{2,6},{3,7},{4,0},{5,1},{6,2},{7,3},{8,12},{9,13},{10,... | collective-permute-start | bytes 1769480 | tf_op jit(solution)/shard_map/ppermute | solution.py:387
  413.2 63.8 %reduce-scatter.9.cloned.1.call-start = ((), (), s32[]{:S(2)}) async-start(), calls=%async_computation.12 | async-start | bytes 737280 | tf_op jit(solution)/shard_map/reduce_scatter | solution.py:392
  417.6 21.1 %collective-permute-start.5 = (bf16[2,768,288]{1,2,0:T(8,128)(2,1)}, bf16[2,768,288]{1,2,0:T(8,128)(2,1)}, u32[]{:S(2)}, u32[]{:S(2)}) collective-permute-start(bf16[2,768,288]{1,2,0:T(8,128)(2,1)} %fusion.51), channel_id=1, source_target_pairs={{0,2},{1,3},{2,0},{3,1},{4,6},{5,7},{6,4},{7,5},{8,10},{9,11},{10,... | collective-permute-start | bytes 2654216 | tf_op jit(solution)/shard_map/ppermute | solution.py:387
  428.9 6.0 %collective-permute-start.16 = (f32[3081]{0:T(1024)S(1)}, f32[3081]{0:T(1024)}, u32[]{:S(2)}, u32[]{:S(2)}) collective-permute-start(f32[3081]{0:T(1024)S(1)} %concatenate.59), channel_id=1, source_target_pairs={{0,1},{1,0},{2,3},{3,2},{4,5},{5,4},{6,7},{7,6},{8,9},{9,8},{10,11... | collective-permute-start | bytes 36980 | tf_op jit(solution)/shard_map/ppermute | solution.py:406
  431.4 58.7 %reduce-scatter.13.cloned.1.call-start = ((), (), s32[]{:S(2)}) async-start(), calls=%async_computation.14 | async-start | bytes 737280
  435.7 8.7 %collective-permute-start.17 = (f32[3081]{0:T(1024)S(1)}, f32[3081]{0:T(1024)}, u32[]{:S(2)}, u32[]{:S(2)}) collective-permute-start(f32[3081]{0:T(1024)S(1)} %add.338), channel_id=1, source_target_pairs={{0,2},{1,3},{2,0},{3,1},{4,6},{5,7},{6,4},{7,5},{8,10},{9,11},{10,... | collective-permute-start | bytes 36980 | tf_op jit(solution)/shard_map/ppermute | solution.py:406
  441.4 10.8 %collective-permute-start.6 = (bf16[768,288]{0,1:T(8,128)(2,1)S(1)}, bf16[768,288]{0,1:T(8,128)(2,1)S(1)}, u32[]{:S(2)}, u32[]{:S(2)}) collective-permute-start(bf16[768,288]{0,1:T(8,128)(2,1)S(1)} %fusion.65), channel_id=1, source_target_pairs={{0,4},{1,5},{2,6},{3,7},{4,0},{5,1},{6,2},{7,3},{8,12},{9,13},{10,... | collective-permute-start | bytes 1327112 | tf_op jit(solution)/shard_map/ppermute | solution.py:387
  445.1 9.4 %collective-permute-start.18 = (f32[3081]{0:T(1024)S(1)}, f32[3081]{0:T(1024)S(1)}, u32[]{:S(2)}, u32[]{:S(2)}) collective-permute-start(f32[3081]{0:T(1024)S(1)} %add.339), channel_id=1, source_target_pairs={{0,4},{1,5},{2,6},{3,7},{4,0},{5,1},{6,2},{7,3},{8,12},{9,13},{10,... | collective-permute-start | bytes 36980 | tf_op jit(solution)/shard_map/ppermute | solution.py:406
  454.5 13.9 %collective-permute-start.19 = (f32[3081]{0:T(1024)S(1)}, f32[3081]{0:T(1024)S(1)}, u32[]{:S(2)}, u32[]{:S(2)}) collective-permute-start(f32[3081]{0:T(1024)S(1)} %add.340), channel_id=1, source_target_pairs={{0,8},{8,0},{16,24},{24,16},{1,9},{9,1},{17,25},{25,17},{2,10},{10... | collective-permute-start | bytes 36980 | tf_op jit(solution)/shard_map/ppermute | solution.py:406
  (65 other events, 1164.3 us)
Sparse Core Ops, SparseCore 0:
  33.2 33.2 all-gather.5
  74.6 25.9 all-gather.7
  102.5 54.5 all-gather.11
  158.8 47.8 all-gather.9
  387.8 28.4 reduce-scatter.14
  418.4 25.8 reduce-scatter.10
  446.6 20.5 reduce-scatter.8
  469.5 20.5 reduce-scatter.12

commit v2 on v1

--- a/solution.py
+++ b/solution.py
@@ -290,10 +290,7 @@
     ).reshape(n_seq, per_dev, 3, HD, piece_len)
     incoming = lax.all_to_all(send, "seq", split_axis=0, concat_axis=0, tiled=True)
     later = (proj_weight, up_weight, down_weight)
-    later_flat, _ = lax.optimization_barrier(
-        (jnp.concatenate([w.reshape(-1) for w in later]), qkv_rows)
-    )
-    later_rows = gather_rows(later_flat)
+    later_rows = gather_rows(jnp.concatenate([w.reshape(-1) for w in later]))
     offset = 0
     later_full = []
     for w in later:

time: 508 us -> 517 us (1.018)
  waiting for transfers between devices: 134 us -> 152 us
    all_gather x3, waiting for transfers between devices: 4.7 us -> 19.1 us  [local(): later_full.append(lax.all_gather(rows, 'seq', axis=1, tiled=True))]
    all_gather x1, waiting for transfers between devices: 0.02 us -> 9.91 us  [local(): w_qkv = lax.all_gather(qkv_rows, 'seq', axis=1, tiled=True)]
    ppermute x4, waiting for transfers between devices: 36.7 us -> 27.9 us  [gather_rows(): got = lax.ppermute(acc, 'batch', partner)]
    unnamed x142 -> x144, local copies, waits for them, and re-layouts: 29.1 us -> 27.6 us
  transfers between devices with their start and end apart: 33 -> 33, of which waited for: 13 -> 13; matrix products, arithmetic and copies ran while one was open for 34% -> 34% of each run, Pallas kernels for 8% -> 7%
where the time goes in v2:
time: 517 us; the launch traced here: 508 us
  waiting for transfers between devices  152 us (29%)
  local copies, waits for them, and re-layouts  105 us (20%)
  other arithmetic  67.1 us (13%)
  matrix products  63.9 us (12%)
  starting transfers between devices  51.5 us (10%)
  Pallas kernels  38 us (7%)
  between operations  15.9 us (3%)
  blocking collectives  14.7 us (3%)
    ppermute x12, waiting for transfers between devices, by_cols(): got = lax.ppermute(send.astype(jnp.bfloat16), 'seq', partner)  36.5 us
    all_to_all x1, waiting for transfers between devices, local(): lax.all_to_all(send, 'seq', split_axis=0, concat_axis=0, tiled=True)  30.8 us
    ppermute x4, waiting for transfers between devices, gather_rows(): got = lax.ppermute(acc, 'batch', partner)  27.9 us
    unnamed x144, local copies, waits for them, and re-layouts  27.6 us
    pallas_call x1, Pallas kernels, attn_backward(): pl.pallas_call(functools.partial(bwd_kernel, bk=bk, bq=bq, scale=scale),...  20.9 us
    all_gather x3, waiting for transfers between devices, local(): later_full.append(lax.all_gather(rows, 'seq', axis=1, tiled=True))  19.1 us
    ppermute x5, starting transfers between devices, local(): small_sums = small_sums + lax.ppermute(small_sums, axis, partner)  18.1 us
    pallas_call x1, Pallas kernels, attn_forward(): pl.pallas_call(functools.partial(fwd_kernel, bq=bq, bk=bk, scale=scale),...  17.1 us
  transfers between devices with their start and end apart: 33, of which 13 were waited for; matrix products, arithmetic and copies ran while one was open for 34% of the time, Pallas kernels for 7%

profile of v2, /device:TPU:0, one launch (start us, length us, event | category | flops | bytes accessed | tf_op | source)
XLA Modules:
  0.0 508.0 jit_solution(16051658092936124885)
XLA Ops:
  7.2 4.1 collective-permute-start
  15.6 10.8 %collective-permute-done = bf16[192,288]{1,0:T(8,128)(2,1)S(1)} collective-permute-done((bf16[192,288]{1,0:T(8,128)(2,1)}, bf16[192,288]{1,0:T(8,128)(2,1)S(1)}, u32[]{:S(2)}, u32[]{:S(2)}) %collective-permute-start) | collective-permute-done | bytes 110624 | tf_op jit(solution)/shard_map/ppermute | solution.py:269
  26.9 6.0 %collective-permute-done.2 = bf16[165888]{0:T(1024)(128)(2,1)S(1)} collective-permute-done((bf16[165888]{0:T(1024)(128)(2,1)S(1)}, bf16[165888]{0:T(1024)(128)(2,1)S(1)}, u32[]{:S(2)}, u32[]{:S(2)}) %collective-permute-start.2) | collective-permute-done | bytes 331808 | tf_op jit(solution)/shard_map/ppermute | solution.py:269
  42.3 11.0 %collective-permute-done.3 = bf16[2,165888]{1,0:T(2,128)(2,1)S(1)} collective-permute-done((bf16[2,165888]{1,0:T(2,128)(2,1)S(1)}, bf16[2,165888]{1,0:T(2,128)(2,1)S(1)}, u32[]{:S(2)}, u32[]{:S(2)}) %collective-permute-start.3) | collective-permute-done | bytes 663584 | tf_op jit(solution)/shard_map/ppermute | solution.py:269
  55.3 4.1 copy.153
  67.4 9.9 %all-gather.6.cloned.1.call-done = bf16[768,2304]{0,1:T(8,128)(2,1)} async-done(((bf16[768,288]{0,1:T(8,128)(2,1)}), bf16[768,2304]{0,1:T(8,128)(2,1)}) %all-gather.6.cloned.1.call-update) | async-done | bytes 3538960 | tf_op jit(solution)/shard_map/all_gather | solution.py:277
  77.3 4.2 fusion.73
  97.9 4.2 all-to-all-start
  107.1 4.5 multiply_convert_fusion
  111.6 30.8 %all-to-all-done = bf16[8,3,3,64,256]{4,3,2,1,0:T(8,128)(2,1)S(1)} async-done(((bf16[8,3,3,64,256]{4,3,2,1,0:T(8,128)(2,1)}), bf16[8,3,3,64,256]{4,3,2,1,0:T(8,128)(2,1)S(1)}, u32[]{:S(2)}, u32[]{:S(2)}) %all-to-all-start) | async-done | bytes 2359328 | tf_op jit(solution)/shard_map/all_to_all | solution.py:291
  144.2 17.1 %attn_fwd.1 = (bf16[3,64,2048]{2,1,0:T(8,128)(2,1)}, f32[3,1,2048]{2,1,0:T(1,128)}) custom-call(s32[3]{0:T(128)} %and_select_fusion.2.seg_ref, bf16[3,3,64,2048]{3,2,1,0:T(8,128)(2,1)} %bitcast.306, bf16[3,3,64,2048]{3,2,1,0:T(8,128)(2,1)} %bitcast.307, bf16[3,3,64,2048]{3,2,1,0:T(8,128)(2,1)} %bitcast.308), custom_call_target="tpu_custom_call" | custom-call | flops 2013265920 | bytes 3170304 | tf_op jit(solution)/shard_map/attn_fwd/pallas_call | solution.py:86
  168.9 14.7 %all-gather = f32[24,1,2048]{2,1,0:T(1,128)S(1)} all-gather(f32[3,1,2048]{2,1,0:T(1,128)S(1)} %copy-done.41), channel_id=2, replica_groups=mesh['batch'=4,'seq'=8] {'seq'}, dimensions={0}, use_global_device_ids=true | all-gather | bytes 221184 | tf_op jit(solution)/shard_map/all_gather | solution.py:305
  184.4 6.8 %fusion.84 = f32[512,3072]{1,0:T(8,128)} fusion(bf16[512,768]{1,0:T(8,128)(2,1)S(1)} %copy-done.5, bf16[3072,768]{0,1:T(8,128)(2,1)} %all-gather.12.cloned.1.call-done), kind=kOutput, calls=%fused_computation.203 | convolution fusion | flops 2415919104 | bytes 11796480 | tf_op jit(solution)/shard_map/nd,fd->nf/dot_general | solution.py:334
  195.9 19.1 %all-gather.10.cloned.1.call-done = bf16[768,3072]{1,0:T(8,128)(2,1)} async-done(((bf16[768,384]{1,0:T(8,128)(2,1)}), bf16[768,3072]{1,0:T(8,128)(2,1)}) %all-gather.10.cloned.1.call-update) | async-done | bytes 4718608 | tf_op jit(solution)/shard_map/all_gather | solution.py:298
  215.1 12.2 %fusion.6 = (bf16[512,3072]{1,0:T(8,128)(2,1)}, f32[512,3072]{1,0:T(8,128)}) fusion(f32[512,3072]{1,0:T(8,128)} %fusion.84, bf16[768,3072]{1,0:T(8,128)(2,1)} %all-gather.10.cloned.1.call-done, f32[512,768]{1,0:T(8,128)S(1)} %get-tuple-element.143, f32[768]{0:T(1024)S(1)} %copy-done.53, f32[768]{0:T(1024)S(1)} %copy-done.46, f32[512]{0:T(512)S(1)} %add_rsqrt_fusion, ...), kind=kOutput, calls=%fused_computation.11 | convolution fusion | flops 2449342464 | bytes 22030336 | tf_op jit(solution)/shard_map/dot_general | solution.py:313
  227.3 5.0 copy.181
  232.3 7.5 %multiply_reduce_fusion = (f32[768]{0:T(1024)}, f32[512]{0:T(512)S(1)}, f32[512]{0:T(512)S(1)}, f32[768]{0:T(1024)}, f32[512,768]{1,0:T(8,128)S(1)}) fusion(f32[512,768]{1,0:T(8,128)} %copy-done.11, f32[512]{0:T(512)S(1)} %add_rsqrt_fusion, f32[512]{0:T(512)S(1)} %broadcast_multiply_fusion.5, f32[768]{0:T(1024)S(1)} %copy-done.46, ...), kind=kOutput, calls=%fused_computation.92 | convolution fusion | flops 2419455488 | bytes 11027456 | tf_op jit(solution)/shard_map/nf,df->nd/dot_general | solution.py:340
  239.8 13.7 %fusion.36 = (bf16[512,768]{1,0:T(8,128)(2,1)}, f32[512,768]{1,0:T(8,128)S(1)}) fusion(f32[]{:T(128)} %bitcast.34, f32[]{:T(128)} %bitcast.32, f32[]{:T(128)} %bitcast.30, f32[]{:T(128)} %bitcast.28, f32[]{:T(128)} %bitcast.26, f32[]{:T(128)} %bitcast.24, f32[]{:T(128)} %bitcast.22, f32[]{:T(128)} %bitcast.20, f32[]{:T(128)} %bitcast, ...), kind=kOutput, calls=%fused_computation.79 | convolution fusion | flops 2440691712 | bytes 21233700 | tf_op jit(solution)/shard_map/dot_general | solution.py:316
  253.5 4.6 fusion.44
  263.2 4.4 all-to-all-start.2
  267.6 5.0 fusion.7
  289.0 6.1 %copy.169 = f32[2,2,1,768,384]{4,3,0,1,2:T(8,128)} copy(f32[2,2,1,768,384]{3,4,2,1,0:T(8,128)} %constant_dynamic-slice_fusion.3) | data formatting | bytes 9437184 | tf_op jit(solution)/shard_map/jit(dynamic_index_in_dim)/dynamic_slice | solution.py:381
  306.7 20.9 %attn_bwd.1 = bf16[3,3,64,2048]{3,2,1,0:T(8,128)(2,1)} custom-call(s32[3]{0:T(128)} %and_select_fusion.2.seg_ref, bf16[3,3,64,2048]{3,2,1,0:T(8,128)(2,1)} %bitcast.309, bf16[3,3,64,2048]{3,2,1,0:T(8,128)(2,1)} %bitcast.310, bf16[3,3,64,2048]{3,2,1,0:T(8,128)(2,1)} %bitcast.311, bf16[3,64,2048]{2,1,0:T(8,128)(2,1)} %bitcast.318, ...), custom_call_target="tpu_custom_call" | custom-call | flops 5033164800 | bytes 6316032 | tf_op jit(solution)/shard_map/attn_bwd/pallas_call | solution.py:174
  338.6 3.7 bitcast_add_fusion
  350.0 14.5 %all-to-all-done.3 = bf16[8,3,3,64,256]{4,3,2,1,0:T(8,128)(2,1)S(1)} async-done(((bf16[8,3,3,64,256]{4,3,2,1,0:T(8,128)(2,1)}), bf16[8,3,3,64,256]{4,3,2,1,0:T(8,128)(2,1)S(1)}, u32[]{:S(2)}, u32[]{:S(2)}) %all-to-all-start.3) | async-done | bytes 2359328 | tf_op jit(solution)/shard_map/all_to_all | solution.py:360
  377.0 12.0 %collective-permute-done.14 = bf16[2,3072,96]{1,2,0:T(8,128)(2,1)} collective-permute-done((bf16[2,3072,96]{1,2,0:T(8,128)(2,1)}, bf16[2,3072,96]{1,2,0:T(8,128)(2,1)}, u32[]{:S(2)}, u32[]{:S(2)}) %collective-permute-start.14) | collective-permute-done | bytes 1179680 | tf_op jit(solution)/shard_map/ppermute | solution.py:384
  396.3 17.3 %collective-permute-done.11 = bf16[2,768,384]{2,1,0:T(8,128)(2,1)} collective-permute-done((bf16[2,768,384]{2,1,0:T(8,128)(2,1)S(1)}, bf16[2,768,384]{2,1,0:T(8,128)(2,1)}, u32[]{:S(2)}, u32[]{:S(2)}) %collective-permute-start.11) | collective-permute-done | bytes 1179680 | tf_op jit(solution)/shard_map/ppermute | solution.py:384
  427.2 4.1 fusion.26
  431.3 6.3 %concatenate.59 = f32[3081]{0:T(1024)S(1)} concatenate(f32[768]{0:T(1024)} %get-tuple-element.96, f32[768]{0:T(1024)} %get-tuple-element.101, f32[768]{0:T(1024)} %get-tuple-element.94, f32[768]{0:T(1024)} %get-tuple-element.100, f32[1]{0:T(128)} %bitcast.98, f32[1]{0:T(128)} %bitcast.100, f32[1]{0:T(128)} %bitcast.102, f32[1]{0:T(128)} %bitcast.104, f32[1]{0:T(128)} %bitcast.106, ...), dimensions={0} | concatenate | bytes 24648 | tf_op jit(solution)/shard_map/concatenate | solution.py:397
  455.4 5.5 %collective-permute-done.6 = bf16[768,288]{0,1:T(8,128)(2,1)S(1)} collective-permute-done((bf16[768,288]{0,1:T(8,128)(2,1)S(1)}, bf16[768,288]{0,1:T(8,128)(2,1)S(1)}, u32[]{:S(2)}, u32[]{:S(2)}) %collective-permute-start.6) | collective-permute-done | bytes 442400 | tf_op jit(solution)/shard_map/ppermute | solution.py:384
  463.2 12.2 %collective-permute-start.19 = (f32[3081]{0:T(1024)S(1)}, f32[3081]{0:T(1024)S(1)}, u32[]{:S(2)}, u32[]{:S(2)}) collective-permute-start(f32[3081]{0:T(1024)S(1)} %add.340), channel_id=1, source_target_pairs={{0,8},{8,0},{16,24},{24,16},{1,9},{9,1},{17,25},{25,17},{2,10},{10... | collective-permute-start | bytes 36980 | tf_op jit(solution)/shard_map/ppermute | solution.py:403
  487.4 11.4 %reduce-scatter.13.cloned.1.call-done = bf16[192,288]{1,0:T(8,128)(2,1)} async-done(((bf16[768,288]{1,0:T(8,128)(2,1)}), bf16[192,288]{1,0:T(8,128)(2,1)}) %reduce-scatter.13.cloned.1.call-update) | async-done | bytes 110608
  (333 shorter events, 178.4 us)
Async XLA Ops:
  7.2 70.1 %all-gather.6.cloned.1.call-start = ((), (), s32[]{:S(2)}) async-start(), calls=%async_computation.8 | async-start | bytes 3981312 | tf_op jit(solution)/shard_map/all_gather | solution.py:277
  7.2 19.2 %collective-permute-start = (bf16[192,288]{1,0:T(8,128)(2,1)}, bf16[192,288]{1,0:T(8,128)(2,1)S(1)}, u32[]{:S(2)}, u32[]{:S(2)}) collective-permute-start(bf16[192,288]{1,0:T(8,128)(2,1)} %param.17), channel_id=1, source_target_pairs={{0,16},{8,24},{16,0},{24,8},{1,17},{9,25},{17,1},{25,9},{2,18},{10... | collective-permute-start | bytes 331784 | tf_op jit(solution)/shard_map/ppermute | solution.py:269
  14.7 18.2 %collective-permute-start.2 = (bf16[165888]{0:T(1024)(128)(2,1)S(1)}, bf16[165888]{0:T(1024)(128)(2,1)S(1)}, u32[]{:S(2)}, u32[]{:S(2)}) collective-permute-start(bf16[165888]{0:T(1024)(128)(2,1)S(1)} %constant_dynamic-update-slice_fusion), channel_id=1, source_target_pairs={{0,16},{8,24},{16,0},{24,8},{1,17},{9,25},{17,1},{25,9},{2,18},{10... | collective-permute-start | bytes 995336 | tf_op jit(solution)/shard_map/ppermute | solution.py:269
  26.5 13.7 %collective-permute-start.1 = (bf16[2,192,288]{2,1,0:T(8,128)(2,1)S(1)}, bf16[2,192,288]{2,1,0:T(8,128)(2,1)S(1)}, u32[]{:S(2)}, u32[]{:S(2)}) collective-permute-start(bf16[2,192,288]{2,1,0:T(8,128)(2,1)S(1)} %maximum_select_fusion.2), channel_id=1, source_target_pairs={{0,8},{8,0},{16,24},{24,16},{1,9},{9,1},{17,25},{25,17},{2,10},{10... | collective-permute-start | bytes 663560 | tf_op jit(solution)/shard_map/ppermute | solution.py:269
  36.2 17.1 %collective-permute-start.3 = (bf16[2,165888]{1,0:T(2,128)(2,1)S(1)}, bf16[2,165888]{1,0:T(2,128)(2,1)S(1)}, u32[]{:S(2)}, u32[]{:S(2)}) collective-permute-start(bf16[2,165888]{1,0:T(2,128)(2,1)S(1)} %broadcast_select_fusion.1), channel_id=1, source_target_pairs={{0,8},{8,0},{16,24},{24,16},{1,9},{9,1},{17,25},{25,17},{2,10},{10... | collective-permute-start | bytes 1990664 | tf_op jit(solution)/shard_map/ppermute | solution.py:269
  42.2 142.2 %all-gather.12.cloned.1.call-start = ((), (), s32[]{:S(2)}) async-start(), calls=%async_computation.11 | async-start | bytes 5308416 | tf_op jit(solution)/shard_map/all_gather | solution.py:298
  62.1 131.1 %all-gather.8.cloned.1.call-start = ((), (), s32[]{:S(2)}) async-start(), calls=%async_computation.9 | async-start | bytes 1327104 | tf_op jit(solution)/shard_map/all_gather | solution.py:298
  63.2 151.8 %all-gather.10.cloned.1.call-start = ((), (), s32[]{:S(2)}) async-start(), calls=%async_computation.10 | async-start | bytes 5308416 | tf_op jit(solution)/shard_map/all_gather | solution.py:298
  97.9 44.6 %all-to-all-start = ((bf16[8,3,3,64,256]{4,3,2,1,0:T(8,128)(2,1)}), bf16[8,3,3,64,256]{4,3,2,1,0:T(8,128)(2,1)S(1)}, u32[]{:S(2)}, u32[]{:S(2)}) async-start(bf16[8,3,3,64,256]{4,3,2,1,0:T(8,128)(2,1)} %copy.148), calls=%async_computation | async-start | bytes 4718592 | tf_op jit(solution)/shard_map/all_to_all | solution.py:291
  163.5 27.7 %all-to-all-start.1 = ((bf16[8,3,64,256]{3,2,1,0:T(8,128)(2,1)}), bf16[8,3,64,256]{3,2,1,0:T(8,128)(2,1)S(1)}, u32[]{:S(2)}, u32[]{:S(2)}) async-start(bf16[8,3,64,256]{3,2,1,0:T(8,128)(2,1)} %bitcast.265), calls=%async_computation.1 | async-start | bytes 1572864 | tf_op jit(solution)/shard_map/all_to_all | solution.py:304
  263.2 41.3 %all-to-all-start.2 = ((bf16[8,3,64,256]{3,2,1,0:T(8,128)(2,1)}), bf16[8,3,64,256]{3,2,1,0:T(8,128)(2,1)}, u32[]{:S(2)}, u32[]{:S(2)}) async-start(bf16[8,3,64,256]{3,2,1,0:T(8,128)(2,1)} %bitcast.37), calls=%async_computation.2 | async-start | bytes 1572864 | tf_op jit(solution)/shard_map/all_to_all | solution.py:354
  274.4 64.2 %collective-permute-start.13 = (bf16[2,2,3072,96]{2,3,0,1:T(8,128)(2,1)}, bf16[2,2,3072,96]{2,3,0,1:T(8,128)(2,1)}, u32[]{:S(2)}, u32[]{:S(2)}) collective-permute-start(bf16[2,2,3072,96]{2,3,0,1:T(8,128)(2,1)} %fusion.9), channel_id=1, source_target_pairs={{0,1},{1,0},{2,3},{3,2},{4,5},{5,4},{6,7},{7,6},{8,9},{9,8},{10,11... | collective-permute-start | bytes 7077896 | tf_op jit(solution)/shard_map/ppermute | solution.py:384
  278.9 21.7 %collective-permute-start.7 = (bf16[2,2,768,96]{2,3,1,0:T(8,128)(2,1)S(1)}, bf16[2,2,768,96]{2,3,1,0:T(8,128)(2,1)}, u32[]{:S(2)}, u32[]{:S(2)}) collective-permute-start(bf16[2,2,768,96]{2,3,1,0:T(8,128)(2,1)S(1)} %fusion.63), channel_id=1, source_target_pairs={{0,1},{1,0},{2,3},{3,2},{4,5},{5,4},{6,7},{7,6},{8,9},{9,8},{10,11... | collective-permute-start | bytes 1769480 | tf_op jit(solution)/shard_map/ppermute | solution.py:384
  300.1 45.0 %collective-permute-start.10 = (bf16[2,2,768,384]{3,2,0,1:T(8,128)(2,1)}, bf16[2,2,768,384]{3,2,0,1:T(8,128)(2,1)}, u32[]{:S(2)}, u32[]{:S(2)}) collective-permute-start(bf16[2,2,768,384]{3,2,0,1:T(8,128)(2,1)} %bitcast.312), channel_id=1, source_target_pairs={{0,1},{1,0},{2,3},{3,2},{4,5},{5,4},{6,7},{7,6},{8,9},{9,8},{10,11... | collective-permute-start | bytes 7077896 | tf_op jit(solution)/shard_map/ppermute | solution.py:384
  302.9 31.9 %collective-permute-start.8 = (bf16[2,768,96]{1,2,0:T(8,128)(2,1)}, bf16[2,768,96]{1,2,0:T(8,128)(2,1)}, u32[]{:S(2)}, u32[]{:S(2)}) collective-permute-start(bf16[2,768,96]{1,2,0:T(8,128)(2,1)} %fusion.66), channel_id=1, source_target_pairs={{0,2},{1,3},{2,0},{3,1},{4,6},{5,7},{6,4},{7,5},{8,10},{9,11},{10,... | collective-permute-start | bytes 884744 | tf_op jit(solution)/shard_map/ppermute | solution.py:384
  330.9 33.6 %all-to-all-start.3 = ((bf16[8,3,3,64,256]{4,3,2,1,0:T(8,128)(2,1)}), bf16[8,3,3,64,256]{4,3,2,1,0:T(8,128)(2,1)S(1)}, u32[]{:S(2)}, u32[]{:S(2)}) async-start(bf16[8,3,3,64,256]{4,3,2,1,0:T(8,128)(2,1)} %bitcast.274), calls=%async_computation.3 | async-start | bytes 4718592 | tf_op jit(solution)/shard_map/all_to_all | solution.py:360
  334.5 116.9 %reduce-scatter.15.cloned.1.call-start = ((), (), s32[]{:S(2)}) async-start(), calls=%async_computation.15 | async-start | bytes 245760
  336.7 56.2 %collective-permute-start.9 = (bf16[768,96]{0,1:T(8,128)(2,1)}, bf16[768,96]{0,1:T(8,128)(2,1)}, u32[]{:S(2)}, u32[]{:S(2)}) collective-permute-start(bf16[768,96]{0,1:T(8,128)(2,1)} %fusion.68), channel_id=1, source_target_pairs={{0,4},{1,5},{2,6},{3,7},{4,0},{5,1},{6,2},{7,3},{8,12},{9,13},{10,... | collective-permute-start | bytes 442376 | tf_op jit(solution)/shard_map/ppermute | solution.py:384
  343.6 45.3 %collective-permute-start.14 = (bf16[2,3072,96]{1,2,0:T(8,128)(2,1)}, bf16[2,3072,96]{1,2,0:T(8,128)(2,1)}, u32[]{:S(2)}, u32[]{:S(2)}) collective-permute-start(bf16[2,3072,96]{1,2,0:T(8,128)(2,1)} %fusion.48), channel_id=1, source_target_pairs={{0,2},{1,3},{2,0},{3,1},{4,6},{5,7},{6,4},{7,5},{8,10},{9,11},{10,... | collective-permute-start | bytes 3538952 | tf_op jit(solution)/shard_map/ppermute | solution.py:384
  349.4 64.2 %collective-permute-start.11 = (bf16[2,768,384]{2,1,0:T(8,128)(2,1)S(1)}, bf16[2,768,384]{2,1,0:T(8,128)(2,1)}, u32[]{:S(2)}, u32[]{:S(2)}) collective-permute-start(bf16[2,768,384]{2,1,0:T(8,128)(2,1)S(1)} %fusion.47), channel_id=1, source_target_pairs={{0,2},{1,3},{2,0},{3,1},{4,6},{5,7},{6,4},{7,5},{8,10},{9,11},{10,... | collective-permute-start | bytes 3538952 | tf_op jit(solution)/shard_map/ppermute | solution.py:384
  377.0 45.1 %collective-permute-start.4 = (bf16[2,2,768,288]{2,3,1,0:T(8,128)(2,1)}, bf16[2,2,768,288]{2,3,1,0:T(8,128)(2,1)}, u32[]{:S(2)}, u32[]{:S(2)}) collective-permute-start(bf16[2,2,768,288]{2,3,1,0:T(8,128)(2,1)} %fusion.18), channel_id=1, source_target_pairs={{0,1},{1,0},{2,3},{3,2},{4,5},{5,4},{6,7},{7,6},{8,9},{9,8},{10,11... | collective-permute-start | bytes 5308424 | tf_op jit(solution)/shard_map/ppermute | solution.py:384
  391.4 28.3 %collective-permute-start.15 = (bf16[3072,96]{0,1:T(8,128)(2,1)}, bf16[3072,96]{0,1:T(8,128)(2,1)}, u32[]{:S(2)}, u32[]{:S(2)}) collective-permute-start(bf16[3072,96]{0,1:T(8,128)(2,1)} %fusion.62), channel_id=1, source_target_pairs={{0,4},{1,5},{2,6},{3,7},{4,0},{5,1},{6,2},{7,3},{8,12},{9,13},{10,... | collective-permute-start | bytes 1769480 | tf_op jit(solution)/shard_map/ppermute | solution.py:384
  396.3 87.8 %reduce-scatter.11.cloned.1.call-start = ((), (), s32[]{:S(2)}) async-start(), calls=%async_computation.13 | async-start | bytes 737280 | tf_op jit(solution)/shard_map/reduce_scatter | solution.py:389
  418.3 19.4 %collective-permute-start.12 = (bf16[768,384]{1,0:T(8,128)(2,1)}, bf16[768,384]{1,0:T(8,128)(2,1)}, u32[]{:S(2)}, u32[]{:S(2)}) collective-permute-start(bf16[768,384]{1,0:T(8,128)(2,1)} %fusion.61), channel_id=1, source_target_pairs={{0,4},{1,5},{2,6},{3,7},{4,0},{5,1},{6,2},{7,3},{8,12},{9,13},{10,... | collective-permute-start | bytes 1769480 | tf_op jit(solution)/shard_map/ppermute | solution.py:384
  421.8 64.0 %reduce-scatter.9.cloned.1.call-start = ((), (), s32[]{:S(2)}) async-start(), calls=%async_computation.12 | async-start | bytes 737280 | tf_op jit(solution)/shard_map/reduce_scatter | solution.py:389
  426.3 21.1 %collective-permute-start.5 = (bf16[2,768,288]{1,2,0:T(8,128)(2,1)}, bf16[2,768,288]{1,2,0:T(8,128)(2,1)}, u32[]{:S(2)}, u32[]{:S(2)}) collective-permute-start(bf16[2,768,288]{1,2,0:T(8,128)(2,1)} %fusion.51), channel_id=1, source_target_pairs={{0,2},{1,3},{2,0},{3,1},{4,6},{5,7},{6,4},{7,5},{8,10},{9,11},{10,... | collective-permute-start | bytes 2654216 | tf_op jit(solution)/shard_map/ppermute | solution.py:384
  437.6 6.0 %collective-permute-start.16 = (f32[3081]{0:T(1024)S(1)}, f32[3081]{0:T(1024)}, u32[]{:S(2)}, u32[]{:S(2)}) collective-permute-start(f32[3081]{0:T(1024)S(1)} %concatenate.59), channel_id=1, source_target_pairs={{0,1},{1,0},{2,3},{3,2},{4,5},{5,4},{6,7},{7,6},{8,9},{9,8},{10,11... | collective-permute-start | bytes 36980 | tf_op jit(solution)/shard_map/ppermute | solution.py:403
  440.1 58.7 %reduce-scatter.13.cloned.1.call-start = ((), (), s32[]{:S(2)}) async-start(), calls=%async_computation.14 | async-start | bytes 737280
  444.4 8.7 %collective-permute-start.17 = (f32[3081]{0:T(1024)S(1)}, f32[3081]{0:T(1024)}, u32[]{:S(2)}, u32[]{:S(2)}) collective-permute-start(f32[3081]{0:T(1024)S(1)} %add.338), channel_id=1, source_target_pairs={{0,2},{1,3},{2,0},{3,1},{4,6},{5,7},{6,4},{7,5},{8,10},{9,11},{10,... | collective-permute-start | bytes 36980 | tf_op jit(solution)/shard_map/ppermute | solution.py:403
  450.1 10.8 %collective-permute-start.6 = (bf16[768,288]{0,1:T(8,128)(2,1)S(1)}, bf16[768,288]{0,1:T(8,128)(2,1)S(1)}, u32[]{:S(2)}, u32[]{:S(2)}) collective-permute-start(bf16[768,288]{0,1:T(8,128)(2,1)S(1)} %fusion.65), channel_id=1, source_target_pairs={{0,4},{1,5},{2,6},{3,7},{4,0},{5,1},{6,2},{7,3},{8,12},{9,13},{10,... | collective-permute-start | bytes 1327112 | tf_op jit(solution)/shard_map/ppermute | solution.py:384
  453.8 9.4 %collective-permute-start.18 = (f32[3081]{0:T(1024)S(1)}, f32[3081]{0:T(1024)S(1)}, u32[]{:S(2)}, u32[]{:S(2)}) collective-permute-start(f32[3081]{0:T(1024)S(1)} %add.339), channel_id=1, source_target_pairs={{0,4},{1,5},{2,6},{3,7},{4,0},{5,1},{6,2},{7,3},{8,12},{9,13},{10,... | collective-permute-start | bytes 36980 | tf_op jit(solution)/shard_map/ppermute | solution.py:403
  463.2 14.0 %collective-permute-start.19 = (f32[3081]{0:T(1024)S(1)}, f32[3081]{0:T(1024)S(1)}, u32[]{:S(2)}, u32[]{:S(2)}) collective-permute-start(f32[3081]{0:T(1024)S(1)} %add.340), channel_id=1, source_target_pairs={{0,8},{8,0},{16,24},{24,16},{1,9},{9,1},{17,25},{25,17},{2,10},{10... | collective-permute-start | bytes 36980 | tf_op jit(solution)/shard_map/ppermute | solution.py:403
  (65 other events, 1280.0 us)
Sparse Core Ops, SparseCore 0:
  42.4 34.9 all-gather.5
  79.2 56.3 all-gather.11
  138.0 30.5 all-gather.7
  170.3 44.6 all-gather.9
  396.4 28.4 reduce-scatter.14
  427.0 25.8 reduce-scatter.10
  455.2 20.5 reduce-scatter.8
  478.1 20.7 reduce-scatter.12

commit v3 on v1

--- a/solution.py
+++ b/solution.py
@@ -389,9 +389,17 @@
         return acc.astype(jnp.bfloat16)
 
     def by_rows(col_sum):
-        return lax.psum_scatter(col_sum, "batch", scatter_dimension=0, tiled=True).astype(
-            jnp.float32
-        )
+        rows, cols = col_sum.shape
+        bits = n_batch.bit_length() - 1
+        acc = col_sum.astype(jnp.float32).reshape((2,) * bits + (rows // n_batch, cols))
+        for bit in range(bits):
+            mine = (batch_index >> bit) & 1
+            keep = lax.dynamic_index_in_dim(acc, mine, axis=bits - 1 - bit, keepdims=False)
+            send = lax.dynamic_index_in_dim(acc, 1 - mine, axis=bits - 1 - bit, keepdims=False)
+            partner = [(i, i ^ (1 << bit)) for i in range(n_batch)]
+            got = lax.ppermute(send.astype(jnp.bfloat16), "batch", partner)
+            acc = keep + got.astype(jnp.float32)
+        return acc
 
     qkv_grad = by_rows(by_cols(qkv_local))
     proj_grad = by_rows(by_cols(proj_local))

time: 508 us -> 525 us (1.033)
  waiting for transfers between devices: 134 us -> 146 us
  other arithmetic: 68.5 us -> 58.7 us
  starting transfers between devices: 54.7 us -> 63.5 us
    ppermute x5, waiting for transfers between devices: 1.72 us -> 29.8 us  [local(): small_sums = small_sums + lax.ppermute(small_sums, axis, partner)]
    ppermute x12, waiting for transfers between devices: 36.5 us -> 17 us  [by_cols(): got = lax.ppermute(send.astype(jnp.bfloat16), 'seq', partner)]
    ppermute x0 -> x8, waiting for transfers between devices: none -> 15.6 us  [by_rows(): got = lax.ppermute(send.astype(jnp.bfloat16), 'batch', partner)]
    unnamed x142 -> x100, local copies, waits for them, and re-layouts: 29.1 us -> 15.4 us
    ppermute x0 -> x8, starting transfers between devices: none -> 12.2 us  [by_rows(): got = lax.ppermute(send.astype(jnp.bfloat16), 'batch', partner)]
    unnamed x10 -> x4, waiting for transfers between devices: 11.6 us -> 0.07 us
    convert_element_type x4 -> x1, other arithmetic: 7.25 us -> 1.18 us  [by_cols(): return acc.astype(jnp.bfloat16)]
    add x0 -> x8, other arithmetic: none -> 5.83 us  [by_rows(): acc = keep + got.astype(jnp.float32)]
  transfers between devices with their start and end apart: 33 -> 37, of which waited for: 13 -> 19; matrix products, arithmetic and copies ran while one was open for 34% -> 32% of each run, Pallas kernels for 8% -> 7%
where the time goes in v3:
time: 525 us; the launch traced here: 516 us
  waiting for transfers between devices  146 us (28%)
  local copies, waits for them, and re-layouts  108 us (21%)
  matrix products  69 us (13%)
  starting transfers between devices  63.5 us (12%)
  other arithmetic  58.7 us (11%)
  Pallas kernels  38 us (7%)
  blocking collectives  17.6 us (3%)
  between operations  15.2 us (3%)
    ppermute x4, waiting for transfers between devices, gather_rows(): got = lax.ppermute(acc, 'batch', partner)  36.7 us
    ppermute x5, waiting for transfers between devices, local(): small_sums = small_sums + lax.ppermute(small_sums, axis, partner)  29.8 us
    all_to_all x1, waiting for transfers between devices, local(): lax.all_to_all(send, 'seq', split_axis=0, concat_axis=0, tiled=True)  28.3 us
    pallas_call x1, Pallas kernels, attn_backward(): pl.pallas_call(functools.partial(bwd_kernel, bk=bk, bq=bq, scale=scale),...  20.8 us
    all_gather x1, blocking collectives, local(): lax.all_gather(lse_rows.reshape(per_dev, SLOT), 'seq', axis=0, tiled=True)  17.6 us
    pallas_call x1, Pallas kernels, attn_forward(): pl.pallas_call(functools.partial(fwd_kernel, bq=bq, bk=bk, scale=scale),...  17.1 us
    ppermute x12, waiting for transfers between devices, by_cols(): got = lax.ppermute(send.astype(jnp.bfloat16), 'seq', partner)  17 us
    dot_general x1, matrix products, local(): jnp.dot(gelu_low, w_down, preferred_element_type=jnp.float32)  16.1 us
  transfers between devices with their start and end apart: 37, of which 19 were waited for; matrix products, arithmetic and copies ran while one was open for 32% of the time, Pallas kernels for 7%

profile of v3, /device:TPU:0, one launch (start us, length us, event | category | flops | bytes accessed | tf_op | source)
XLA Modules:
  0.0 516.3 jit_solution(5692813445170809939)
XLA Ops:
  7.2 4.1 collective-permute-start
  14.7 3.9 collective-permute-done
  20.7 7.2 %collective-permute-done.1 = bf16[2,192,288]{2,1,0:T(8,128)(2,1)S(1)} collective-permute-done((bf16[2,192,288]{2,1,0:T(8,128)(2,1)S(1)}, bf16[2,192,288]{2,1,0:T(8,128)(2,1)S(1)}, u32[]{:S(2)}, u32[]{:S(2)}) %collective-permute-start.1) | collective-permute-done | bytes 221216 | tf_op jit(solution)/shard_map/ppermute | solution.py:269
  33.9 13.6 %collective-permute-done.2 = bf16[165888]{0:T(1024)(128)(2,1)S(1)} collective-permute-done((bf16[165888]{0:T(1024)(128)(2,1)S(1)}, bf16[165888]{0:T(1024)(128)(2,1)S(1)}, u32[]{:S(2)}, u32[]{:S(2)}) %collective-permute-start.2) | collective-permute-done | bytes 331808 | tf_op jit(solution)/shard_map/ppermute | solution.py:269
  54.9 11.9 %collective-permute-done.3 = bf16[2,165888]{1,0:T(2,128)(2,1)S(1)} collective-permute-done((bf16[2,165888]{1,0:T(2,128)(2,1)S(1)}, bf16[2,165888]{1,0:T(2,128)(2,1)S(1)}, u32[]{:S(2)}, u32[]{:S(2)}) %collective-permute-start.3) | collective-permute-done | bytes 663584 | tf_op jit(solution)/shard_map/ppermute | solution.py:269
  68.8 4.1 copy.153
  81.1 4.2 fusion.81
  103.2 4.0 all-to-all-start
  114.6 28.3 %all-to-all-done = bf16[8,3,3,64,256]{4,3,2,1,0:T(8,128)(2,1)S(1)} async-done(((bf16[8,3,3,64,256]{4,3,2,1,0:T(8,128)(2,1)}), bf16[8,3,3,64,256]{4,3,2,1,0:T(8,128)(2,1)S(1)}, u32[]{:S(2)}, u32[]{:S(2)}) %all-to-all-start) | async-done | bytes 2359328 | tf_op jit(solution)/shard_map/all_to_all | solution.py:291
  144.6 17.1 %attn_fwd.1 = (bf16[3,64,2048]{2,1,0:T(8,128)(2,1)}, f32[3,1,2048]{2,1,0:T(1,128)}) custom-call(s32[3]{0:T(128)} %and_select_fusion.2.seg_ref, bf16[3,3,64,2048]{3,2,1,0:T(8,128)(2,1)} %bitcast.345, bf16[3,3,64,2048]{3,2,1,0:T(8,128)(2,1)} %bitcast.346, bf16[3,3,64,2048]{3,2,1,0:T(8,128)(2,1)} %bitcast.347), custom_call_target="tpu_custom_call" | custom-call | flops 2013265920 | bytes 3170304 | tf_op jit(solution)/shard_map/attn_fwd/pallas_call | solution.py:86
  167.7 4.5 multiply_convert_fusion
  172.2 17.6 %all-gather = f32[24,1,2048]{2,1,0:T(1,128)S(1)} all-gather(f32[3,1,2048]{2,1,0:T(1,128)S(1)} %copy-done.27), channel_id=2, replica_groups=mesh['batch'=4,'seq'=8] {'seq'}, dimensions={0}, use_global_device_ids=true | all-gather | bytes 221184 | tf_op jit(solution)/shard_map/all_gather | solution.py:308
  198.2 7.0 %fusion.92 = f32[512,3072]{1,0:T(8,128)} fusion(bf16[512,768]{1,0:T(8,128)(2,1)S(1)} %copy-done.3, bf16[3072,768]{0,1:T(8,128)(2,1)} %all-gather.12.cloned.1.call-done), kind=kOutput, calls=%fused_computation.233 | convolution fusion | flops 2415919104 | bytes 11796480 | tf_op jit(solution)/shard_map/nd,fd->nf/dot_general | solution.py:337
  208.1 12.5 %fusion.6 = (bf16[512,3072]{1,0:T(8,128)(2,1)}, f32[512,3072]{1,0:T(8,128)}) fusion(f32[512,3072]{1,0:T(8,128)} %fusion.92, bf16[768,3072]{1,0:T(8,128)(2,1)} %all-gather.10.cloned.1.call-done, f32[512,768]{1,0:T(8,128)} %copy-done.6, f32[768]{0:T(1024)S(1)} %copy-done.32, f32[768]{0:T(1024)S(1)} %copy-done.28, f32[512]{0:T(512)S(1)} %add_rsqrt_fusion, ...), kind=kOutput, calls=%fused_computation.11 | convolution fusion | flops 2449342464 | bytes 22030336 | tf_op jit(solution)/shard_map/dot_general | solution.py:316
  220.7 4.8 copy.187
  225.4 6.4 %multiply_reduce_fusion = (f32[768]{0:T(1024)S(1)}, f32[512]{0:T(512)S(1)}, f32[512]{0:T(512)S(1)}, f32[768]{0:T(1024)S(1)}, f32[512,768]{1,0:T(8,128)S(1)}) fusion(f32[512,768]{1,0:T(8,128)S(1)} %copy-done.7, f32[512]{0:T(512)S(1)} %add_rsqrt_fusion, f32[512]{0:T(512)S(1)} %broadcast_multiply_fusion.5, f32[768]{0:T(1024)S(1)} %copy-done.28, ...), kind=kOutput, calls=%fused_computation.92 | convolution fusion | flops 2419455488 | bytes 11027456 | tf_op jit(solution)/shard_map/nf,df->nd/dot_general | solution.py:343
  231.9 16.1 %fusion.36 = (bf16[512,768]{1,0:T(8,128)(2,1)}, f32[512,768]{1,0:T(8,128)S(1)}) fusion(f32[]{:T(128)} %bitcast.34, f32[]{:T(128)} %bitcast.32, f32[]{:T(128)} %bitcast.30, f32[]{:T(128)} %bitcast.28, f32[]{:T(128)} %bitcast.26, f32[]{:T(128)} %bitcast.24, f32[]{:T(128)} %bitcast.22, f32[]{:T(128)} %bitcast.20, f32[]{:T(128)} %bitcast, ...), kind=kOutput, calls=%fused_computation.79 | convolution fusion | flops 2440691712 | bytes 21233700 | tf_op jit(solution)/shard_map/dot_general | solution.py:319
  248.1 4.9 fusion.44
  263.1 4.2 all-to-all-start.2
  269.8 5.0 fusion.7
  290.0 6.1 %copy.175 = f32[2,2,1,768,384]{4,3,0,1,2:T(8,128)} copy(f32[2,2,1,768,384]{3,4,2,1,0:T(8,128)} %constant_dynamic-slice_fusion.4) | data formatting | bytes 9437184 | tf_op jit(solution)/shard_map/jit(dynamic_index_in_dim)/dynamic_slice | solution.py:384
  315.4 20.8 %attn_bwd.1 = bf16[3,3,64,2048]{3,2,1,0:T(8,128)(2,1)} custom-call(s32[3]{0:T(128)} %and_select_fusion.2.seg_ref, bf16[3,3,64,2048]{3,2,1,0:T(8,128)(2,1)} %bitcast.348, bf16[3,3,64,2048]{3,2,1,0:T(8,128)(2,1)} %bitcast.349, bf16[3,3,64,2048]{3,2,1,0:T(8,128)(2,1)} %bitcast.350, bf16[3,64,2048]{2,1,0:T(8,128)(2,1)} %bitcast.357, ...), custom_call_target="tpu_custom_call" | custom-call | flops 5033164800 | bytes 6316032 | tf_op jit(solution)/shard_map/attn_bwd/pallas_call | solution.py:174
  339.6 3.8 all-to-all-start.3
  345.0 3.7 bitcast_add_fusion
  357.4 16.0 %all-to-all-done.3 = bf16[8,3,3,64,256]{4,3,2,1,0:T(8,128)(2,1)S(1)} async-done(((bf16[8,3,3,64,256]{4,3,2,1,0:T(8,128)(2,1)}), bf16[8,3,3,64,256]{4,3,2,1,0:T(8,128)(2,1)S(1)}, u32[]{:S(2)}, u32[]{:S(2)}) %all-to-all-start.3) | async-done | bytes 2359328 | tf_op jit(solution)/shard_map/all_to_all | solution.py:363
  383.4 3.7 fusion.26
  387.2 5.8 %concatenate.59 = f32[3081]{0:T(1024)S(1)} concatenate(f32[768]{0:T(1024)S(1)} %get-tuple-element.98, f32[768]{0:T(1024)S(1)} %get-tuple-element.103, f32[768]{0:T(1024)S(1)} %get-tuple-element.96, f32[768]{0:T(1024)S(1)} %get-tuple-element.102, f32[1]{0:T(128)} %bitcast.116, f32[1]{0:T(128)} %bitcast.118, f32[1]{0:T(128)} %bitcast.120, f32[1]{0:T(128)} %bitcast.122, ...), dimensions={0} | concatenate | bytes 24648 | tf_op jit(solution)/shard_map/concatenate | solution.py:408
  393.0 4.0 fusion.59
  399.0 23.7 %collective-permute-done.25 = f32[3081]{0:T(1024)S(1)} collective-permute-done((f32[3081]{0:T(1024)S(1)}, f32[3081]{0:T(1024)S(1)}, u32[]{:S(2)}, u32[]{:S(2)}) %collective-permute-start.25) | collective-permute-done | bytes 12356 | tf_op jit(solution)/shard_map/ppermute | solution.py:414
  426.5 12.1 %collective-permute-start.27 = (f32[3081]{0:T(1024)S(1)}, f32[3081]{0:T(1024)S(1)}, u32[]{:S(2)}, u32[]{:S(2)}) collective-permute-start(f32[3081]{0:T(1024)S(1)} %add.400), channel_id=1, source_target_pairs={{0,8},{8,0},{16,24},{24,16},{1,9},{9,1},{17,25},{25,17},{2,10},{10... | collective-permute-start | bytes 36980 | tf_op jit(solution)/shard_map/ppermute | solution.py:414
  452.3 11.1 %collective-permute-done.21 = bf16[3072,96]{0,1:T(8,128)(2,1)S(1)} collective-permute-done((bf16[3072,96]{0,1:T(8,128)(2,1)S(1)}, bf16[3072,96]{0,1:T(8,128)(2,1)S(1)}, u32[]{:S(2)}, u32[]{:S(2)}) %collective-permute-start.21) | collective-permute-done | bytes 589856 | tf_op jit(solution)/shard_map/ppermute | solution.py:387
  503.4 5.3 %collective-permute-done.8 = bf16[192,288]{1,0:T(8,128)(2,1)S(1)} collective-permute-done((bf16[192,288]{1,0:T(8,128)(2,1)S(1)}, bf16[192,288]{1,0:T(8,128)(2,1)S(1)}, u32[]{:S(2)}, u32[]{:S(2)}) %collective-permute-start.8) | collective-permute-done | bytes 110624 | tf_op jit(solution)/shard_map/ppermute | solution.py:400
  (320 shorter events, 203.1 us)
Async XLA Ops:
  7.2 73.9 %all-gather.6.cloned.1.call-start = ((), (), s32[]{:S(2)}) async-start(), calls=%async_computation.4 | async-start | bytes 3981312 | tf_op jit(solution)/shard_map/all_gather | solution.py:277
  7.2 11.4 %collective-permute-start = (bf16[192,288]{1,0:T(8,128)(2,1)}, bf16[192,288]{1,0:T(8,128)(2,1)S(1)}, u32[]{:S(2)}, u32[]{:S(2)}) collective-permute-start(bf16[192,288]{1,0:T(8,128)(2,1)} %param.17), channel_id=1, source_target_pairs={{0,16},{8,24},{16,0},{24,8},{1,17},{9,25},{17,1},{25,9},{2,18},{10... | collective-permute-start | bytes 331784 | tf_op jit(solution)/shard_map/ppermute | solution.py:269
  19.7 8.2 %collective-permute-start.1 = (bf16[2,192,288]{2,1,0:T(8,128)(2,1)S(1)}, bf16[2,192,288]{2,1,0:T(8,128)(2,1)S(1)}, u32[]{:S(2)}, u32[]{:S(2)}) collective-permute-start(bf16[2,192,288]{2,1,0:T(8,128)(2,1)S(1)} %maximum_select_fusion.2), channel_id=1, source_target_pairs={{0,8},{8,0},{16,24},{24,16},{1,9},{9,1},{17,25},{25,17},{2,10},{10... | collective-permute-start | bytes 663560 | tf_op jit(solution)/shard_map/ppermute | solution.py:269
  29.9 17.6 %collective-permute-start.2 = (bf16[165888]{0:T(1024)(128)(2,1)S(1)}, bf16[165888]{0:T(1024)(128)(2,1)S(1)}, u32[]{:S(2)}, u32[]{:S(2)}) collective-permute-start(bf16[165888]{0:T(1024)(128)(2,1)S(1)} %pad_maximum_fusion.5), channel_id=1, source_target_pairs={{0,16},{8,24},{16,0},{24,8},{1,17},{9,25},{17,1},{25,9},{2,18},{10... | collective-permute-start | bytes 995336 | tf_op jit(solution)/shard_map/ppermute | solution.py:269
  33.0 161.3 %all-gather.8.cloned.1.call-start = ((), (), s32[]{:S(2)}) async-start(), calls=%async_computation.5 | async-start | bytes 1327104 | tf_op jit(solution)/shard_map/all_gather | solution.py:301
  50.8 16.0 %collective-permute-start.3 = (bf16[2,165888]{1,0:T(2,128)(2,1)S(1)}, bf16[2,165888]{1,0:T(2,128)(2,1)S(1)}, u32[]{:S(2)}, u32[]{:S(2)}) collective-permute-start(bf16[2,165888]{1,0:T(2,128)(2,1)S(1)} %broadcast_select_fusion.1), channel_id=1, source_target_pairs={{0,8},{8,0},{16,24},{24,16},{1,9},{9,1},{17,25},{25,17},{2,10},{10... | collective-permute-start | bytes 1990664 | tf_op jit(solution)/shard_map/ppermute | solution.py:269
  74.4 123.6 %all-gather.12.cloned.1.call-start = ((), (), s32[]{:S(2)}) async-start(), calls=%async_computation.7 | async-start | bytes 5308416 | tf_op jit(solution)/shard_map/all_gather | solution.py:301
  76.7 131.5 %all-gather.10.cloned.1.call-start = ((), (), s32[]{:S(2)}) async-start(), calls=%async_computation.6 | async-start | bytes 5308416 | tf_op jit(solution)/shard_map/all_gather | solution.py:301
  103.2 39.7 %all-to-all-start = ((bf16[8,3,3,64,256]{4,3,2,1,0:T(8,128)(2,1)}), bf16[8,3,3,64,256]{4,3,2,1,0:T(8,128)(2,1)S(1)}, u32[]{:S(2)}, u32[]{:S(2)}) async-start(bf16[8,3,3,64,256]{4,3,2,1,0:T(8,128)(2,1)} %copy.148), calls=%async_computation | async-start | bytes 4718592 | tf_op jit(solution)/shard_map/all_to_all | solution.py:291
  164.0 25.9 %all-to-all-start.1 = ((bf16[8,3,64,256]{3,2,1,0:T(8,128)(2,1)}), bf16[8,3,64,256]{3,2,1,0:T(8,128)(2,1)S(1)}, u32[]{:S(2)}, u32[]{:S(2)}) async-start(bf16[8,3,64,256]{3,2,1,0:T(8,128)(2,1)} %bitcast.335), calls=%async_computation.1 | async-start | bytes 1572864 | tf_op jit(solution)/shard_map/all_to_all | solution.py:307
  263.1 41.7 %all-to-all-start.2 = ((bf16[8,3,64,256]{3,2,1,0:T(8,128)(2,1)}), bf16[8,3,64,256]{3,2,1,0:T(8,128)(2,1)}, u32[]{:S(2)}, u32[]{:S(2)}) async-start(bf16[8,3,64,256]{3,2,1,0:T(8,128)(2,1)} %bitcast.37), calls=%async_computation.2 | async-start | bytes 1572864 | tf_op jit(solution)/shard_map/all_to_all | solution.py:357
  269.4 7.6 %collective-permute-start.9 = (bf16[2,2,768,96]{2,3,0,1:T(8,128)(2,1)S(1)}, bf16[2,2,768,96]{2,3,0,1:T(8,128)(2,1)S(1)}, u32[]{:S(2)}, u32[]{:S(2)}) collective-permute-start(bf16[2,2,768,96]{2,3,0,1:T(8,128)(2,1)S(1)} %fusion.64), channel_id=1, source_target_pairs={{0,1},{1,0},{2,3},{3,2},{4,5},{5,4},{6,7},{7,6},{8,9},{9,8},{10,11... | collective-permute-start | bytes 1769480 | tf_op jit(solution)/shard_map/ppermute | solution.py:387
  276.8 68.2 %collective-permute-start.19 = (bf16[2,2,3072,96]{2,3,0,1:T(8,128)(2,1)}, bf16[2,2,3072,96]{2,3,0,1:T(8,128)(2,1)}, u32[]{:S(2)}, u32[]{:S(2)}) collective-permute-start(bf16[2,2,3072,96]{2,3,0,1:T(8,128)(2,1)} %fusion.9), channel_id=1, source_target_pairs={{0,1},{1,0},{2,3},{3,2},{4,5},{5,4},{6,7},{7,6},{8,9},{9,8},{10,11... | collective-permute-start | bytes 7077896 | tf_op jit(solution)/shard_map/ppermute | solution.py:387
  277.9 18.2 %collective-permute-start.10 = (bf16[2,768,96]{1,2,0:T(8,128)(2,1)}, bf16[2,768,96]{1,2,0:T(8,128)(2,1)}, u32[]{:S(2)}, u32[]{:S(2)}) collective-permute-start(bf16[2,768,96]{1,2,0:T(8,128)(2,1)} %fusion.68), channel_id=1, source_target_pairs={{0,2},{1,3},{2,0},{3,1},{4,6},{5,7},{6,4},{7,5},{8,10},{9,11},{10,... | collective-permute-start | bytes 884744 | tf_op jit(solution)/shard_map/ppermute | solution.py:387
  298.0 9.0 %collective-permute-start.11 = (bf16[768,96]{0,1:T(8,128)(2,1)}, bf16[768,96]{0,1:T(8,128)(2,1)S(1)}, u32[]{:S(2)}, u32[]{:S(2)}) collective-permute-start(bf16[768,96]{0,1:T(8,128)(2,1)} %fusion.72), channel_id=1, source_target_pairs={{0,4},{1,5},{2,6},{3,7},{4,0},{5,1},{6,2},{7,3},{8,12},{9,13},{10,... | collective-permute-start | bytes 442376 | tf_op jit(solution)/shard_map/ppermute | solution.py:387
  304.7 47.5 %collective-permute-start.14 = (bf16[2,2,768,384]{3,2,0,1:T(8,128)(2,1)}, bf16[2,2,768,384]{3,2,0,1:T(8,128)(2,1)}, u32[]{:S(2)}, u32[]{:S(2)}) collective-permute-start(bf16[2,2,768,384]{3,2,0,1:T(8,128)(2,1)} %bitcast.351), channel_id=1, source_target_pairs={{0,1},{1,0},{2,3},{3,2},{4,5},{5,4},{6,7},{7,6},{8,9},{9,8},{10,11... | collective-permute-start | bytes 7077896 | tf_op jit(solution)/shard_map/ppermute | solution.py:387
  312.9 30.5 %collective-permute-start.13 = (bf16[192,96]{1,0:T(8,128)(2,1)S(1)}, bf16[192,96]{1,0:T(8,128)(2,1)}, u32[]{:S(2)}, u32[]{:S(2)}) collective-permute-start(bf16[192,96]{1,0:T(8,128)(2,1)S(1)} %fusion.76), channel_id=1, source_target_pairs={{0,16},{8,24},{16,0},{24,8},{1,17},{9,25},{17,1},{25,9},{2,18},{10... | collective-permute-start | bytes 110600 | tf_op jit(solution)/shard_map/ppermute | solution.py:400
  339.6 33.7 %all-to-all-start.3 = ((bf16[8,3,3,64,256]{4,3,2,1,0:T(8,128)(2,1)}), bf16[8,3,3,64,256]{4,3,2,1,0:T(8,128)(2,1)S(1)}, u32[]{:S(2)}, u32[]{:S(2)}) async-start(bf16[8,3,3,64,256]{4,3,2,1,0:T(8,128)(2,1)} %bitcast.312), calls=%async_computation.3 | async-start | bytes 4718592 | tf_op jit(solution)/shard_map/all_to_all | solution.py:363
  350.2 95.3 %collective-permute-start.20 = (bf16[2,3072,96]{1,2,0:T(8,128)(2,1)}, bf16[2,3072,96]{1,2,0:T(8,128)(2,1)}, u32[]{:S(2)}, u32[]{:S(2)}) collective-permute-start(bf16[2,3072,96]{1,2,0:T(8,128)(2,1)} %fusion.48), channel_id=1, source_target_pairs={{0,2},{1,3},{2,0},{3,1},{4,6},{5,7},{6,4},{7,5},{8,10},{9,11},{10,... | collective-permute-start | bytes 3538952 | tf_op jit(solution)/shard_map/ppermute | solution.py:387
  356.8 92.5 %collective-permute-start.15 = (bf16[2,768,384]{2,1,0:T(8,128)(2,1)}, bf16[2,768,384]{2,1,0:T(8,128)(2,1)}, u32[]{:S(2)}, u32[]{:S(2)}) collective-permute-start(bf16[2,768,384]{2,1,0:T(8,128)(2,1)} %fusion.47), channel_id=1, source_target_pairs={{0,2},{1,3},{2,0},{3,1},{4,6},{5,7},{6,4},{7,5},{8,10},{9,11},{10,... | collective-permute-start | bytes 3538952 | tf_op jit(solution)/shard_map/ppermute | solution.py:387
  397.0 25.7 %collective-permute-start.25 = (f32[3081]{0:T(1024)S(1)}, f32[3081]{0:T(1024)S(1)}, u32[]{:S(2)}, u32[]{:S(2)}) collective-permute-start(f32[3081]{0:T(1024)S(1)} %add.398), channel_id=1, source_target_pairs={{0,2},{1,3},{2,0},{3,1},{4,6},{5,7},{6,4},{7,5},{8,10},{9,11},{10,... | collective-permute-start | bytes 36980 | tf_op jit(solution)/shard_map/ppermute | solution.py:414
  398.6 67.1 %collective-permute-start.4 = (bf16[2,2,768,288]{2,3,0,1:T(8,128)(2,1)}, bf16[2,2,768,288]{2,3,0,1:T(8,128)(2,1)}, u32[]{:S(2)}, u32[]{:S(2)}) collective-permute-start(bf16[2,2,768,288]{2,3,0,1:T(8,128)(2,1)} %fusion.18), channel_id=1, source_target_pairs={{0,1},{1,0},{2,3},{3,2},{4,5},{5,4},{6,7},{7,6},{8,9},{9,8},{10,11... | collective-permute-start | bytes 5308424 | tf_op jit(solution)/shard_map/ppermute | solution.py:387
  426.5 13.9 %collective-permute-start.27 = (f32[3081]{0:T(1024)S(1)}, f32[3081]{0:T(1024)S(1)}, u32[]{:S(2)}, u32[]{:S(2)}) collective-permute-start(f32[3081]{0:T(1024)S(1)} %add.400), channel_id=1, source_target_pairs={{0,8},{8,0},{16,24},{24,16},{1,9},{9,1},{17,25},{25,17},{2,10},{10... | collective-permute-start | bytes 36980 | tf_op jit(solution)/shard_map/ppermute | solution.py:414
  447.2 16.3 %collective-permute-start.21 = (bf16[3072,96]{0,1:T(8,128)(2,1)S(1)}, bf16[3072,96]{0,1:T(8,128)(2,1)S(1)}, u32[]{:S(2)}, u32[]{:S(2)}) collective-permute-start(bf16[3072,96]{0,1:T(8,128)(2,1)S(1)} %fusion.62), channel_id=1, source_target_pairs={{0,4},{1,5},{2,6},{3,7},{4,0},{5,1},{6,2},{7,3},{8,12},{9,13},{10,... | collective-permute-start | bytes 1769480 | tf_op jit(solution)/shard_map/ppermute | solution.py:387
  451.8 20.7 %collective-permute-start.16 = (bf16[768,384]{1,0:T(8,128)(2,1)}, bf16[768,384]{1,0:T(8,128)(2,1)}, u32[]{:S(2)}, u32[]{:S(2)}) collective-permute-start(bf16[768,384]{1,0:T(8,128)(2,1)} %fusion.61), channel_id=1, source_target_pairs={{0,4},{1,5},{2,6},{3,7},{4,0},{5,1},{6,2},{7,3},{8,12},{9,13},{10,... | collective-permute-start | bytes 1769480 | tf_op jit(solution)/shard_map/ppermute | solution.py:387
  468.7 13.1 %collective-permute-start.5 = (bf16[2,768,288]{1,2,0:T(8,128)(2,1)S(1)}, bf16[2,768,288]{1,2,0:T(8,128)(2,1)S(1)}, u32[]{:S(2)}, u32[]{:S(2)}) collective-permute-start(bf16[2,768,288]{1,2,0:T(8,128)(2,1)S(1)} %fusion.51), channel_id=1, source_target_pairs={{0,2},{1,3},{2,0},{3,1},{4,6},{5,7},{6,4},{7,5},{8,10},{9,11},{10,... | collective-permute-start | bytes 2654216 | tf_op jit(solution)/shard_map/ppermute | solution.py:387
  470.4 7.9 %collective-permute-start.22 = (bf16[2,768,96]{1,2,0:T(8,128)(2,1)S(1)}, bf16[2,768,96]{1,2,0:T(8,128)(2,1)S(1)}, u32[]{:S(2)}, u32[]{:S(2)}) collective-permute-start(bf16[2,768,96]{1,2,0:T(8,128)(2,1)S(1)} %bitcast.363), channel_id=1, source_target_pairs={{0,8},{8,0},{16,24},{24,16},{1,9},{9,1},{17,25},{25,17},{2,10},{10... | collective-permute-start | bytes 884744 | tf_op jit(solution)/shard_map/ppermute | solution.py:400
  473.8 11.5 %collective-permute-start.17 = (bf16[2,192,384]{2,1,0:T(8,128)(2,1)S(1)}, bf16[2,192,384]{2,1,0:T(8,128)(2,1)S(1)}, u32[]{:S(2)}, u32[]{:S(2)}) collective-permute-start(bf16[2,192,384]{2,1,0:T(8,128)(2,1)S(1)} %fusion.69), channel_id=1, source_target_pairs={{0,8},{8,0},{16,24},{24,16},{1,9},{9,1},{17,25},{25,17},{2,10},{10... | collective-permute-start | bytes 884744 | tf_op jit(solution)/shard_map/ppermute | solution.py:400
  482.0 8.4 %collective-permute-start.6 = (bf16[768,288]{0,1:T(8,128)(2,1)S(1)}, bf16[768,288]{0,1:T(8,128)(2,1)S(1)}, u32[]{:S(2)}, u32[]{:S(2)}) collective-permute-start(bf16[768,288]{0,1:T(8,128)(2,1)S(1)} %fusion.66), channel_id=1, source_target_pairs={{0,4},{1,5},{2,6},{3,7},{4,0},{5,1},{6,2},{7,3},{8,12},{9,13},{10,... | collective-permute-start | bytes 1327112 | tf_op jit(solution)/shard_map/ppermute | solution.py:387
  484.3 11.1 %collective-permute-start.23 = (bf16[768,96]{0,1:T(8,128)(2,1)}, bf16[768,96]{0,1:T(8,128)(2,1)}, u32[]{:S(2)}, u32[]{:S(2)}) collective-permute-start(bf16[768,96]{0,1:T(8,128)(2,1)} %fusion.74), channel_id=1, source_target_pairs={{0,16},{8,24},{16,0},{24,8},{1,17},{9,25},{17,1},{25,9},{2,18},{10... | collective-permute-start | bytes 442376 | tf_op jit(solution)/shard_map/ppermute | solution.py:400
  486.1 15.7 %collective-permute-start.18 = (bf16[192,384]{1,0:T(8,128)(2,1)}, bf16[192,384]{1,0:T(8,128)(2,1)}, u32[]{:S(2)}, u32[]{:S(2)}) collective-permute-start(bf16[192,384]{1,0:T(8,128)(2,1)} %fusion.73), channel_id=1, source_target_pairs={{0,16},{8,24},{16,0},{24,8},{1,17},{9,25},{17,1},{25,9},{2,18},{10... | collective-permute-start | bytes 442376 | tf_op jit(solution)/shard_map/ppermute | solution.py:400
  492.7 8.8 %collective-permute-start.7 = (bf16[2,192,288]{2,1,0:T(8,128)(2,1)S(1)}, bf16[2,192,288]{2,1,0:T(8,128)(2,1)S(1)}, u32[]{:S(2)}, u32[]{:S(2)}) collective-permute-start(bf16[2,192,288]{2,1,0:T(8,128)(2,1)S(1)} %bitcast.364), channel_id=1, source_target_pairs={{0,8},{8,0},{16,24},{24,16},{1,9},{9,1},{17,25},{25,17},{2,10},{10... | collective-permute-start | bytes 663560 | tf_op jit(solution)/shard_map/ppermute | solution.py:400
  (51 other events, 534.9 us)
Sparse Core Ops, SparseCore 0:
  33.2 33.2 all-gather.5
  74.6 25.9 all-gather.7
  102.5 56.1 all-gather.11
  160.4 47.6 all-gather.9

commit v4 on v1

--- a/solution.py
+++ b/solution.py
@@ -18,8 +18,8 @@
 NT_DIMS = (((1,), (1,)), ((), ()))
 
 
-def fwd_kernel(seg_ref, q_ref, k_ref, v_ref, o_ref, lse_ref, *, bq, bk, scale):
-    pair = pl.program_id(0)
+def fwd_kernel(seg_ref, q_ref, k_ref, v_ref, o_ref, lse_ref, *, bq, bk, scale, first):
+    pair = first + pl.program_id(0)
     qi = pl.program_id(1)
     seg_len = seg_ref[pair]
     q_start = qi * bq
@@ -60,8 +60,8 @@
     lse_ref[0] = jnp.transpose(jnp.broadcast_to(lse, (bq, 128)))[0:1, :]
 
 
-def attn_forward(qkv_t, seg_pairs, bq=512, bk=512):
-    pairs, _, head_size, seq_len = qkv_t.shape
+def attn_forward(qkv_t, seg_pairs, first, pairs, bq=512, bk=512):
+    _, _, head_size, seq_len = qkv_t.shape
     scale = head_size ** (-0.5)
     n_q = seq_len // bq
     blocks_done = pairs * (seq_len // bk) * (seq_len // bk + 1) // 2
@@ -74,9 +74,9 @@
         num_scalar_prefetch=1,
         grid=(pairs, n_q),
         in_specs=[
-            pl.BlockSpec((1, 1, head_size, bq), lambda p, i, seg: (p, 0, 0, i)),
-            pl.BlockSpec((1, 1, head_size, seq_len), lambda p, i, seg: (p, 1, 0, 0)),
-            pl.BlockSpec((1, 1, head_size, seq_len), lambda p, i, seg: (p, 2, 0, 0)),
+            pl.BlockSpec((1, 1, head_size, bq), lambda p, i, seg: (p + first, 0, 0, i)),
+            pl.BlockSpec((1, 1, head_size, seq_len), lambda p, i, seg: (p + first, 1, 0, 0)),
+            pl.BlockSpec((1, 1, head_size, seq_len), lambda p, i, seg: (p + first, 2, 0, 0)),
         ],
         out_specs=[
             pl.BlockSpec((1, head_size, bq), lambda p, i, seg: (p, 0, i)),
@@ -84,7 +84,7 @@
         ],
     )
     return pl.pallas_call(
-        functools.partial(fwd_kernel, bq=bq, bk=bk, scale=scale),
+        functools.partial(fwd_kernel, bq=bq, bk=bk, scale=scale, first=first),
         grid_spec=grid_spec,
         out_shape=[
             jax.ShapeDtypeStruct((pairs, head_size, seq_len), jnp.bfloat16),
@@ -95,8 +95,8 @@
     )(seg_pairs, qkv_t, qkv_t, qkv_t)
 
 
-def bwd_kernel(seg_ref, q_ref, k_ref, v_ref, do_ref, o_ref, lse_ref, out_ref, dq_acc, *, bk, bq, scale):
-    pair = pl.program_id(0)
+def bwd_kernel(seg_ref, q_ref, k_ref, v_ref, do_ref, o_ref, lse_ref, out_ref, dq_acc, *, bk, bq, scale, first):
+    pair = first + pl.program_id(0)
     kj = pl.program_id(1)
 
     @pl.when(kj == 0)
@@ -147,8 +147,8 @@
     out_ref[0, 2] = dv_t.astype(out_ref.dtype)
 
 
-def attn_backward(qkv_t, dout_t, out_t, lse, seg_pairs, bk=512, bq=512):
-    pairs, _, head_size, seq_len = qkv_t.shape
+def attn_backward(qkv_t, dout_t, out_t, lse, seg_pairs, first, pairs, bk=512, bq=512):
+    _, _, head_size, seq_len = qkv_t.shape
     scale = head_size ** (-0.5)
     n_k = seq_len // bk
     blocks_done = pairs * (seq_len // bq) * (seq_len // bq + 1) // 2
@@ -161,18 +161,18 @@
         num_scalar_prefetch=1,
         grid=(pairs, n_k),
         in_specs=[
-            pl.BlockSpec((1, 1, head_size, seq_len), lambda p, j, seg: (p, 0, 0, 0)),
-            pl.BlockSpec((1, 1, head_size, bk), lambda p, j, seg: (p, 1, 0, j)),
-            pl.BlockSpec((1, 1, head_size, bk), lambda p, j, seg: (p, 2, 0, j)),
-            pl.BlockSpec((1, head_size, seq_len), lambda p, j, seg: (p, 0, 0)),
-            pl.BlockSpec((1, head_size, seq_len), lambda p, j, seg: (p, 0, 0)),
-            pl.BlockSpec((1, 1, seq_len), lambda p, j, seg: (p, 0, 0)),
+            pl.BlockSpec((1, 1, head_size, seq_len), lambda p, j, seg: (p + first, 0, 0, 0)),
+            pl.BlockSpec((1, 1, head_size, bk), lambda p, j, seg: (p + first, 1, 0, j)),
+            pl.BlockSpec((1, 1, head_size, bk), lambda p, j, seg: (p + first, 2, 0, j)),
+            pl.BlockSpec((1, head_size, seq_len), lambda p, j, seg: (p + first, 0, 0)),
+            pl.BlockSpec((1, head_size, seq_len), lambda p, j, seg: (p + first, 0, 0)),
+            pl.BlockSpec((1, 1, seq_len), lambda p, j, seg: (p + first, 0, 0)),
         ],
         out_specs=pl.BlockSpec((1, 3, head_size, bk), lambda p, j, seg: (p, 0, 0, j)),
         scratch_shapes=[pltpu.VMEM((head_size, seq_len), jnp.float32)],
     )
     return pl.pallas_call(
-        functools.partial(bwd_kernel, bk=bk, bq=bq, scale=scale),
+        functools.partial(bwd_kernel, bk=bk, bq=bq, scale=scale, first=first),
         grid_spec=grid_spec,
         out_shape=jax.ShapeDtypeStruct((pairs, 3, head_size, seq_len), jnp.bfloat16),
         cost_estimate=cost,
@@ -302,7 +302,9 @@
         offset += w.size
     w_proj, w_up, w_down = later_full
     qkv_t = jnp.transpose(incoming, (1, 2, 3, 0, 4)).reshape(per_dev, 3, HD, SLOT)
-    attn_t, lse_rows = attn_forward(qkv_t, seg_pairs)
+    fwd_parts = [attn_forward(qkv_t, seg_pairs, c, 1) for c in range(per_dev)]
+    attn_t = jnp.concatenate([part[0] for part in fwd_parts], axis=0)
+    lse_rows = jnp.concatenate([part[1] for part in fwd_parts], axis=0)
     back = jnp.transpose(attn_t.reshape(per_dev, HD, n_seq, piece_len), (2, 0, 1, 3))
     returned = lax.all_to_all(back, "seq", split_axis=0, concat_axis=0, tiled=True)
     lse_all = lax.all_gather(lse_rows.reshape(per_dev, SLOT), "seq", axis=0, tiled=True)
@@ -356,7 +358,10 @@
     ).reshape(n_seq, per_dev, HD, piece_len)
     dattn_in = lax.all_to_all(dsend, "seq", split_axis=0, concat_axis=0, tiled=True)
     dout_t = jnp.transpose(dattn_in, (1, 2, 0, 3)).reshape(per_dev, HD, SLOT)
-    dpairs = attn_backward(qkv_t, dout_t, attn_t, lse_rows, seg_pairs)
+    dpairs = jnp.concatenate(
+        [attn_backward(qkv_t, dout_t, attn_t, lse_rows, seg_pairs, c, 1) for c in range(per_dev)],
+        axis=0,
+    )
     dback = jnp.transpose(
         dpairs.reshape(per_dev, 3, HD, n_seq, piece_len), (3, 0, 1, 2, 4)
     )

time: 508 us -> 523 us (1.030)
  starting transfers between devices: 54.7 us -> 69.9 us
  local copies, waits for them, and re-layouts: 107 us -> 120 us
    ppermute x5, starting transfers between devices: 18 us -> 32.4 us  [local(): small_sums = small_sums + lax.ppermute(small_sums, axis, partner)]
    pallas_call x0 -> x2, local copies, waits for them, and re-layouts: none -> 12.2 us  [attn_forward(): pl.pallas_call(functools.partial(fwd_kernel, bq=bq, bk=bk, scale=scale, f...]
    pallas_call x2 -> x4, Pallas kernels: 38 us -> 32.9 us  [the longest x3 25.5 us: attn_backward(): pl.pallas_call(functools.partial(bwd_kernel, bk=bk, bq=bq, scale=scale, f...]
    unnamed x142 -> x159, local copies, waits for them, and re-layouts: 29.1 us -> 30.7 us
  transfers between devices with their start and end apart: 33 -> 33, of which waited for: 13 -> 12; matrix products, arithmetic and copies ran while one was open for 34% -> 36% of each run, Pallas kernels for 8% -> 6%
where the time goes in v4:
time: 523 us; the launch traced here: 514 us
  waiting for transfers between devices  129 us (25%)
  local copies, waits for them, and re-layouts  120 us (23%)
  starting transfers between devices  69.9 us (13%)
  other arithmetic  69.6 us (13%)
  matrix products  64.4 us (12%)
  Pallas kernels  32.9 us (6%)
  between operations  15.9 us (3%)
  blocking collectives  11.8 us (2%)
    ppermute x4, waiting for transfers between devices, gather_rows(): got = lax.ppermute(acc, 'batch', partner)  36.7 us
    ppermute x12, waiting for transfers between devices, by_cols(): got = lax.ppermute(send.astype(jnp.bfloat16), 'seq', partner)  36.5 us
    ppermute x5, starting transfers between devices, local(): small_sums = small_sums + lax.ppermute(small_sums, axis, partner)  32.4 us
    unnamed x159, local copies, waits for them, and re-layouts  30.7 us
    all_to_all x1, waiting for transfers between devices, local(): lax.all_to_all(send, 'seq', split_axis=0, concat_axis=0, tiled=True)  28.4 us
    pallas_call x3, Pallas kernels, attn_backward(): pl.pallas_call(functools.partial(bwd_kernel, bk=bk, bq=bq, scale=scale, f...  25.5 us
    add x8, other arithmetic, by_cols(): acc = keep + got.astype(jnp.float32)  16.8 us
    all_to_all x1, waiting for transfers between devices, local(): lax.all_to_all(dback, 'seq', split_axis=0, concat_axis=0, tiled=True)  14.4 us
  transfers between devices with their start and end apart: 33, of which 12 were waited for; matrix products, arithmetic and copies ran while one was open for 36% of the time, Pallas kernels for 6%

profile of v4, /device:TPU:0, one launch (start us, length us, event | category | flops | bytes accessed | tf_op | source)
XLA Modules:
  0.0 514.2 jit_solution(822796967904408929)
XLA Ops:
  20.7 7.2 %collective-permute-done.1 = bf16[2,192,288]{2,1,0:T(8,128)(2,1)S(1)} collective-permute-done((bf16[2,192,288]{2,1,0:T(8,128)(2,1)S(1)}, bf16[2,192,288]{2,1,0:T(8,128)(2,1)S(1)}, u32[]{:S(2)}, u32[]{:S(2)}) %collective-permute-start.1) | collective-permute-done | bytes 221216 | tf_op jit(solution)/shard_map/ppermute | solution.py:269
  33.9 13.6 %collective-permute-done.2 = bf16[165888]{0:T(1024)(128)(2,1)S(1)} collective-permute-done((bf16[165888]{0:T(1024)(128)(2,1)S(1)}, bf16[165888]{0:T(1024)(128)(2,1)S(1)}, u32[]{:S(2)}, u32[]{:S(2)}) %collective-permute-start.2) | collective-permute-done | bytes 331808 | tf_op jit(solution)/shard_map/ppermute | solution.py:269
  54.9 11.9 %collective-permute-done.3 = bf16[2,165888]{1,0:T(2,128)(2,1)S(1)} collective-permute-done((bf16[2,165888]{1,0:T(2,128)(2,1)S(1)}, bf16[2,165888]{1,0:T(2,128)(2,1)S(1)}, u32[]{:S(2)}, u32[]{:S(2)}) %collective-permute-start.3) | collective-permute-done | bytes 663584 | tf_op jit(solution)/shard_map/ppermute | solution.py:269
  80.9 4.2 fusion.73
  112.7 28.4 %all-to-all-done = bf16[8,3,3,64,256]{4,3,2,1,0:T(8,128)(2,1)S(1)} async-done(((bf16[8,3,3,64,256]{4,3,2,1,0:T(8,128)(2,1)}), bf16[8,3,3,64,256]{4,3,2,1,0:T(8,128)(2,1)S(1)}, u32[]{:S(2)}, u32[]{:S(2)}) %all-to-all-start) | async-done | bytes 2359328 | tf_op jit(solution)/shard_map/all_to_all | solution.py:291
  142.8 7.4 %attn_fwd.3 = (bf16[1,64,2048]{2,1,0:T(8,128)(2,1)}, f32[1,1,2048]{2,1,0:T(1,128)}) custom-call(s32[3]{0:T(128)} %and_select_fusion.2.seg_ref, bf16[3,3,64,2048]{3,2,1,0:T(8,128)(2,1)} %bitcast.268, bf16[3,3,64,2048]{3,2,1,0:T(8,128)(2,1)} %bitcast.269, bf16[3,3,64,2048]{3,2,1,0:T(8,128)(2,1)} %bitcast.270), custom_call_target="tpu_custom_call" | custom-call | flops 671088640 | bytes 1056768 | tf_op jit(solution)/shard_map/attn_fwd/pallas_call | solution.py:86
  150.9 6.1 %attn_fwd.5 = (f32[3,1,2048]{2,1,0:T(1,128)S(1)}, bf16[1,64,2048]{2,1,0:T(8,128)(2,1)}) fusion(f32[3,1,2048]{2,1,0:T(1,128)S(1)} %constant_dynamic-update-slice_fusion.2, s32[3]{0:T(128)S(1)} %copy-done.49, bf16[3,3,64,2048]{3,2,1,0:T(8,128)(2,1)S(1)} %bitcast.280), kind=kCustom, calls=%fused_computation.165 | custom fusion | bytes 2630144 | tf_op jit(solution)/shard_map/attn_fwd/pallas_call | solution.py:86
  156.9 6.1 %attn_fwd.4 = (f32[3,1,2048]{2,1,0:T(1,128)S(1)}, bf16[1,64,2048]{2,1,0:T(8,128)(2,1)}) fusion(f32[3,1,2048]{2,1,0:T(1,128)S(1)} %get-tuple-element.98, s32[3]{0:T(128)S(1)} %copy-done.49, bf16[3,3,64,2048]{3,2,1,0:T(8,128)(2,1)S(1)} %bitcast.281), kind=kCustom, calls=%fused_computation.164 | custom fusion | bytes 2630144 | tf_op jit(solution)/shard_map/attn_fwd/pallas_call | solution.py:86
  166.2 4.2 all-to-all-start.1
  171.1 4.5 multiply_convert_fusion
  175.6 11.8 %all-gather = f32[24,1,2048]{2,1,0:T(1,128)S(1)} all-gather(f32[3,1,2048]{2,1,0:T(1,128)S(1)} %get-tuple-element.102.lse_ref), channel_id=2, replica_groups=mesh['batch'=4,'seq'=8] {'seq'}, dimensions={0}, use_global_device_ids=true | all-gather | bytes 221184 | tf_op jit(solution)/shard_map/all_gather | solution.py:310
  195.4 7.2 %fusion.90 = f32[512,3072]{1,0:T(8,128)} fusion(bf16[512,768]{1,0:T(8,128)(2,1)S(1)} %copy-done.7, bf16[3072,768]{0,1:T(8,128)(2,1)} %all-gather.12.cloned.1.call-done), kind=kOutput, calls=%fused_computation.214 | convolution fusion | flops 2415919104 | bytes 11796480 | tf_op jit(solution)/shard_map/nd,fd->nf/dot_general | solution.py:339
  202.6 12.3 %fusion.6 = (bf16[512,3072]{1,0:T(8,128)(2,1)}, f32[512,3072]{1,0:T(8,128)}) fusion(f32[512,3072]{1,0:T(8,128)} %fusion.90, bf16[768,3072]{1,0:T(8,128)(2,1)} %all-gather.10.cloned.1.call-done, f32[512,768]{1,0:T(8,128)S(1)} %get-tuple-element.161, f32[768]{0:T(1024)S(1)} %copy-done.59, f32[768]{0:T(1024)S(1)} %copy-done.52, f32[512]{0:T(512)S(1)} %add_rsqrt_fusion, ...), kind=kOutput, calls=%fused_computation.11 | convolution fusion | flops 2449342464 | bytes 22030336 | tf_op jit(solution)/shard_map/dot_general | solution.py:318
  214.9 4.8 copy.181
  219.7 7.5 %multiply_reduce_fusion = (f32[768]{0:T(1024)}, f32[512]{0:T(512)S(1)}, f32[512]{0:T(512)S(1)}, f32[768]{0:T(1024)}, f32[512,768]{1,0:T(8,128)S(1)}) fusion(f32[512,768]{1,0:T(8,128)} %copy-done.13, f32[512]{0:T(512)S(1)} %add_rsqrt_fusion, f32[512]{0:T(512)S(1)} %broadcast_multiply_fusion.5, f32[768]{0:T(1024)S(1)} %copy-done.52, ...), kind=kOutput, calls=%fused_computation.93 | convolution fusion | flops 2419455488 | bytes 11027456 | tf_op jit(solution)/shard_map/nf,df->nd/dot_general | solution.py:345
  227.2 13.9 %fusion.36 = (bf16[512,768]{1,0:T(8,128)(2,1)}, f32[512,768]{1,0:T(8,128)S(1)}) fusion(f32[]{:T(128)} %bitcast.34, f32[]{:T(128)} %bitcast.32, f32[]{:T(128)} %bitcast.30, f32[]{:T(128)} %bitcast.28, f32[]{:T(128)} %bitcast.26, f32[]{:T(128)} %bitcast.24, f32[]{:T(128)} %bitcast.22, f32[]{:T(128)} %bitcast.20, f32[]{:T(128)} %bitcast, ...), kind=kOutput, calls=%fused_computation.80 | convolution fusion | flops 2440691712 | bytes 21233700 | tf_op jit(solution)/shard_map/dot_general | solution.py:321
  241.1 4.6 fusion.44
  250.8 4.4 all-to-all-start.2
  255.2 5.0 fusion.7
  276.5 6.0 %copy.169 = f32[2,2,1,768,384]{4,3,0,1,2:T(8,128)} copy(f32[2,2,1,768,384]{3,4,2,1,0:T(8,128)} %constant_dynamic-slice_fusion.3) | data formatting | bytes 9437184 | tf_op jit(solution)/shard_map/jit(dynamic_index_in_dim)/dynamic_slice | solution.py:389
  294.2 8.5 %attn_bwd.3 = bf16[1,3,64,2048]{3,2,1,0:T(8,128)(2,1)} custom-call(s32[3]{0:T(128)} %and_select_fusion.2.seg_ref, bf16[3,3,64,2048]{3,2,1,0:T(8,128)(2,1)} %bitcast.271, bf16[3,3,64,2048]{3,2,1,0:T(8,128)(2,1)} %bitcast.272, bf16[3,3,64,2048]{3,2,1,0:T(8,128)(2,1)} %bitcast.273, bf16[3,64,2048]{2,1,0:T(8,128)(2,1)} %bitcast.289, ...), custom_call_target="tpu_custom_call" | custom-call | flops 1677721600 | bytes 2105344 | tf_op jit(solution)/shard_map/attn_bwd/pallas_call | solution.py:174
  302.7 8.4 %attn_bwd.4 = bf16[1,3,64,2048]{3,2,1,0:T(8,128)(2,1)} custom-call(s32[3]{0:T(128)} %and_select_fusion.2.seg_ref, bf16[3,3,64,2048]{3,2,1,0:T(8,128)(2,1)} %bitcast.274, bf16[3,3,64,2048]{3,2,1,0:T(8,128)(2,1)} %bitcast.275, bf16[3,3,64,2048]{3,2,1,0:T(8,128)(2,1)} %bitcast.276, bf16[3,64,2048]{2,1,0:T(8,128)(2,1)} %bitcast.290, ...), custom_call_target="tpu_custom_call" | custom-call | flops 1677721600 | bytes 2105344 | tf_op jit(solution)/shard_map/attn_bwd/pallas_call | solution.py:174
  311.1 8.6 %attn_bwd.5 = bf16[1,3,64,2048]{3,2,1,0:T(8,128)(2,1)} custom-call(s32[3]{0:T(128)} %and_select_fusion.2.seg_ref, bf16[3,3,64,2048]{3,2,1,0:T(8,128)(2,1)} %bitcast.277, bf16[3,3,64,2048]{3,2,1,0:T(8,128)(2,1)} %bitcast.278, bf16[3,3,64,2048]{3,2,1,0:T(8,128)(2,1)} %bitcast.279, bf16[3,64,2048]{2,1,0:T(8,128)(2,1)} %bitcast.291, ...), custom_call_target="tpu_custom_call" | custom-call | flops 1677721600 | bytes 2105344 | tf_op jit(solution)/shard_map/attn_bwd/pallas_call | solution.py:174
  342.0 14.4 %all-to-all-done.3 = bf16[8,3,3,64,256]{4,3,2,1,0:T(8,128)(2,1)S(1)} async-done(((bf16[8,3,3,64,256]{4,3,2,1,0:T(8,128)(2,1)}), bf16[8,3,3,64,256]{4,3,2,1,0:T(8,128)(2,1)S(1)}, u32[]{:S(2)}, u32[]{:S(2)}) %all-to-all-start.3) | async-done | bytes 2359328 | tf_op jit(solution)/shard_map/all_to_all | solution.py:368
  368.9 12.0 %collective-permute-done.14 = bf16[2,3072,96]{1,2,0:T(8,128)(2,1)} collective-permute-done((bf16[2,3072,96]{1,2,0:T(8,128)(2,1)}, bf16[2,3072,96]{1,2,0:T(8,128)(2,1)}, u32[]{:S(2)}, u32[]{:S(2)}) %collective-permute-start.14) | collective-permute-done | bytes 1179680 | tf_op jit(solution)/shard_map/ppermute | solution.py:392
  388.3 17.3 %collective-permute-done.11 = bf16[2,768,384]{2,1,0:T(8,128)(2,1)} collective-permute-done((bf16[2,768,384]{2,1,0:T(8,128)(2,1)S(1)}, bf16[2,768,384]{2,1,0:T(8,128)(2,1)}, u32[]{:S(2)}, u32[]{:S(2)}) %collective-permute-start.11) | collective-permute-done | bytes 1179680 | tf_op jit(solution)/shard_map/ppermute | solution.py:392
  419.1 4.2 fusion.26
  423.2 6.3 %concatenate.71 = f32[3081]{0:T(1024)S(1)} concatenate(f32[768]{0:T(1024)} %get-tuple-element.114, f32[768]{0:T(1024)} %get-tuple-element.119, f32[768]{0:T(1024)} %get-tuple-element.112, f32[768]{0:T(1024)} %get-tuple-element.118, f32[1]{0:T(128)} %bitcast.98, f32[1]{0:T(128)} %bitcast.100, f32[1]{0:T(128)} %bitcast.102, f32[1]{0:T(128)} %bitcast.104, f32[1]{0:T(128)} %bitcast.106, ...), dimensions={0} | concatenate | bytes 24648 | tf_op jit(solution)/shard_map/concatenate | solution.py:405
  447.3 5.5 %collective-permute-done.6 = bf16[768,288]{0,1:T(8,128)(2,1)S(1)} collective-permute-done((bf16[768,288]{0,1:T(8,128)(2,1)S(1)}, bf16[768,288]{0,1:T(8,128)(2,1)S(1)}, u32[]{:S(2)}, u32[]{:S(2)}) %collective-permute-start.6) | collective-permute-done | bytes 442400 | tf_op jit(solution)/shard_map/ppermute | solution.py:392
  455.2 25.0 %collective-permute-start.19 = (f32[3081]{0:T(1024)S(1)}, f32[3081]{0:T(1024)S(1)}, u32[]{:S(2)}, u32[]{:S(2)}) collective-permute-start(f32[3081]{0:T(1024)S(1)} %add.340), channel_id=1, source_target_pairs={{0,8},{8,0},{16,24},{24,16},{1,9},{9,1},{17,25},{25,17},{2,10},{10... | collective-permute-start | bytes 36980 | tf_op jit(solution)/shard_map/ppermute | solution.py:411
  482.0 4.5 collective-permute-start.20
  493.8 11.2 %reduce-scatter.13.cloned.1.call-done = bf16[192,288]{1,0:T(8,128)(2,1)} async-done(((bf16[768,288]{1,0:T(8,128)(2,1)}), bf16[192,288]{1,0:T(8,128)(2,1)}) %reduce-scatter.13.cloned.1.call-update) | async-done | bytes 110608
  (354 shorter events, 201.2 us)
Async XLA Ops:
  7.2 73.6 %all-gather.6.cloned.1.call-start = ((), (), s32[]{:S(2)}) async-start(), calls=%async_computation.8 | async-start | bytes 3981312 | tf_op jit(solution)/shard_map/all_gather | solution.py:277
  7.2 11.4 %collective-permute-start = (bf16[192,288]{1,0:T(8,128)(2,1)}, bf16[192,288]{1,0:T(8,128)(2,1)S(1)}, u32[]{:S(2)}, u32[]{:S(2)}) collective-permute-start(bf16[192,288]{1,0:T(8,128)(2,1)} %param.17), channel_id=1, source_target_pairs={{0,16},{8,24},{16,0},{24,8},{1,17},{9,25},{17,1},{25,9},{2,18},{10... | collective-permute-start | bytes 331784 | tf_op jit(solution)/shard_map/ppermute | solution.py:269
  19.7 8.2 %collective-permute-start.1 = (bf16[2,192,288]{2,1,0:T(8,128)(2,1)S(1)}, bf16[2,192,288]{2,1,0:T(8,128)(2,1)S(1)}, u32[]{:S(2)}, u32[]{:S(2)}) collective-permute-start(bf16[2,192,288]{2,1,0:T(8,128)(2,1)S(1)} %maximum_select_fusion.2), channel_id=1, source_target_pairs={{0,8},{8,0},{16,24},{24,16},{1,9},{9,1},{17,25},{25,17},{2,10},{10... | collective-permute-start | bytes 663560 | tf_op jit(solution)/shard_map/ppermute | solution.py:269
  29.9 17.6 %collective-permute-start.2 = (bf16[165888]{0:T(1024)(128)(2,1)S(1)}, bf16[165888]{0:T(1024)(128)(2,1)S(1)}, u32[]{:S(2)}, u32[]{:S(2)}) collective-permute-start(bf16[165888]{0:T(1024)(128)(2,1)S(1)} %pad_maximum_fusion.6), channel_id=1, source_target_pairs={{0,16},{8,24},{16,0},{24,8},{1,17},{9,25},{17,1},{25,9},{2,18},{10... | collective-permute-start | bytes 995336 | tf_op jit(solution)/shard_map/ppermute | solution.py:269
  33.0 158.3 %all-gather.8.cloned.1.call-start = ((), (), s32[]{:S(2)}) async-start(), calls=%async_computation.9 | async-start | bytes 1327104 | tf_op jit(solution)/shard_map/all_gather | solution.py:301
  50.8 16.0 %collective-permute-start.3 = (bf16[2,165888]{1,0:T(2,128)(2,1)S(1)}, bf16[2,165888]{1,0:T(2,128)(2,1)S(1)}, u32[]{:S(2)}, u32[]{:S(2)}) collective-permute-start(bf16[2,165888]{1,0:T(2,128)(2,1)S(1)} %broadcast_select_fusion.1), channel_id=1, source_target_pairs={{0,8},{8,0},{16,24},{24,16},{1,9},{9,1},{17,25},{25,17},{2,10},{10... | collective-permute-start | bytes 1990664 | tf_op jit(solution)/shard_map/ppermute | solution.py:269
  74.4 119.7 %all-gather.12.cloned.1.call-start = ((), (), s32[]{:S(2)}) async-start(), calls=%async_computation.11 | async-start | bytes 5308416 | tf_op jit(solution)/shard_map/all_gather | solution.py:301
  76.7 126.0 %all-gather.10.cloned.1.call-start = ((), (), s32[]{:S(2)}) async-start(), calls=%async_computation.10 | async-start | bytes 5308416 | tf_op jit(solution)/shard_map/all_gather | solution.py:301
  101.3 39.7 %all-to-all-start = ((bf16[8,3,3,64,256]{4,3,2,1,0:T(8,128)(2,1)}), bf16[8,3,3,64,256]{4,3,2,1,0:T(8,128)(2,1)S(1)}, u32[]{:S(2)}, u32[]{:S(2)}) async-start(bf16[8,3,3,64,256]{4,3,2,1,0:T(8,128)(2,1)} %copy.148), calls=%async_computation | async-start | bytes 4718592 | tf_op jit(solution)/shard_map/all_to_all | solution.py:291
  166.2 22.1 %all-to-all-start.1 = ((bf16[8,3,64,256]{3,2,1,0:T(8,128)(2,1)}), bf16[8,3,64,256]{3,2,1,0:T(8,128)(2,1)}, u32[]{:S(2)}, u32[]{:S(2)}) async-start(bf16[8,3,64,256]{3,2,1,0:T(8,128)(2,1)} %bitcast.316), calls=%async_computation.1 | async-start | bytes 1572864 | tf_op jit(solution)/shard_map/all_to_all | solution.py:309
  250.8 41.3 %all-to-all-start.2 = ((bf16[8,3,64,256]{3,2,1,0:T(8,128)(2,1)}), bf16[8,3,64,256]{3,2,1,0:T(8,128)(2,1)}, u32[]{:S(2)}, u32[]{:S(2)}) async-start(bf16[8,3,64,256]{3,2,1,0:T(8,128)(2,1)} %bitcast.37), calls=%async_computation.2 | async-start | bytes 1572864 | tf_op jit(solution)/shard_map/all_to_all | solution.py:359
  262.0 68.5 %collective-permute-start.13 = (bf16[2,2,3072,96]{2,3,0,1:T(8,128)(2,1)}, bf16[2,2,3072,96]{2,3,0,1:T(8,128)(2,1)}, u32[]{:S(2)}, u32[]{:S(2)}) collective-permute-start(bf16[2,2,3072,96]{2,3,0,1:T(8,128)(2,1)} %fusion.9), channel_id=1, source_target_pairs={{0,1},{1,0},{2,3},{3,2},{4,5},{5,4},{6,7},{7,6},{8,9},{9,8},{10,11... | collective-permute-start | bytes 7077896 | tf_op jit(solution)/shard_map/ppermute | solution.py:392
  266.5 21.6 %collective-permute-start.7 = (bf16[2,2,768,96]{2,3,1,0:T(8,128)(2,1)S(1)}, bf16[2,2,768,96]{2,3,1,0:T(8,128)(2,1)}, u32[]{:S(2)}, u32[]{:S(2)}) collective-permute-start(bf16[2,2,768,96]{2,3,1,0:T(8,128)(2,1)S(1)} %fusion.63), channel_id=1, source_target_pairs={{0,1},{1,0},{2,3},{3,2},{4,5},{5,4},{6,7},{7,6},{8,9},{9,8},{10,11... | collective-permute-start | bytes 1769480 | tf_op jit(solution)/shard_map/ppermute | solution.py:392
  287.6 49.4 %collective-permute-start.10 = (bf16[2,2,768,384]{3,2,0,1:T(8,128)(2,1)}, bf16[2,2,768,384]{3,2,0,1:T(8,128)(2,1)}, u32[]{:S(2)}, u32[]{:S(2)}) collective-permute-start(bf16[2,2,768,384]{3,2,0,1:T(8,128)(2,1)} %bitcast.325), channel_id=1, source_target_pairs={{0,1},{1,0},{2,3},{3,2},{4,5},{5,4},{6,7},{7,6},{8,9},{9,8},{10,11... | collective-permute-start | bytes 7077896 | tf_op jit(solution)/shard_map/ppermute | solution.py:392
  290.4 36.3 %collective-permute-start.8 = (bf16[2,768,96]{1,2,0:T(8,128)(2,1)}, bf16[2,768,96]{1,2,0:T(8,128)(2,1)}, u32[]{:S(2)}, u32[]{:S(2)}) collective-permute-start(bf16[2,768,96]{1,2,0:T(8,128)(2,1)} %fusion.66), channel_id=1, source_target_pairs={{0,2},{1,3},{2,0},{3,1},{4,6},{5,7},{6,4},{7,5},{8,10},{9,11},{10,... | collective-permute-start | bytes 884744 | tf_op jit(solution)/shard_map/ppermute | solution.py:392
  322.8 33.6 %all-to-all-start.3 = ((bf16[8,3,3,64,256]{4,3,2,1,0:T(8,128)(2,1)}), bf16[8,3,3,64,256]{4,3,2,1,0:T(8,128)(2,1)S(1)}, u32[]{:S(2)}, u32[]{:S(2)}) async-start(bf16[8,3,3,64,256]{4,3,2,1,0:T(8,128)(2,1)} %bitcast.293), calls=%async_computation.3 | async-start | bytes 4718592 | tf_op jit(solution)/shard_map/all_to_all | solution.py:368
  326.4 116.9 %reduce-scatter.15.cloned.1.call-start = ((), (), s32[]{:S(2)}) async-start(), calls=%async_computation.15 | async-start | bytes 245760
  328.6 56.3 %collective-permute-start.9 = (bf16[768,96]{0,1:T(8,128)(2,1)}, bf16[768,96]{0,1:T(8,128)(2,1)}, u32[]{:S(2)}, u32[]{:S(2)}) collective-permute-start(bf16[768,96]{0,1:T(8,128)(2,1)} %fusion.68), channel_id=1, source_target_pairs={{0,4},{1,5},{2,6},{3,7},{4,0},{5,1},{6,2},{7,3},{8,12},{9,13},{10,... | collective-permute-start | bytes 442376 | tf_op jit(solution)/shard_map/ppermute | solution.py:392
  335.5 45.3 %collective-permute-start.14 = (bf16[2,3072,96]{1,2,0:T(8,128)(2,1)}, bf16[2,3072,96]{1,2,0:T(8,128)(2,1)}, u32[]{:S(2)}, u32[]{:S(2)}) collective-permute-start(bf16[2,3072,96]{1,2,0:T(8,128)(2,1)} %fusion.48), channel_id=1, source_target_pairs={{0,2},{1,3},{2,0},{3,1},{4,6},{5,7},{6,4},{7,5},{8,10},{9,11},{10,... | collective-permute-start | bytes 3538952 | tf_op jit(solution)/shard_map/ppermute | solution.py:392
  341.4 64.2 %collective-permute-start.11 = (bf16[2,768,384]{2,1,0:T(8,128)(2,1)S(1)}, bf16[2,768,384]{2,1,0:T(8,128)(2,1)}, u32[]{:S(2)}, u32[]{:S(2)}) collective-permute-start(bf16[2,768,384]{2,1,0:T(8,128)(2,1)S(1)} %fusion.47), channel_id=1, source_target_pairs={{0,2},{1,3},{2,0},{3,1},{4,6},{5,7},{6,4},{7,5},{8,10},{9,11},{10,... | collective-permute-start | bytes 3538952 | tf_op jit(solution)/shard_map/ppermute | solution.py:392
  368.9 45.1 %collective-permute-start.4 = (bf16[2,2,768,288]{2,3,1,0:T(8,128)(2,1)}, bf16[2,2,768,288]{2,3,1,0:T(8,128)(2,1)}, u32[]{:S(2)}, u32[]{:S(2)}) collective-permute-start(bf16[2,2,768,288]{2,3,1,0:T(8,128)(2,1)} %fusion.18), channel_id=1, source_target_pairs={{0,1},{1,0},{2,3},{3,2},{4,5},{5,4},{6,7},{7,6},{8,9},{9,8},{10,11... | collective-permute-start | bytes 5308424 | tf_op jit(solution)/shard_map/ppermute | solution.py:392
  383.4 28.3 %collective-permute-start.15 = (bf16[3072,96]{0,1:T(8,128)(2,1)}, bf16[3072,96]{0,1:T(8,128)(2,1)}, u32[]{:S(2)}, u32[]{:S(2)}) collective-permute-start(bf16[3072,96]{0,1:T(8,128)(2,1)} %fusion.62), channel_id=1, source_target_pairs={{0,4},{1,5},{2,6},{3,7},{4,0},{5,1},{6,2},{7,3},{8,12},{9,13},{10,... | collective-permute-start | bytes 1769480 | tf_op jit(solution)/shard_map/ppermute | solution.py:392
  388.2 102.3 %reduce-scatter.11.cloned.1.call-start = ((), (), s32[]{:S(2)}) async-start(), calls=%async_computation.13 | async-start | bytes 737280 | tf_op jit(solution)/shard_map/reduce_scatter | solution.py:397
  410.2 19.5 %collective-permute-start.12 = (bf16[768,384]{1,0:T(8,128)(2,1)}, bf16[768,384]{1,0:T(8,128)(2,1)}, u32[]{:S(2)}, u32[]{:S(2)}) collective-permute-start(bf16[768,384]{1,0:T(8,128)(2,1)} %fusion.61), channel_id=1, source_target_pairs={{0,4},{1,5},{2,6},{3,7},{4,0},{5,1},{6,2},{7,3},{8,12},{9,13},{10,... | collective-permute-start | bytes 1769480 | tf_op jit(solution)/shard_map/ppermute | solution.py:392
  413.7 78.4 %reduce-scatter.9.cloned.1.call-start = ((), (), s32[]{:S(2)}) async-start(), calls=%async_computation.12 | async-start | bytes 737280 | tf_op jit(solution)/shard_map/reduce_scatter | solution.py:397
  418.2 21.1 %collective-permute-start.5 = (bf16[2,768,288]{1,2,0:T(8,128)(2,1)}, bf16[2,768,288]{1,2,0:T(8,128)(2,1)}, u32[]{:S(2)}, u32[]{:S(2)}) collective-permute-start(bf16[2,768,288]{1,2,0:T(8,128)(2,1)} %fusion.51), channel_id=1, source_target_pairs={{0,2},{1,3},{2,0},{3,1},{4,6},{5,7},{6,4},{7,5},{8,10},{9,11},{10,... | collective-permute-start | bytes 2654216 | tf_op jit(solution)/shard_map/ppermute | solution.py:392
  432.1 72.9 %reduce-scatter.13.cloned.1.call-start = ((), (), s32[]{:S(2)}) async-start(), calls=%async_computation.14 | async-start | bytes 737280
  436.4 8.6 %collective-permute-start.17 = (f32[3081]{0:T(1024)S(1)}, f32[3081]{0:T(1024)}, u32[]{:S(2)}, u32[]{:S(2)}) collective-permute-start(f32[3081]{0:T(1024)S(1)} %add.338), channel_id=1, source_target_pairs={{0,2},{1,3},{2,0},{3,1},{4,6},{5,7},{6,4},{7,5},{8,10},{9,11},{10,... | collective-permute-start | bytes 36980 | tf_op jit(solution)/shard_map/ppermute | solution.py:411
  442.0 10.8 %collective-permute-start.6 = (bf16[768,288]{0,1:T(8,128)(2,1)S(1)}, bf16[768,288]{0,1:T(8,128)(2,1)S(1)}, u32[]{:S(2)}, u32[]{:S(2)}) collective-permute-start(bf16[768,288]{0,1:T(8,128)(2,1)S(1)} %fusion.65), channel_id=1, source_target_pairs={{0,4},{1,5},{2,6},{3,7},{4,0},{5,1},{6,2},{7,3},{8,12},{9,13},{10,... | collective-permute-start | bytes 1327112 | tf_op jit(solution)/shard_map/ppermute | solution.py:392
  445.7 9.5 %collective-permute-start.18 = (f32[3081]{0:T(1024)S(1)}, f32[3081]{0:T(1024)S(1)}, u32[]{:S(2)}, u32[]{:S(2)}) collective-permute-start(f32[3081]{0:T(1024)S(1)} %add.339), channel_id=1, source_target_pairs={{0,4},{1,5},{2,6},{3,7},{4,0},{5,1},{6,2},{7,3},{8,12},{9,13},{10,... | collective-permute-start | bytes 36980 | tf_op jit(solution)/shard_map/ppermute | solution.py:411
  455.2 26.8 %collective-permute-start.19 = (f32[3081]{0:T(1024)S(1)}, f32[3081]{0:T(1024)S(1)}, u32[]{:S(2)}, u32[]{:S(2)}) collective-permute-start(f32[3081]{0:T(1024)S(1)} %add.340), channel_id=1, source_target_pairs={{0,8},{8,0},{16,24},{24,16},{1,9},{9,1},{17,25},{25,17},{2,10},{10... | collective-permute-start | bytes 36980 | tf_op jit(solution)/shard_map/ppermute | solution.py:411
  482.0 7.3 %collective-permute-start.20 = (f32[3081]{0:T(1024)S(1)}, f32[3081]{0:T(1024)S(1)}, u32[]{:S(2)}, u32[]{:S(2)}) collective-permute-start(f32[3081]{0:T(1024)S(1)} %add.341), channel_id=1, source_target_pairs={{0,16},{8,24},{16,0},{24,8},{1,17},{9,25},{17,1},{25,9},{2,18},{10... | collective-permute-start | bytes 36980 | tf_op jit(solution)/shard_map/ppermute | solution.py:411
  (72 other events, 1287.0 us)
Sparse Core Ops, SparseCore 0:
  33.2 33.2 all-gather.5
  74.6 25.9 all-gather.7
  102.5 52.9 all-gather.11
  157.2 43.6 all-gather.9
  388.3 42.7 reduce-scatter.14
  433.3 25.9 reduce-scatter.10
  461.5 20.3 reduce-scatter.8
  484.3 20.7 reduce-scatter.12

commit v5 on v1

--- a/solution.py
+++ b/solution.py
@@ -381,8 +381,10 @@
         acc = blocks.reshape((2,) * bits + blocks.shape[1:])
         for bit in range(bits):
             mine = (my_index >> bit) & 1
-            keep = lax.dynamic_index_in_dim(acc, mine, axis=bits - 1 - bit, keepdims=False)
-            send = lax.dynamic_index_in_dim(acc, 1 - mine, axis=bits - 1 - bit, keepdims=False)
+            low = lax.index_in_dim(acc, 0, axis=bits - 1 - bit, keepdims=False)
+            high = lax.index_in_dim(acc, 1, axis=bits - 1 - bit, keepdims=False)
+            keep = jnp.where(mine == 0, low, high)
+            send = jnp.where(mine == 0, high, low)
             partner = [(i, i ^ (1 << bit)) for i in range(n_seq)]
             got = lax.ppermute(send.astype(jnp.bfloat16), "seq", partner)
             acc = keep + got.astype(jnp.float32)

time: 508 us -> 518 us (1.020)
  other arithmetic: 68.5 us -> 80.4 us
    convert_element_type x0 -> x12, other arithmetic: none -> 11.8 us  [by_cols(): got = lax.ppermute(send.astype(jnp.bfloat16), 'seq', partner)]
    dynamic_slice x3 -> x0, local copies, waits for them, and re-layouts: 11.1 us -> none  [the longest x2 8.49 us: by_cols(): lax.dynamic_index_in_dim(acc, mine, axis=bits - 1 - bit, keepdims=False)]
    convert_element_type x11 -> x0, local copies, waits for them, and re-layouts: 9.04 us -> none  [by_cols(): got = lax.ppermute(send.astype(jnp.bfloat16), 'seq', partner)]
    unnamed x142 -> x143, local copies, waits for them, and re-layouts: 29.1 us -> 36.8 us
    slice x0 -> x2, local copies, waits for them, and re-layouts: none -> 5.75 us  [the longest x1 4.58 us: by_cols(): low = lax.index_in_dim(acc, 0, axis=bits - 1 - bit, keepdims=False)]
  transfers between devices with their start and end apart: 33 -> 33, of which waited for: 13 -> 14; matrix products, arithmetic and copies ran while one was open for 34% -> 35% of each run, Pallas kernels for 8% -> 7%
where the time goes in v5:
time: 518 us; the launch traced here: 509 us
  waiting for transfers between devices  138 us (27%)
  local copies, waits for them, and re-layouts  102 us (20%)
  other arithmetic  80.4 us (16%)
  matrix products  64.7 us (12%)
  starting transfers between devices  54 us (10%)
  Pallas kernels  38 us (7%)
  blocking collectives  16.9 us (3%)
  between operations  15.7 us (3%)
    ppermute x12, waiting for transfers between devices, by_cols(): got = lax.ppermute(send.astype(jnp.bfloat16), 'seq', partner)  40.9 us
    unnamed x143, local copies, waits for them, and re-layouts  36.8 us
    ppermute x4, waiting for transfers between devices, gather_rows(): got = lax.ppermute(acc, 'batch', partner)  36.7 us
    all_to_all x1, waiting for transfers between devices, local(): lax.all_to_all(send, 'seq', split_axis=0, concat_axis=0, tiled=True)  28.4 us
    pallas_call x1, Pallas kernels, attn_backward(): pl.pallas_call(functools.partial(bwd_kernel, bk=bk, bq=bq, scale=scale),...  20.9 us
    add x8, other arithmetic, by_cols(): acc = keep + got.astype(jnp.float32)  18.7 us
    ppermute x5, starting transfers between devices, local(): small_sums = small_sums + lax.ppermute(small_sums, axis, partner)  17.9 us
    pallas_call x1, Pallas kernels, attn_forward(): pl.pallas_call(functools.partial(fwd_kernel, bq=bq, bk=bk, scale=scale),...  17.1 us
  transfers between devices with their start and end apart: 33, of which 14 were waited for; matrix products, arithmetic and copies ran while one was open for 35% of the time, Pallas kernels for 7%

profile of v5, /device:TPU:0, one launch (start us, length us, event | category | flops | bytes accessed | tf_op | source)
XLA Modules:
  0.0 509.4 jit_solution(1681316826193138596)
XLA Ops:
  20.7 7.2 %collective-permute-done.1 = bf16[2,192,288]{2,1,0:T(8,128)(2,1)S(1)} collective-permute-done((bf16[2,192,288]{2,1,0:T(8,128)(2,1)S(1)}, bf16[2,192,288]{2,1,0:T(8,128)(2,1)S(1)}, u32[]{:S(2)}, u32[]{:S(2)}) %collective-permute-start.1) | collective-permute-done | bytes 221216 | tf_op jit(solution)/shard_map/ppermute | solution.py:269
  33.9 13.6 %collective-permute-done.2 = bf16[165888]{0:T(1024)(128)(2,1)S(1)} collective-permute-done((bf16[165888]{0:T(1024)(128)(2,1)S(1)}, bf16[165888]{0:T(1024)(128)(2,1)S(1)}, u32[]{:S(2)}, u32[]{:S(2)}) %collective-permute-start.2) | collective-permute-done | bytes 331808 | tf_op jit(solution)/shard_map/ppermute | solution.py:269
  54.9 11.9 %collective-permute-done.3 = bf16[2,165888]{1,0:T(2,128)(2,1)S(1)} collective-permute-done((bf16[2,165888]{1,0:T(2,128)(2,1)S(1)}, bf16[2,165888]{1,0:T(2,128)(2,1)S(1)}, u32[]{:S(2)}, u32[]{:S(2)}) %collective-permute-start.3) | collective-permute-done | bytes 663584 | tf_op jit(solution)/shard_map/ppermute | solution.py:269
  81.2 4.2 fusion.76
  113.0 28.4 %all-to-all-done = bf16[8,3,3,64,256]{4,3,2,1,0:T(8,128)(2,1)S(1)} async-done(((bf16[8,3,3,64,256]{4,3,2,1,0:T(8,128)(2,1)}), bf16[8,3,3,64,256]{4,3,2,1,0:T(8,128)(2,1)S(1)}, u32[]{:S(2)}, u32[]{:S(2)}) %all-to-all-start) | async-done | bytes 2359328 | tf_op jit(solution)/shard_map/all_to_all | solution.py:291
  143.2 17.1 %attn_fwd.1 = (bf16[3,64,2048]{2,1,0:T(8,128)(2,1)}, f32[3,1,2048]{2,1,0:T(1,128)}) custom-call(s32[3]{0:T(128)} %and_select_fusion.2.seg_ref, bf16[3,3,64,2048]{3,2,1,0:T(8,128)(2,1)} %bitcast.344, bf16[3,3,64,2048]{3,2,1,0:T(8,128)(2,1)} %bitcast.345, bf16[3,3,64,2048]{3,2,1,0:T(8,128)(2,1)} %bitcast.346), custom_call_target="tpu_custom_call" | custom-call | flops 2013265920 | bytes 3170304 | tf_op jit(solution)/shard_map/attn_fwd/pallas_call | solution.py:86
  166.8 4.5 multiply_convert_fusion
  171.4 16.9 %all-gather = f32[24,1,2048]{2,1,0:T(1,128)S(1)} all-gather(f32[3,1,2048]{2,1,0:T(1,128)S(1)} %copy-done.41), channel_id=2, replica_groups=mesh['batch'=4,'seq'=8] {'seq'}, dimensions={0}, use_global_device_ids=true | all-gather | bytes 221184 | tf_op jit(solution)/shard_map/all_gather | solution.py:308
  195.1 7.2 %fusion.89 = f32[512,3072]{1,0:T(8,128)} fusion(bf16[512,768]{1,0:T(8,128)(2,1)S(1)} %copy-done.9, bf16[3072,768]{0,1:T(8,128)(2,1)} %all-gather.12.cloned.1.call-done), kind=kOutput, calls=%fused_computation.206 | convolution fusion | flops 2415919104 | bytes 11796480 | tf_op jit(solution)/shard_map/nd,fd->nf/dot_general | solution.py:337
  202.3 4.3 all-gather.10.cloned.1.call-done
  206.7 12.3 %fusion.6 = (bf16[512,3072]{1,0:T(8,128)(2,1)}, f32[512,3072]{1,0:T(8,128)}) fusion(f32[512,3072]{1,0:T(8,128)} %fusion.89, bf16[768,3072]{1,0:T(8,128)(2,1)} %all-gather.10.cloned.1.call-done, f32[512,768]{1,0:T(8,128)S(1)} %get-tuple-element.149, f32[768]{0:T(1024)S(1)} %copy-done.53, f32[768]{0:T(1024)S(1)} %copy-done.46, f32[512]{0:T(512)S(1)} %add_rsqrt_fusion, ...), kind=kOutput, calls=%fused_computation.11 | convolution fusion | flops 2449342464 | bytes 22030336 | tf_op jit(solution)/shard_map/dot_general | solution.py:316
  219.0 4.8 copy.193
  223.8 7.5 %multiply_reduce_fusion = (f32[768]{0:T(1024)}, f32[512]{0:T(512)S(1)}, f32[512]{0:T(512)S(1)}, f32[768]{0:T(1024)}, f32[512,768]{1,0:T(8,128)S(1)}) fusion(f32[512,768]{1,0:T(8,128)} %copy-done.15, f32[512]{0:T(512)S(1)} %add_rsqrt_fusion, f32[512]{0:T(512)S(1)} %broadcast_multiply_fusion.5, f32[768]{0:T(1024)S(1)} %copy-done.46, ...), kind=kOutput, calls=%fused_computation.95 | convolution fusion | flops 2419455488 | bytes 11027456 | tf_op jit(solution)/shard_map/nf,df->nd/dot_general | solution.py:343
  231.3 13.9 %fusion.37 = (bf16[512,768]{1,0:T(8,128)(2,1)}, f32[512,768]{1,0:T(8,128)S(1)}) fusion(f32[]{:T(128)} %bitcast.34, f32[]{:T(128)} %bitcast.32, f32[]{:T(128)} %bitcast.30, f32[]{:T(128)} %bitcast.28, f32[]{:T(128)} %bitcast.26, f32[]{:T(128)} %bitcast.24, f32[]{:T(128)} %bitcast.22, f32[]{:T(128)} %bitcast.20, f32[]{:T(128)} %bitcast, ...), kind=kOutput, calls=%fused_computation.82 | convolution fusion | flops 2440691712 | bytes 21233700 | tf_op jit(solution)/shard_map/dot_general | solution.py:319
  245.2 4.7 fusion.45
  255.9 4.2 all-to-all-start.2
  260.1 5.2 %fusion.7 = f32[8,96,3072]{2,1,0:T(8,128)S(1)} fusion(bf16[512,8,96]{0,2,1:T(8,128)(2,1)} %bitcast.354, f32[512,3072]{1,0:T(8,128)} %get-tuple-element.153), kind=kOutput, calls=%fused_computation.32 | convolution fusion | flops 2430074880 | bytes 16515072 | tf_op jit(solution)/shard_map/nf,nbd->bfd/dot_general | solution.py:333
  276.6 4.6 fusion.82
  281.2 6.1 %copy.206 = f32[2,2,1,768,384]{4,3,0,1,2:T(8,128)} copy(f32[2,2,1,768,384]{3,4,2,1,0:T(8,128)} %get-tuple-element.111) | data formatting | bytes 9437184
  287.3 6.0 %copy.207 = f32[2,2,1,768,384]{4,3,0,1,2:T(8,128)} copy(f32[2,2,1,768,384]{3,4,2,1,0:T(8,128)} %get-tuple-element.112) | data formatting | bytes 9437184
  296.5 4.4 fusion.9
  306.9 20.9 %attn_bwd.1 = bf16[3,3,64,2048]{3,2,1,0:T(8,128)(2,1)} custom-call(s32[3]{0:T(128)} %and_select_fusion.2.seg_ref, bf16[3,3,64,2048]{3,2,1,0:T(8,128)(2,1)} %bitcast.347, bf16[3,3,64,2048]{3,2,1,0:T(8,128)(2,1)} %bitcast.348, bf16[3,3,64,2048]{3,2,1,0:T(8,128)(2,1)} %bitcast.349, bf16[3,64,2048]{2,1,0:T(8,128)(2,1)} %bitcast.355, ...), custom_call_target="tpu_custom_call" | custom-call | flops 5033164800 | bytes 6316032 | tf_op jit(solution)/shard_map/attn_bwd/pallas_call | solution.py:174
  336.0 5.6 %bitcast_add_fusion = f32[2,2,3072,96]{2,3,0,1:T(8,128)S(1)} fusion(bf16[2,2,3072,96]{2,3,0,1:T(8,128)(2,1)} %collective-permute-done.13, f32[2,2,1,3072,96]{3,4,2,1,0:T(8,128)} %copy-done.1, f32[2,2,1,3072,96]{3,4,2,1,0:T(8,128)} %copy-done.2, pred[]{:T(512)S(6)} %eq.27), kind=kLoop, calls=%fused_computation.14 | loop fusion | flops 3538944 | bytes 16515073 | tf_op jit(solution)/shard_map/add | solution.py:390
  351.6 13.3 %all-to-all-done.3 = bf16[8,3,3,64,256]{4,3,2,1,0:T(8,128)(2,1)S(1)} async-done(((bf16[8,3,3,64,256]{4,3,2,1,0:T(8,128)(2,1)}), bf16[8,3,3,64,256]{4,3,2,1,0:T(8,128)(2,1)S(1)}, u32[]{:S(2)}, u32[]{:S(2)}) %all-to-all-start.3) | async-done | bytes 2359328 | tf_op jit(solution)/shard_map/all_to_all | solution.py:363
  379.3 9.9 %collective-permute-done.14 = bf16[2,3072,96]{1,2,0:T(8,128)(2,1)S(1)} collective-permute-done((bf16[2,3072,96]{1,2,0:T(8,128)(2,1)}, bf16[2,3072,96]{1,2,0:T(8,128)(2,1)S(1)}, u32[]{:S(2)}, u32[]{:S(2)}) %collective-permute-start.14) | collective-permute-done | bytes 1179680 | tf_op jit(solution)/shard_map/ppermute | solution.py:389
  391.5 22.6 %collective-permute-done.11 = bf16[2,768,384]{2,1,0:T(8,128)(2,1)} collective-permute-done((bf16[2,768,384]{2,1,0:T(8,128)(2,1)}, bf16[2,768,384]{2,1,0:T(8,128)(2,1)}, u32[]{:S(2)}, u32[]{:S(2)}) %collective-permute-start.11) | collective-permute-done | bytes 1179680 | tf_op jit(solution)/shard_map/ppermute | solution.py:389
  420.8 4.3 bitcast_add_fusion.2
  427.1 4.2 fusion.27
  431.3 6.4 %concatenate.59 = f32[3081]{0:T(1024)S(1)} concatenate(f32[768]{0:T(1024)} %get-tuple-element.98, f32[768]{0:T(1024)} %get-tuple-element.103, f32[768]{0:T(1024)} %get-tuple-element.96, f32[768]{0:T(1024)} %get-tuple-element.102, f32[1]{0:T(128)} %bitcast.101, f32[1]{0:T(128)} %bitcast.103, f32[1]{0:T(128)} %bitcast.105, f32[1]{0:T(128)} %bitcast.107, f32[1]{0:T(128)} %bitcast.109, ...), dimensions={0} | concatenate | bytes 24648 | tf_op jit(solution)/shard_map/concatenate | solution.py:402
  455.6 5.8 %collective-permute-done.6 = bf16[768,288]{0,1:T(8,128)(2,1)S(1)} collective-permute-done((bf16[768,288]{0,1:T(8,128)(2,1)S(1)}, bf16[768,288]{0,1:T(8,128)(2,1)S(1)}, u32[]{:S(2)}, u32[]{:S(2)}) %collective-permute-start.6) | collective-permute-done | bytes 442400 | tf_op jit(solution)/shard_map/ppermute | solution.py:389
  464.1 12.2 %collective-permute-start.19 = (f32[3081]{0:T(1024)S(1)}, f32[3081]{0:T(1024)S(1)}, u32[]{:S(2)}, u32[]{:S(2)}) collective-permute-start(f32[3081]{0:T(1024)S(1)} %add.283), channel_id=1, source_target_pairs={{0,8},{8,0},{16,24},{24,16},{1,9},{9,1},{17,25},{25,17},{2,10},{10... | collective-permute-start | bytes 36980 | tf_op jit(solution)/shard_map/ppermute | solution.py:408
  488.2 12.1 %reduce-scatter.13.cloned.1.call-done = bf16[192,288]{1,0:T(8,128)(2,1)} async-done(((bf16[768,288]{1,0:T(8,128)(2,1)}), bf16[192,288]{1,0:T(8,128)(2,1)}) %reduce-scatter.13.cloned.1.call-update) | async-done | bytes 110608
  (332 shorter events, 187.2 us)
Async XLA Ops:
  7.2 74.0 %all-gather.6.cloned.1.call-start = ((), (), s32[]{:S(2)}) async-start(), calls=%async_computation.8 | async-start | bytes 3981312 | tf_op jit(solution)/shard_map/all_gather | solution.py:277
  7.2 11.4 %collective-permute-start = (bf16[192,288]{1,0:T(8,128)(2,1)}, bf16[192,288]{1,0:T(8,128)(2,1)S(1)}, u32[]{:S(2)}, u32[]{:S(2)}) collective-permute-start(bf16[192,288]{1,0:T(8,128)(2,1)} %param.17), channel_id=1, source_target_pairs={{0,16},{8,24},{16,0},{24,8},{1,17},{9,25},{17,1},{25,9},{2,18},{10... | collective-permute-start | bytes 331784 | tf_op jit(solution)/shard_map/ppermute | solution.py:269
  19.7 8.2 %collective-permute-start.1 = (bf16[2,192,288]{2,1,0:T(8,128)(2,1)S(1)}, bf16[2,192,288]{2,1,0:T(8,128)(2,1)S(1)}, u32[]{:S(2)}, u32[]{:S(2)}) collective-permute-start(bf16[2,192,288]{2,1,0:T(8,128)(2,1)S(1)} %maximum_select_fusion.2), channel_id=1, source_target_pairs={{0,8},{8,0},{16,24},{24,16},{1,9},{9,1},{17,25},{25,17},{2,10},{10... | collective-permute-start | bytes 663560 | tf_op jit(solution)/shard_map/ppermute | solution.py:269
  29.9 17.6 %collective-permute-start.2 = (bf16[165888]{0:T(1024)(128)(2,1)S(1)}, bf16[165888]{0:T(1024)(128)(2,1)S(1)}, u32[]{:S(2)}, u32[]{:S(2)}) collective-permute-start(bf16[165888]{0:T(1024)(128)(2,1)S(1)} %pad_maximum_fusion.5), channel_id=1, source_target_pairs={{0,16},{8,24},{16,0},{24,8},{1,17},{9,25},{17,1},{25,9},{2,18},{10... | collective-permute-start | bytes 995336 | tf_op jit(solution)/shard_map/ppermute | solution.py:269
  33.0 157.9 %all-gather.8.cloned.1.call-start = ((), (), s32[]{:S(2)}) async-start(), calls=%async_computation.9 | async-start | bytes 1327104 | tf_op jit(solution)/shard_map/all_gather | solution.py:301
  50.8 16.0 %collective-permute-start.3 = (bf16[2,165888]{1,0:T(2,128)(2,1)S(1)}, bf16[2,165888]{1,0:T(2,128)(2,1)S(1)}, u32[]{:S(2)}, u32[]{:S(2)}) collective-permute-start(bf16[2,165888]{1,0:T(2,128)(2,1)S(1)} %broadcast_select_fusion.1), channel_id=1, source_target_pairs={{0,8},{8,0},{16,24},{24,16},{1,9},{9,1},{17,25},{25,17},{2,10},{10... | collective-permute-start | bytes 1990664 | tf_op jit(solution)/shard_map/ppermute | solution.py:269
  74.4 119.4 %all-gather.12.cloned.1.call-start = ((), (), s32[]{:S(2)}) async-start(), calls=%async_computation.11 | async-start | bytes 5308416 | tf_op jit(solution)/shard_map/all_gather | solution.py:301
  76.7 130.0 %all-gather.10.cloned.1.call-start = ((), (), s32[]{:S(2)}) async-start(), calls=%async_computation.10 | async-start | bytes 5308416 | tf_op jit(solution)/shard_map/all_gather | solution.py:301
  101.8 39.6 %all-to-all-start = ((bf16[8,3,3,64,256]{4,3,2,1,0:T(8,128)(2,1)}), bf16[8,3,3,64,256]{4,3,2,1,0:T(8,128)(2,1)S(1)}, u32[]{:S(2)}, u32[]{:S(2)}) async-start(bf16[8,3,3,64,256]{4,3,2,1,0:T(8,128)(2,1)} %copy.154), calls=%async_computation | async-start | bytes 4718592 | tf_op jit(solution)/shard_map/all_to_all | solution.py:291
  162.6 26.5 %all-to-all-start.1 = ((bf16[8,3,64,256]{3,2,1,0:T(8,128)(2,1)}), bf16[8,3,64,256]{3,2,1,0:T(8,128)(2,1)S(1)}, u32[]{:S(2)}, u32[]{:S(2)}) async-start(bf16[8,3,64,256]{3,2,1,0:T(8,128)(2,1)} %bitcast.335), calls=%async_computation.1 | async-start | bytes 1572864 | tf_op jit(solution)/shard_map/all_to_all | solution.py:307
  255.9 45.1 %all-to-all-start.2 = ((bf16[8,3,64,256]{3,2,1,0:T(8,128)(2,1)}), bf16[8,3,64,256]{3,2,1,0:T(8,128)(2,1)}, u32[]{:S(2)}, u32[]{:S(2)}) async-start(bf16[8,3,64,256]{3,2,1,0:T(8,128)(2,1)} %bitcast.37), calls=%async_computation.2 | async-start | bytes 1572864 | tf_op jit(solution)/shard_map/all_to_all | solution.py:357
  270.9 65.1 %collective-permute-start.13 = (bf16[2,2,3072,96]{2,3,0,1:T(8,128)(2,1)}, bf16[2,2,3072,96]{2,3,0,1:T(8,128)(2,1)}, u32[]{:S(2)}, u32[]{:S(2)}) collective-permute-start(bf16[2,2,3072,96]{2,3,0,1:T(8,128)(2,1)} %fusion.10), channel_id=1, source_target_pairs={{0,1},{1,0},{2,3},{3,2},{4,5},{5,4},{6,7},{7,6},{8,9},{9,8},{10,11... | collective-permute-start | bytes 7077896 | tf_op jit(solution)/shard_map/ppermute | solution.py:389
  272.2 21.2 %collective-permute-start.7 = (bf16[2,2,768,96]{2,3,1,0:T(8,128)(2,1)S(1)}, bf16[2,2,768,96]{2,3,1,0:T(8,128)(2,1)}, u32[]{:S(2)}, u32[]{:S(2)}) collective-permute-start(bf16[2,2,768,96]{2,3,1,0:T(8,128)(2,1)S(1)} %fusion.62), channel_id=1, source_target_pairs={{0,1},{1,0},{2,3},{3,2},{4,5},{5,4},{6,7},{7,6},{8,9},{9,8},{10,11... | collective-permute-start | bytes 1769480 | tf_op jit(solution)/shard_map/ppermute | solution.py:389
  294.8 9.3 %collective-permute-start.8 = (bf16[2,768,96]{1,2,0:T(8,128)(2,1)S(1)}, bf16[2,768,96]{1,2,0:T(8,128)(2,1)S(1)}, u32[]{:S(2)}, u32[]{:S(2)}) collective-permute-start(bf16[2,768,96]{1,2,0:T(8,128)(2,1)S(1)} %fusion.69), channel_id=1, source_target_pairs={{0,2},{1,3},{2,0},{3,1},{4,6},{5,7},{6,4},{7,5},{8,10},{9,11},{10,... | collective-permute-start | bytes 884744 | tf_op jit(solution)/shard_map/ppermute | solution.py:389
  300.9 44.0 %collective-permute-start.10 = (bf16[2,2,768,384]{3,2,0,1:T(8,128)(2,1)}, bf16[2,2,768,384]{3,2,0,1:T(8,128)(2,1)}, u32[]{:S(2)}, u32[]{:S(2)}) collective-permute-start(bf16[2,2,768,384]{3,2,0,1:T(8,128)(2,1)} %fusion.9), channel_id=1, source_target_pairs={{0,1},{1,0},{2,3},{3,2},{4,5},{5,4},{6,7},{7,6},{8,9},{9,8},{10,11... | collective-permute-start | bytes 7077896 | tf_op jit(solution)/shard_map/ppermute | solution.py:389
  305.1 30.0 %collective-permute-start.9 = (bf16[768,96]{0,1:T(8,128)(2,1)S(1)}, bf16[768,96]{0,1:T(8,128)(2,1)S(1)}, u32[]{:S(2)}, u32[]{:S(2)}) collective-permute-start(bf16[768,96]{0,1:T(8,128)(2,1)S(1)} %fusion.71), channel_id=1, source_target_pairs={{0,4},{1,5},{2,6},{3,7},{4,0},{5,1},{6,2},{7,3},{8,12},{9,13},{10,... | collective-permute-start | bytes 442376 | tf_op jit(solution)/shard_map/ppermute | solution.py:389
  331.2 33.7 %all-to-all-start.3 = ((bf16[8,3,3,64,256]{4,3,2,1,0:T(8,128)(2,1)}), bf16[8,3,3,64,256]{4,3,2,1,0:T(8,128)(2,1)S(1)}, u32[]{:S(2)}, u32[]{:S(2)}) async-start(bf16[8,3,3,64,256]{4,3,2,1,0:T(8,128)(2,1)} %bitcast.320), calls=%async_computation.3 | async-start | bytes 4718592 | tf_op jit(solution)/shard_map/all_to_all | solution.py:363
  335.0 116.6 %reduce-scatter.15.cloned.1.call-start = ((), (), s32[]{:S(2)}) async-start(), calls=%async_computation.15 | async-start | bytes 245760
  336.0 149.0 %reduce-scatter.11.cloned.1.call-start = ((), (), s32[]{:S(2)}) async-start(), calls=%async_computation.13 | async-start | bytes 737280 | tf_op jit(solution)/shard_map/reduce_scatter | solution.py:394
  343.0 46.3 %collective-permute-start.14 = (bf16[2,3072,96]{1,2,0:T(8,128)(2,1)}, bf16[2,3072,96]{1,2,0:T(8,128)(2,1)S(1)}, u32[]{:S(2)}, u32[]{:S(2)}) collective-permute-start(bf16[2,3072,96]{1,2,0:T(8,128)(2,1)} %fusion.49), channel_id=1, source_target_pairs={{0,2},{1,3},{2,0},{3,1},{4,6},{5,7},{6,4},{7,5},{8,10},{9,11},{10,... | collective-permute-start | bytes 3538952 | tf_op jit(solution)/shard_map/ppermute | solution.py:389
  351.0 63.1 %collective-permute-start.11 = (bf16[2,768,384]{2,1,0:T(8,128)(2,1)}, bf16[2,768,384]{2,1,0:T(8,128)(2,1)}, u32[]{:S(2)}, u32[]{:S(2)}) collective-permute-start(bf16[2,768,384]{2,1,0:T(8,128)(2,1)} %fusion.48), channel_id=1, source_target_pairs={{0,2},{1,3},{2,0},{3,1},{4,6},{5,7},{6,4},{7,5},{8,10},{9,11},{10,... | collective-permute-start | bytes 3538952 | tf_op jit(solution)/shard_map/ppermute | solution.py:389
  379.3 41.5 %collective-permute-start.4 = (bf16[2,2,768,288]{2,3,1,0:T(8,128)(2,1)S(1)}, bf16[2,2,768,288]{2,3,1,0:T(8,128)(2,1)}, u32[]{:S(2)}, u32[]{:S(2)}) collective-permute-start(bf16[2,2,768,288]{2,3,1,0:T(8,128)(2,1)S(1)} %fusion.19), channel_id=1, source_target_pairs={{0,1},{1,0},{2,3},{3,2},{4,5},{5,4},{6,7},{7,6},{8,9},{9,8},{10,11... | collective-permute-start | bytes 5308424 | tf_op jit(solution)/shard_map/ppermute | solution.py:389
  389.9 29.8 %collective-permute-start.15 = (bf16[3072,96]{0,1:T(8,128)(2,1)S(1)}, bf16[3072,96]{0,1:T(8,128)(2,1)S(1)}, u32[]{:S(2)}, u32[]{:S(2)}) collective-permute-start(bf16[3072,96]{0,1:T(8,128)(2,1)S(1)} %fusion.64), channel_id=1, source_target_pairs={{0,4},{1,5},{2,6},{3,7},{4,0},{5,1},{6,2},{7,3},{8,12},{9,13},{10,... | collective-permute-start | bytes 1769480 | tf_op jit(solution)/shard_map/ppermute | solution.py:389
  418.2 25.0 %collective-permute-start.12 = (bf16[768,384]{1,0:T(8,128)(2,1)}, bf16[768,384]{1,0:T(8,128)(2,1)}, u32[]{:S(2)}, u32[]{:S(2)}) collective-permute-start(bf16[768,384]{1,0:T(8,128)(2,1)} %fusion.63), channel_id=1, source_target_pairs={{0,4},{1,5},{2,6},{3,7},{4,0},{5,1},{6,2},{7,3},{8,12},{9,13},{10,... | collective-permute-start | bytes 1769480 | tf_op jit(solution)/shard_map/ppermute | solution.py:389
  420.7 65.9 %reduce-scatter.9.cloned.1.call-start = ((), (), s32[]{:S(2)}) async-start(), calls=%async_computation.12 | async-start | bytes 737280 | tf_op jit(solution)/shard_map/reduce_scatter | solution.py:394
  426.3 21.3 %collective-permute-start.5 = (bf16[2,768,288]{1,2,0:T(8,128)(2,1)}, bf16[2,768,288]{1,2,0:T(8,128)(2,1)}, u32[]{:S(2)}, u32[]{:S(2)}) collective-permute-start(bf16[2,768,288]{1,2,0:T(8,128)(2,1)} %fusion.52), channel_id=1, source_target_pairs={{0,2},{1,3},{2,0},{3,1},{4,6},{5,7},{6,4},{7,5},{8,10},{9,11},{10,... | collective-permute-start | bytes 2654216 | tf_op jit(solution)/shard_map/ppermute | solution.py:389
  442.0 11.3 %collective-permute-start.17 = (f32[3081]{0:T(1024)S(1)}, f32[3081]{0:T(1024)}, u32[]{:S(2)}, u32[]{:S(2)}) collective-permute-start(f32[3081]{0:T(1024)S(1)} %add.281), channel_id=1, source_target_pairs={{0,2},{1,3},{2,0},{3,1},{4,6},{5,7},{6,4},{7,5},{8,10},{9,11},{10,... | collective-permute-start | bytes 36980 | tf_op jit(solution)/shard_map/ppermute | solution.py:408
  446.0 54.3 %reduce-scatter.13.cloned.1.call-start = ((), (), s32[]{:S(2)}) async-start(), calls=%async_computation.14 | async-start | bytes 737280
  450.3 11.1 %collective-permute-start.6 = (bf16[768,288]{0,1:T(8,128)(2,1)S(1)}, bf16[768,288]{0,1:T(8,128)(2,1)S(1)}, u32[]{:S(2)}, u32[]{:S(2)}) collective-permute-start(bf16[768,288]{0,1:T(8,128)(2,1)S(1)} %fusion.68), channel_id=1, source_target_pairs={{0,4},{1,5},{2,6},{3,7},{4,0},{5,1},{6,2},{7,3},{8,12},{9,13},{10,... | collective-permute-start | bytes 1327112 | tf_op jit(solution)/shard_map/ppermute | solution.py:389
  454.1 10.0 %collective-permute-start.18 = (f32[3081]{0:T(1024)S(1)}, f32[3081]{0:T(1024)S(1)}, u32[]{:S(2)}, u32[]{:S(2)}) collective-permute-start(f32[3081]{0:T(1024)S(1)} %add.282), channel_id=1, source_target_pairs={{0,4},{1,5},{2,6},{3,7},{4,0},{5,1},{6,2},{7,3},{8,12},{9,13},{10,... | collective-permute-start | bytes 36980 | tf_op jit(solution)/shard_map/ppermute | solution.py:408
  464.1 13.9 %collective-permute-start.19 = (f32[3081]{0:T(1024)S(1)}, f32[3081]{0:T(1024)S(1)}, u32[]{:S(2)}, u32[]{:S(2)}) collective-permute-start(f32[3081]{0:T(1024)S(1)} %add.283), channel_id=1, source_target_pairs={{0,8},{8,0},{16,24},{24,16},{1,9},{9,1},{17,25},{25,17},{2,10},{10... | collective-permute-start | bytes 36980 | tf_op jit(solution)/shard_map/ppermute | solution.py:408
  478.0 5.8 %collective-permute-start.20 = (f32[3081]{0:T(1024)S(1)}, f32[3081]{0:T(1024)S(1)}, u32[]{:S(2)}, u32[]{:S(2)}) collective-permute-start(f32[3081]{0:T(1024)S(1)} %add.284), channel_id=1, source_target_pairs={{0,16},{8,24},{16,0},{24,8},{1,17},{9,25},{17,1},{25,9},{2,18},{10... | collective-permute-start | bytes 36980 | tf_op jit(solution)/shard_map/ppermute | solution.py:408
  (65 other events, 1200.4 us)
Sparse Core Ops, SparseCore 0:
  33.2 33.2 all-gather.5
  74.6 25.9 all-gather.7
  102.5 54.5 all-gather.11
  158.9 47.7 all-gather.9
  338.3 30.6 reduce-scatter.14
  420.8 30.9 reduce-scatter.10
  454.1 23.2 reduce-scatter.8
  479.7 20.5 reduce-scatter.12
